TPU v7x, 128 devices: a whole 4x4x4 slice. The times are simulated.
128 devices in a mesh: prow: 8 (over x, core), pcol: 16 (over z, y).
Axes of the slice: x: 4, y: 4, z: 4, core: 2. Of those that a mesh axis runs over, the one named last changes fastest.
Arguments:
- front: float32 [16384, 16384], P('prow', 'pcol'), may hold values from -6 to 6
- fill_blocks: int32 [128, 128], P('prow', 'pcol'), may hold values from 0 to 1, as said below
- seg_values: float32 [262144, 128], P(('prow', 'pcol')), may hold values from -6 to 6
- seg_row: int32 [262144], P(('prow', 'pcol')), may hold values from 0 to 16383
- seg_block: int32 [262144], P(('prow', 'pcol')), may hold values from 0 to 127
- seg_live: int32 [128], P(('prow', 'pcol')), may hold values from 1024 to 2048, as said below
- panel_start: int32 [2], replicated, may hold values from 0 to 126, as said below
- panel_inverse: float32 [2, 256, 256], replicated
Outputs:
- factored: float32 [16384, 16384], P('prow', 'pcol')
Inputs may be any that keep to these rules, and one draw needn't show every extreme that they name: `seg_live`: some device has all its segments live. `fill_blocks`: Symmetric, with ones on the diagonal. `panel_start`: each is a multiple of 2; a panel lies within the columns of one index of pcol, and consecutive panels lie on different indices of pcol.
All inputs are finite; a program needn't handle non-finite values.
Results may differ from a plain program's by a relative error of at most 0.0001.
Values sent between devices are 32-bit elements; how exact they have to be, the bound alone decides.
No kernel may reach another device: no remote copies, remote signals or barrier semaphores. Data moves between devices by JAX's collectives and lax.ppermute only.
A program may use at most 128 MiB of HBM per device.

v0:
```python
import jax
import jax.numpy as jnp
from jax import lax
from jax.sharding import PartitionSpec as P

PANELS = 2


def broadcast(value, axis, source):
    kept = jnp.where(lax.axis_index(axis) == source, value, 0).astype(value.dtype)
    return lax.psum(kept, axis)


def masked_product(left_rows, left_cols, mask_part):
    product = jnp.dot(
        left_rows, left_cols.T, precision=lax.Precision.HIGHEST, preferred_element_type=jnp.float32
    )
    rows, cols = product.shape
    shaped = product.reshape(rows // 128, 128, cols // 128, 128) * mask_part[:, None, :, None]
    return shaped.reshape(rows, cols)


def send_panel(columns, start, blocks_local):
    owner = start // blocks_local
    return broadcast(columns, "pcol", owner)


def column_side(left_rows, col_start, cols_local):
    rows_local = left_rows.shape[0]
    piece = lax.dynamic_slice_in_dim(left_rows, col_start % rows_local, cols_local, 0)
    return broadcast(piece, "prow", col_start // rows_local)


def body(front, fill_blocks, seg_values, seg_row, seg_block, seg_live, panel_start, panel_inverse):
    rows_local, cols_local = front.shape
    blocks_local = cols_local // 128
    n_prow = lax.axis_size("prow")
    n_pcol = lax.axis_size("pcol")
    devices = n_prow * n_pcol
    seg_count = seg_values.shape[0]
    capacity = 3 * seg_count // (2 * devices)
    panel_width = panel_inverse.shape[1]
    target = seg_row // rows_local * n_pcol + seg_block // blocks_local
    live = jnp.arange(seg_count, dtype=jnp.int32) < seg_live[0]
    onehot = (target[:, None] == jnp.arange(devices, dtype=jnp.int32)[None, :]).astype(jnp.int32)
    earlier = jnp.cumsum(onehot, axis=0) - onehot
    rank = jnp.sum(earlier * onehot, axis=1)
    slot = jnp.where(live, target * capacity + rank, devices * capacity)
    local_place = (seg_row % rows_local * blocks_local + seg_block % blocks_local).astype(
        jnp.float32
    )
    send_values = (
        jnp.zeros((devices * capacity, 128), jnp.float32).at[slot].set(seg_values, mode="drop")
    )
    send_place = (
        jnp.zeros((devices * capacity,), jnp.float32).at[slot].set(local_place, mode="drop")
    )
    got_values, got_place = (
        lax.all_to_all(send_values, ("prow", "pcol"), split_axis=0, concat_axis=0, tiled=True),
        lax.all_to_all(send_place, ("prow", "pcol"), split_axis=0, concat_axis=0, tiled=True),
    )
    flat = (
        front.reshape(rows_local * blocks_local, 128)
        .at[got_place.astype(jnp.int32)]
        .add(got_values)
    )
    assembled = flat.reshape(rows_local, cols_local)
    col_start = lax.axis_index("pcol") * cols_local
    mask_local = fill_blocks.astype(jnp.float32)
    current = assembled
    for k in range(PANELS):
        offset = panel_start[k] % blocks_local * 128
        columns = send_panel(
            lax.dynamic_slice_in_dim(current, offset, panel_width, 1), panel_start[k], blocks_local
        )
        left_rows = jnp.dot(
            columns,
            panel_inverse[k],
            precision=lax.Precision.HIGHEST,
            preferred_element_type=jnp.float32,
        )
        left_cols = column_side(left_rows, col_start, cols_local)
        left_rows, left_cols = (left_rows, left_cols)
        current = current - masked_product(left_rows, left_cols, mask_local)
    return current


def solution(mesh):
    placed = (
        P("prow", "pcol"),
        P("prow", "pcol"),
        P(("prow", "pcol"), None),
        P(("prow", "pcol")),
        P(("prow", "pcol")),
        P(("prow", "pcol")),
        P(),
        P(),
    )
    return jax.shard_map(
        body, mesh=mesh, in_specs=placed, out_specs=P("prow", "pcol"), check_vma=False
    )
```

profile of v0, /device:TPU:0, one launch (start us, length us, event | category | flops | bytes accessed | tf_op | source)
XLA Modules:
  0.0 460.9 jit_solution(8931668497211479905)
XLA Ops:
  6.5 0.7 fusion.19
  7.3 0.1 copy.13
  7.4 0.3 fusion.4
  7.8 0.1 broadcast_add_fusion
  7.8 0.3 copy.14
  8.2 0.6 fusion.3
  9.5 8.1 %scatter_custom_fusion = f32[3072]{0:T(1024)S(1)} fusion(s32[2048]{0:T(1024)S(1)} %compare_select_fusion.1, f32[2048]{0:T(1024)S(1)} %get-tuple-element.5, f32[]{:T(128)} %constant.104.clone.1), kind=kCustom, calls=%fused_computation.52 | custom fusion | bytes 12292 | tf_op jit(solution)/shard_map/scatter | solution.py:56
  17.6 0.7 all_to_all.14
  18.3 11.2 %all-to-all-start = ((f32[128,24,1]{1,2,0:T(1,128)}), f32[128,24,1]{1,2,0:T(1,128)S(1)}, u32[]{:S(2)}, u32[]{:S(2)}) async-start(f32[128,24,1]{1,2,0:T(1,128)} %bitcast.5), calls=%async_computation | async-start | bytes 131072 | tf_op jit(solution)/shard_map/all_to_all | solution.py:60
  29.5 0.0 copy-start.5
  29.5 7.2 %scatter_custom_fusion.1 = f32[3072,128]{1,0:T(8,128)} fusion(s32[2048]{0:T(1024)S(1)} %compare_select_fusion.1, f32[2048,128]{1,0:T(8,128)} %param.10, f32[]{:T(128)} %constant.104.clone.1), kind=kCustom, calls=%fused_computation.18 | custom fusion | bytes 1573376 | tf_op jit(solution)/shard_map/scatter | solution.py:53
  36.6 2.2 all-to-all-done
  38.9 7.5 %all-to-all-start.1 = ((f32[128,24,128]{2,1,0:T(8,128)}), f32[128,24,128]{2,1,0:T(8,128)S(1)}, u32[]{:S(2)}, u32[]{:S(2)}) async-start(f32[128,24,128]{2,1,0:T(8,128)} %bitcast.7), calls=%async_computation.1 | async-start | bytes 3145728 | tf_op jit(solution)/shard_map/all_to_all | solution.py:59
  46.4 0.0 all-reduce.5.cloned.1.call-start
  46.5 0.0 copy-done.5
  46.5 0.6 fusion.26
  49.7 9.3 %reshape.53 = f32[16384,128]{1,0:T(8,128)} reshape(f32[2048,1024]{1,0:T(8,128)} %param.8) | data formatting | bytes 16777216 | tf_op jit(solution)/shard_map/reshape | solution.py:63
  58.9 0.2 convert_reduce_fusion
  59.1 0.1 convert_element_type.36
  59.3 11.6 %all-to-all-done.1 = f32[128,24,128]{2,1,0:T(8,128)S(1)} async-done(((f32[128,24,128]{2,1,0:T(8,128)}), f32[128,24,128]{2,1,0:T(8,128)S(1)}, u32[]{:S(2)}, u32[]{:S(2)}) %all-to-all-start.1) | async-done | bytes 1572896 | tf_op jit(solution)/shard_map/all_to_all | solution.py:59
  70.9 23.8 %scatter_fusion = f32[16384,128]{1,0:T(8,128)} fusion(f32[16384,128]{1,0:T(8,128)} %reshape.53, s32[3072]{0:T(1024)S(1)} %bitcast.44, f32[3072,128]{1,0:T(8,128)S(1)} %bitcast.42), kind=kCustom, calls=%fused_computation.2 | custom fusion | flops 393216 | bytes 4730880 | tf_op jit(solution)/shard_map/scatter-add | solution.py:65
  94.7 9.3 %reshape.55 = f32[2048,1024]{1,0:T(8,128)} reshape(f32[16384,128]{1,0:T(8,128)} %scatter_fusion) | data formatting | bytes 16777216 | tf_op jit(solution)/shard_map/reshape | solution.py:67
  104.0 3.0 dynamic-slice_select_fusion.1
  107.0 0.0 copy-start.3
  107.0 0.0 all-reduce.5.cloned.1.call-update
  107.1 0.0 all-reduce.7.cloned.1.call-start
  107.2 89.3 %all-reduce.5.cloned.1.call-done = f32[2048,256]{1,0:T(8,128)} async-done(((f32[2048,256]{1,0:T(8,128)}), f32[2048,256]{1,0:T(8,128)}) %all-reduce.5.cloned.1.call-update) | async-done | bytes 2097168 | tf_op jit(solution)/shard_map/psum | solution.py:11
  196.5 0.0 copy-done.3
  196.5 3.4 fusion.11
  199.9 0.0 copy-start.4
  199.9 1.0 dynamic-slice_select_fusion.3
  201.0 0.0 all-reduce.7.cloned.1.call-update
  201.0 0.2 all-reduce.9.cloned.1.call-start
  203.7 0.0 copy-done.4
  203.7 0.1 copy.16
  203.8 59.3 %all-reduce.7.cloned.1.call-done = f32[1024,256]{1,0:T(8,128)} async-done(((f32[1024,256]{1,0:T(8,128)}), f32[1024,256]{1,0:T(8,128)}) %all-reduce.7.cloned.1.call-update) | async-done | bytes 1048592 | tf_op jit(solution)/shard_map/psum | solution.py:11
  263.0 0.0 copy-start.2
  263.0 0.6 mul.54
  263.7 0.0 copy-start
  263.7 0.6 copy-done.2
  264.3 13.0 %fusion = f32[2048,1024]{1,0:T(8,128)S(1)} fusion(f32[2048,1024]{1,0:T(8,128)} %reshape.55, f32[256,8,8,128]{3,2,1,0:T(8,128)S(1)} %bitcast.40, f32[2048,256]{1,0:T(8,128)S(1)} %fusion.11, f32[1024,256]{1,0:T(8,128)S(1)} %copy-done.2), kind=kOutput, calls=%fused_computation.5 | convolution fusion | flops 6446645248 | bytes 28311552 | tf_op jit(solution)/shard_map/dot_general | solution.py:15
  277.3 0.0 copy-done
  277.3 0.0 copy-start.1
  277.3 3.4 copy-done.1
  280.7 1.6 dynamic-slice_select_fusion
  282.3 0.0 all-reduce.9.cloned.1.call-update
  282.3 0.3 all-reduce.11.cloned.1.call-start
  282.6 90.4 %all-reduce.9.cloned.1.call-done = f32[2048,256]{1,0:T(8,128)} async-done(((f32[2048,256]{1,0:T(8,128)}), f32[2048,256]{1,0:T(8,128)}) %all-reduce.9.cloned.1.call-update) | async-done | bytes 2097168 | tf_op jit(solution)/shard_map/psum | solution.py:11
  373.0 3.4 fusion.9
  376.4 1.1 dynamic-slice_select_fusion.2
  377.4 0.0 all-reduce.11.cloned.1.call-update
  377.5 62.1 %all-reduce.11.cloned.1.call-done = f32[1024,256]{1,0:T(8,128)} async-done(((f32[1024,256]{1,0:T(8,128)}), f32[1024,256]{1,0:T(8,128)}) %all-reduce.11.cloned.1.call-update) | async-done | bytes 1048592 | tf_op jit(solution)/shard_map/psum | solution.py:11
  439.6 14.8 %fusion.1 = f32[2048,1024]{1,0:T(8,128)} fusion(f32[2048,1024]{1,0:T(8,128)} %copy-done.1, f32[256,8,8,128]{3,2,1,0:T(8,128)} %bitcast.41, f32[2048,256]{1,0:T(8,128)S(1)} %fusion.9, f32[1024,256]{1,0:T(8,128)} %all-reduce.11.cloned.1.call-done), kind=kOutput, calls=%fused_computation.6 | convolution fusion | flops 6446645248 | bytes 28311552 | tf_op jit(solution)/shard_map/dot_general | solution.py:15
  (6 shorter events, 0.1 us)
Async XLA Ops:
  18.3 20.6 %all-to-all-start = ((f32[128,24,1]{1,2,0:T(1,128)}), f32[128,24,1]{1,2,0:T(1,128)S(1)}, u32[]{:S(2)}, u32[]{:S(2)}) async-start(f32[128,24,1]{1,2,0:T(1,128)} %bitcast.5), calls=%async_computation | async-start | bytes 131072 | tf_op jit(solution)/shard_map/all_to_all | solution.py:60
  29.5 17.0 %copy-start.5 = (s32[2]{0:T(128)S(1)}, s32[2]{0:T(128)}, u32[]{:S(2)}) copy-start(s32[2]{0:T(128)} %param.14) | copy-start | bytes 28
  38.9 32.0 %all-to-all-start.1 = ((f32[128,24,128]{2,1,0:T(8,128)}), f32[128,24,128]{2,1,0:T(8,128)S(1)}, u32[]{:S(2)}, u32[]{:S(2)}) async-start(f32[128,24,128]{2,1,0:T(8,128)} %bitcast.7), calls=%async_computation.1 | async-start | bytes 3145728 | tf_op jit(solution)/shard_map/all_to_all | solution.py:59
  46.4 150.1 %all-reduce.5.cloned.1.call-start = ((), (), s32[]{:S(2)}) async-start(), calls=%async_computation.2 | async-start | bytes 4194304 | tf_op jit(solution)/shard_map/psum | solution.py:11
  107.0 89.4 %copy-start.3 = (f32[2,256,256]{2,1,0:T(8,128)S(1)}, f32[2,256,256]{2,1,0:T(8,128)}, u32[]{:S(2)}) copy-start(f32[2,256,256]{2,1,0:T(8,128)} %param.15) | copy-start | bytes 1572868
  107.1 156.0 %all-reduce.7.cloned.1.call-start = ((), (), s32[]{:S(2)}) async-start(), calls=%async_computation.3 | async-start | bytes 2097152 | tf_op jit(solution)/shard_map/psum | solution.py:11
  199.9 3.8 copy-start.4
  201.0 172.0 %all-reduce.9.cloned.1.call-start = ((), (), s32[]{:S(2)}) async-start(), calls=%async_computation.4 | async-start | bytes 4194304 | tf_op jit(solution)/shard_map/psum | solution.py:11
  263.0 1.2 copy-start.2
  263.7 13.6 %copy-start = (f32[16,128,8,128]{3,2,1,0:T(8,128)}, f32[16,128,8,128]{3,2,1,0:T(8,128)S(1)}, u32[]{:S(2)}) copy-start(f32[16,128,8,128]{3,2,1,0:T(8,128)S(1)} %mul.54) | copy-start | bytes 25165828
  277.3 3.4 copy-start.1
  282.3 157.3 %all-reduce.11.cloned.1.call-start = ((), (), s32[]{:S(2)}) async-start(), calls=%async_computation.5 | async-start | bytes 2097152 | tf_op jit(solution)/shard_map/psum | solution.py:11
Sparse Core Ops, SparseCore 0:
  107.2 89.2 all-reduce.4
  201.1 61.8 all-reduce.6
  282.4 90.5 all-reduce.8
  377.6 61.9 all-reduce.10
where the time goes:
time: 462 us; the launch traced here: 461 us
  waiting for transfers between devices  315 us (68%)
  local copies, waits for them, and re-layouts  40.3 us (9%)
  matrix products  34.6 us (7%)
  other arithmetic  32.6 us (7%)
  starting transfers between devices  19.3 us (4%)
  between operations  19.1 us (4%)
    psum x4, waiting for transfers between devices, broadcast(): return lax.psum(kept, axis)  301 us
    dot_general x2, matrix products, masked_product(): jnp.dot(left_rows, left_cols.T, precision=lax.Precision.HIGHEST, preferre...  27.8 us
    scatter-add x1, other arithmetic, body(): flat = front.reshape(rows_local * blocks_local, 128).at[got_place.astype(...  23.8 us
    all_to_all x1, waiting for transfers between devices, body(): lax.all_to_all(send_values, ('prow', 'pcol'), split_axis=0, concat_axis=0...  11.6 us
    all_to_all x1, starting transfers between devices, body(): lax.all_to_all(send_place, ('prow', 'pcol'), split_axis=0, concat_axis=0,...  11.2 us
    reshape x1, local copies, waits for them, and re-layouts, body(): assembled = flat.reshape(rows_local, cols_local)  9.28 us
    reshape x1, local copies, waits for them, and re-layouts, body(): front.reshape(rows_local * blocks_local, 128)  9.25 us
  transfers between devices with their start and end apart: 6, of which 6 were waited for; matrix products, arithmetic and copies ran while one was open for 4% of the time, Pallas kernels for 0%

commit v1 on v0

v1 whole, which is shorter than its diff:
```python
import jax
import jax.numpy as jnp
from jax import lax
from jax.sharding import PartitionSpec as P

PANELS = 2
HIGHEST = lax.Precision.HIGHEST


def dot(a, b):
    return jnp.dot(a, b, precision=HIGHEST, preferred_element_type=jnp.float32)


def dot_t(a, b):
    dims = (((1,), (1,)), ((), ()))
    return lax.dot_general(a, b, dims, precision=HIGHEST, preferred_element_type=jnp.float32)


def gather_rows(piece, axis, n):
    spread = jnp.broadcast_to(piece[None], (n,) + piece.shape)
    got = lax.all_to_all(spread, axis, 0, 0, tiled=False)
    return got.reshape(n * piece.shape[0], piece.shape[1])


def spread(x, total):
    for bit in range(total.bit_length() - 1):
        pairs = [(i, i ^ (1 << bit)) for i in range(total)]
        x = x + lax.ppermute(x, ("prow", "pcol"), pairs)
    return x


def assemble(front, seg_values, seg_row, seg_block, seg_live, n_prow, n_pcol):
    rows_local, cols_local = front.shape
    blocks_local = cols_local // 128
    devices = n_prow * n_pcol
    seg_count = seg_values.shape[0]
    capacity = 3 * seg_count // (2 * devices)
    target = seg_row // rows_local * n_pcol + seg_block // blocks_local
    live = jnp.arange(seg_count, dtype=jnp.int32) < seg_live[0]
    onehot = (target[:, None] == jnp.arange(devices, dtype=jnp.int32)[None, :]).astype(jnp.int32)
    earlier = jnp.cumsum(onehot, axis=0) - onehot
    rank = jnp.sum(earlier * onehot, axis=1)
    slot = jnp.where(live, target * capacity + rank, devices * capacity)
    local_place = (seg_row % rows_local * blocks_local + seg_block % blocks_local).astype(
        jnp.float32
    )
    send_values = (
        jnp.zeros((devices * capacity, 128), jnp.float32).at[slot].set(seg_values, mode="drop")
    )
    send_place = (
        jnp.zeros((devices * capacity,), jnp.float32).at[slot].set(local_place, mode="drop")
    )
    got_values = lax.all_to_all(send_values, ("prow", "pcol"), 0, 0, tiled=True)
    got_place = lax.all_to_all(send_place, ("prow", "pcol"), 0, 0, tiled=True)
    place = got_place.astype(jnp.int32)
    index = jnp.stack([place // blocks_local, place % blocks_local * 128], axis=1)
    numbers = lax.ScatterDimensionNumbers(
        update_window_dims=(1,), inserted_window_dims=(0,), scatter_dims_to_operand_dims=(0, 1)
    )
    return lax.scatter_add(front, index, got_values, numbers)


def body(front, fill_blocks, seg_values, seg_row, seg_block, seg_live, panel_start, panel_inverse):
    rows_local, cols_local = front.shape
    blocks_local = cols_local // 128
    n_prow = lax.axis_size("prow")
    n_pcol = lax.axis_size("pcol")
    pw = panel_inverse.shape[1]
    piece_rows = rows_local // n_pcol
    r = lax.axis_index("prow")
    c = lax.axis_index("pcol")

    mask_all = lax.all_gather(
        lax.all_gather(fill_blocks, "prow", axis=0, tiled=True), "pcol", axis=1, tiled=True
    ).astype(jnp.float32)

    assembled = assemble(front, seg_values, seg_row, seg_block, seg_live, n_prow, n_pcol)

    owner = [panel_start[k] // blocks_local for k in range(PANELS)]
    offset = [panel_start[k] % blocks_local * 128 for k in range(PANELS)]
    cols = [lax.dynamic_slice_in_dim(assembled, offset[k], pw, 1) for k in range(PANELS)]

    start2 = panel_start[1] * 128
    src_row = start2 // rows_local
    x_local = lax.dynamic_slice_in_dim(cols[0], start2 % rows_local, pw, 0)
    x_mine = jnp.where((r == src_row) & (c == owner[0]), x_local, 0.0)
    x_cols = spread(x_mine, n_prow * n_pcol)

    send = jnp.concatenate(cols, axis=1).reshape(n_pcol, piece_rows, PANELS * pw)
    recv = lax.all_to_all(send, "pcol", 0, 0, tiled=False)
    piece0 = lax.dynamic_index_in_dim(recv, owner[0], 0, keepdims=False)[:, :pw]
    piece1 = lax.dynamic_index_in_dim(recv, owner[1], 0, keepdims=False)[:, pw:]

    left0 = dot(piece0, panel_inverse[0])
    left0_x = dot(x_cols, panel_inverse[0])
    piece_block = (r * rows_local + c * piece_rows) // 128
    m_row = lax.dynamic_slice(mask_all, (piece_block, panel_start[1]), (1, pw // 128))
    m_piece = jnp.repeat(m_row, 128, axis=1)
    piece1 = piece1 - dot_t(left0, left0_x) * m_piece
    left1 = dot(piece1, panel_inverse[1])
    piece = jnp.concatenate([left0, left1], axis=1)

    left_rows = gather_rows(piece, "pcol", n_pcol)

    perm = []
    for sr in range(n_prow):
        for sc in range(n_pcol):
            first = sr * rows_local + sc * piece_rows
            dc = first // cols_local
            dr = first % cols_local // piece_rows
            perm.append((sr * n_pcol + sc, dr * n_pcol + dc))
    moved = lax.ppermute(piece, ("prow", "pcol"), perm)
    left_cols = gather_rows(moved, "prow", n_prow)

    product = dot_t(left_rows, left_cols)
    mask_local = fill_blocks.astype(jnp.float32)
    shaped = product.reshape(rows_local // 128, 128, blocks_local, 128) * mask_local[:, None, :, None]
    return assembled - shaped.reshape(rows_local, cols_local)


def solution(mesh):
    placed = (
        P("prow", "pcol"),
        P("prow", "pcol"),
        P(("prow", "pcol"), None),
        P(("prow", "pcol")),
        P(("prow", "pcol")),
        P(("prow", "pcol")),
        P(),
        P(),
    )
    return jax.shard_map(
        body, mesh=mesh, in_specs=placed, out_specs=P("prow", "pcol"), check_vma=False
    )
```

time: 462 us -> 25100 us (54.33); the launches traced: 461 us -> 24600 us
  other arithmetic: 32.6 us -> 14300 us
  local copies, waits for them, and re-layouts: 40.3 us -> 9990 us
    scatter-add x1 -> x6144, other arithmetic: 23.8 us -> 14200 us  [body(): flat = front.reshape(rows_local * blocks_local, 128).at[got_place.astype(...]
    scatter-add x0 -> x9216, local copies, waits for them, and re-layouts: none -> 9950 us
    psum x4 -> x0, waiting for transfers between devices: 301 us -> none  [broadcast(): return lax.psum(kept, axis)]
where the time goes in v1:
time: 25100 us; the launch traced here: 24600 us
  other arithmetic  14300 us (57%)
  local copies, waits for them, and re-layouts  9990 us (40%)
    scatter-add x6144, other arithmetic  14200 us
    scatter-add x9216, local copies, waits for them, and re-layouts  9950 us

profile of v1, /device:TPU:0, one launch (start us, length us, event | category | flops | bytes accessed | tf_op | source)
XLA Modules:
  0.0 24604.7 jit_solution(7214342805860516888)
XLA Ops:
  0.0 8.5 copy.38
  10.8 8.1 scatter_custom_fusion
  19.5 11.2 all-to-all-start
  35.3 7.2 scatter_custom_fusion.1
  42.5 9.8 all-to-all-start.1
  52.7 24.0 all-to-all-done.1
  76.7 24199.0 %while.1 = (s32[]{:T(128)}, f32[2048,1024]{1,0:T(8,128)}, s32[3072,2]{0,1:T(2,128)S(1)}, f32[3072,128]{1,0:T(8,128)S(1)}, s32[]{:T(128)}, /*index=5*/s32[2]{0:T(128)S(1)}) while((s32[]{:T(128)}, f32[2048,1024]{1,0:T(8,128)}, s32[3072,2]{0,1:T(2,128)S(1)}, f32[3072,128]{1,0:T(8,128)S(1)}, s32[]{:T(128)}, /*index=5*/s32[2]{0:T(128)S(1)}) %tuple.28), condition=%wide.while_cond, body=%wide.while_body.sunk | while | flops 267 | bytes 2707 | solution.py:60
  87.2 2.6 broadcast_select_fusion.2
  95.1 2.6 broadcast_select_fusion.2
  103.0 2.6 broadcast_select_fusion.2
  142.4 2.6 broadcast_select_fusion.2
  150.2 2.6 broadcast_select_fusion.2
  197.5 2.6 broadcast_select_fusion.2
  205.4 2.6 broadcast_select_fusion.2
  221.1 2.6 broadcast_select_fusion.2
  244.7 2.6 broadcast_select_fusion.2
  252.6 2.6 broadcast_select_fusion.2
  276.3 2.6 broadcast_select_fusion.2
  284.1 2.6 broadcast_select_fusion.2
  307.8 2.6 broadcast_select_fusion.2
  315.7 2.6 broadcast_select_fusion.2
  339.3 2.6 broadcast_select_fusion.2
  347.2 2.6 broadcast_select_fusion.2
  363.0 2.6 broadcast_select_fusion.2
  370.8 2.6 broadcast_select_fusion.2
  386.6 2.6 broadcast_select_fusion.2
  410.2 2.6 broadcast_select_fusion.2
  433.8 2.6 broadcast_select_fusion.2
  441.6 2.6 broadcast_select_fusion.2
  465.3 2.6 broadcast_select_fusion.2
  473.2 2.6 broadcast_select_fusion.2
  488.9 2.6 broadcast_select_fusion.2
  536.1 2.6 broadcast_select_fusion.2
  544.0 2.6 broadcast_select_fusion.2
  567.7 2.6 broadcast_select_fusion.2
  575.5 2.6 broadcast_select_fusion.2
  599.2 2.6 broadcast_select_fusion.2
  607.1 2.6 broadcast_select_fusion.2
  622.8 2.6 broadcast_select_fusion.2
  630.7 2.6 broadcast_select_fusion.2
  638.6 2.6 broadcast_select_fusion.2
  654.4 2.6 broadcast_select_fusion.2
  662.2 2.6 broadcast_select_fusion.2
  1064.1 2.7 broadcast_select_fusion.2
  5917.0 2.7 broadcast_select_fusion.2
  8728.9 2.7 broadcast_select_fusion.2
  9004.6 2.6 broadcast_select_fusion.2
  11564.5 2.7 broadcast_select_fusion.2
  18701.5 2.7 broadcast_select_fusion.2
  18993.0 2.7 broadcast_select_fusion.2
  24280.8 14.5 all-to-all-start.2
  24299.9 63.3 collective-permute-done
  24364.8 9.0 collective-permute-done.1
  24374.0 6.9 collective-permute-done.2
  24383.2 5.8 collective-permute-done.3
  24390.8 8.3 collective-permute-done.5
  24403.0 12.9 all-gather
  24416.0 21.3 all_gather.7
  24441.0 51.6 all_to_all.36
  24495.1 8.4 all-to-all-start.3
  24503.6 62.5 all-to-all-done.3
  24566.1 16.5 broadcast_multiply_fusion
  24582.6 9.8 copy.25
  24592.4 12.3 bitcast_subtract_fusion
  (15382 shorter events, 24102.9 us)
Async XLA Ops:
  0.0 9.1 copy-start.3
  0.0 9.1 copy-start.4
  8.5 22.2 copy-start.5
  9.8 66.9 copy-start.2
  19.5 22.9 all-to-all-start
  42.5 34.2 all-to-all-start.1
  24280.8 157.2 all-to-all-start.2
  24295.3 107.7 copy-start.1
  24295.3 142.2 copy-start
  24297.9 65.3 collective-permute-start
  24364.3 9.4 collective-permute-start.1
  24373.8 7.1 collective-permute-start.2
  24381.0 8.0 collective-permute-start.3
  24388.9 1.6 collective-permute-start.4
  24390.6 8.4 collective-permute-start.5
  24399.1 38.5 collective-permute-start.6
  24440.1 0.7 collective-permute-start.7
  24495.1 71.0 all-to-all-start.3

commit v2 on v1

--- a/solution.py
+++ b/solution.py
@@ -52,12 +52,12 @@
     )
     got_values = lax.all_to_all(send_values, ("prow", "pcol"), 0, 0, tiled=True)
     got_place = lax.all_to_all(send_place, ("prow", "pcol"), 0, 0, tiled=True)
-    place = got_place.astype(jnp.int32)
-    index = jnp.stack([place // blocks_local, place % blocks_local * 128], axis=1)
-    numbers = lax.ScatterDimensionNumbers(
-        update_window_dims=(1,), inserted_window_dims=(0,), scatter_dims_to_operand_dims=(0, 1)
+    flat = (
+        front.reshape(rows_local * blocks_local, 128)
+        .at[got_place.astype(jnp.int32)]
+        .add(got_values)
     )
-    return lax.scatter_add(front, index, got_values, numbers)
+    return flat.reshape(rows_local, cols_local)
 
 
 def body(front, fill_blocks, seg_values, seg_row, seg_block, seg_live, panel_start, panel_inverse):

time: 25100 us -> 417 us (0.02); the launches traced: 24600 us -> 416 us
  other arithmetic: 14300 us -> 45.3 us
  local copies, waits for them, and re-layouts: 9990 us -> 52.1 us
    scatter-add x6144 -> x1, other arithmetic: 14200 us -> 25.8 us  [assemble(): flat = front.reshape(rows_local * blocks_local, 128).at[got_place.astype(...]
    scatter-add x9216 -> x0, local copies, waits for them, and re-layouts: 9950 us -> none
where the time goes in v2:
time: 417 us; the launch traced here: 416 us
  waiting for transfers between devices  165 us (40%)
  blocking collectives  87.5 us (21%)
  local copies, waits for them, and re-layouts  52.1 us (12%)
  other arithmetic  45.3 us (11%)
  starting transfers between devices  39.7 us (10%)
  matrix products  17.8 us (4%)
  between operations  8.46 us (2%)
    ppermute x7, waiting for transfers between devices, spread(): x = x + lax.ppermute(x, ('prow', 'pcol'), pairs)  90.2 us
    all_to_all x1, waiting for transfers between devices, gather_rows(): got = lax.all_to_all(spread, axis, 0, 0, tiled=False)  62.5 us
    all_to_all x1, blocking collectives, gather_rows(): got = lax.all_to_all(spread, axis, 0, 0, tiled=False)  51.6 us
    scatter-add x1, other arithmetic, assemble(): flat = front.reshape(rows_local * blocks_local, 128).at[got_place.astype(...  25.8 us
    all_gather x1, blocking collectives, body(): lax.all_gather(lax.all_gather(fill_blocks, 'prow', axis=0, tiled=True), '...  22.8 us
    dot_general x2, matrix products, dot_t(): lax.dot_general(a, b, dims, precision=HIGHEST, preferred_element_type=jnp...  16.9 us
    all_gather x1, blocking collectives, body(): lax.all_gather(fill_blocks, 'prow', axis=0, tiled=True)  13.1 us
    sub x1, other arithmetic, body(): return assembled - shaped.reshape(rows_local, cols_local)  12.3 us
  transfers between devices with their start and end apart: 12, of which 9 were waited for; matrix products, arithmetic and copies ran while one was open for 5% of the time, Pallas kernels for 0%

profile of v2, /device:TPU:0, one launch (start us, length us, event | category | flops | bytes accessed | tf_op | source)
XLA Modules:
  0.0 416.1 jit_solution(7449370376802774948)
XLA Ops:
  0.7 0.7 fusion.28
  1.4 0.1 copy.20
  1.5 0.3 fusion.8
  1.9 0.1 broadcast_add_fusion
  2.0 0.0 copy-start.2
  2.0 0.3 copy.21
  2.3 0.6 fusion.7
  3.0 8.1 %scatter_custom_fusion = f32[3072]{0:T(1024)S(1)} fusion(s32[2048]{0:T(1024)S(1)} %compare_select_fusion.1, f32[2048]{0:T(1024)S(1)} %get-tuple-element.9, f32[]{:T(128)} %constant.124.clone.1), kind=kCustom, calls=%fused_computation.61 | custom fusion | bytes 12292 | tf_op jit(solution)/shard_map/scatter | solution.py:51
  11.0 0.7 all_to_all.23
  11.8 11.2 %all-to-all-start = ((f32[128,24,1]{1,2,0:T(1,128)}), f32[128,24,1]{1,2,0:T(1,128)S(1)}, u32[]{:S(2)}, u32[]{:S(2)}) async-start(f32[128,24,1]{1,2,0:T(1,128)} %bitcast.5), calls=%async_computation | async-start | bytes 131072 | tf_op jit(solution)/shard_map/all_to_all | solution.py:54
  22.9 7.2 %scatter_custom_fusion.1 = f32[3072,128]{1,0:T(8,128)} fusion(s32[2048]{0:T(1024)S(1)} %compare_select_fusion.1, f32[2048,128]{1,0:T(8,128)} %param.10, f32[]{:T(128)} %constant.124.clone.1), kind=kCustom, calls=%fused_computation.18 | custom fusion | bytes 1573376 | tf_op jit(solution)/shard_map/scatter | solution.py:48
  30.1 2.3 all-to-all-done
  32.4 7.5 %all-to-all-start.1 = ((f32[128,24,128]{2,1,0:T(8,128)}), f32[128,24,128]{2,1,0:T(8,128)S(1)}, u32[]{:S(2)}, u32[]{:S(2)}) async-start(f32[128,24,128]{2,1,0:T(8,128)} %bitcast.7), calls=%async_computation.1 | async-start | bytes 3145728 | tf_op jit(solution)/shard_map/all_to_all | solution.py:53
  39.9 0.7 fusion.36
  44.5 9.3 %reshape.67 = f32[16384,128]{1,0:T(8,128)} reshape(f32[2048,1024]{1,0:T(8,128)} %param.8) | data formatting | bytes 16777216 | tf_op jit(solution)/shard_map/reshape | solution.py:56
  53.8 0.2 convert_reduce_fusion
  54.0 0.1 convert_element_type.33
  54.1 10.3 %all-to-all-done.1 = f32[128,24,128]{2,1,0:T(8,128)S(1)} async-done(((f32[128,24,128]{2,1,0:T(8,128)}), f32[128,24,128]{2,1,0:T(8,128)S(1)}, u32[]{:S(2)}, u32[]{:S(2)}) %all-to-all-start.1) | async-done | bytes 1572896 | tf_op jit(solution)/shard_map/all_to_all | solution.py:53
  64.4 25.8 %scatter_fusion = f32[16384,128]{1,0:T(8,128)} fusion(f32[16384,128]{1,0:T(8,128)} %reshape.67, s32[3072]{0:T(1024)S(1)} %bitcast.60, f32[3072,128]{1,0:T(8,128)S(1)} %bitcast.58), kind=kCustom, calls=%fused_computation.2 | custom fusion | flops 393216 | bytes 4730880 | tf_op jit(solution)/shard_map/scatter-add | solution.py:58
  90.1 9.3 %reshape.69 = f32[2048,1024]{1,0:T(8,128)} reshape(f32[16384,128]{1,0:T(8,128)} %scatter_fusion) | data formatting | bytes 16777216 | tf_op jit(solution)/shard_map/reshape | solution.py:60
  99.4 2.5 constant_dynamic-slice_fusion.1
  101.9 2.5 pad_maximum_fusion
  104.5 4.6 %all-to-all-start.2 = ((f32[16,128,512]{2,1,0:T(8,128)}), f32[16,128,512]{2,1,0:T(8,128)}, u32[]{:S(2)}, u32[]{:S(2)}) async-start(f32[16,128,512]{2,1,0:T(8,128)} %bitcast.57), calls=%async_computation.2 | async-start | bytes 8388608 | tf_op jit(solution)/shard_map/all_to_all | solution.py:90
  109.0 0.0 copy-start.1
  109.0 0.0 copy-start
  110.5 1.1 dynamic-slice_select_fusion
  111.6 1.8 collective-permute-start
  113.5 60.9 %collective-permute-done = f32[256,256]{1,0:T(8,128)S(1)} collective-permute-done((f32[256,256]{1,0:T(8,128)S(1)}, f32[256,256]{1,0:T(8,128)S(1)}, u32[]{:S(2)}, u32[]{:S(2)}) %collective-permute-start) | collective-permute-done | bytes 262176 | tf_op jit(solution)/shard_map/ppermute | solution.py:28
  174.4 1.1 fusion.40
  175.5 0.1 collective-permute-start.1
  175.7 7.8 %collective-permute-done.1 = f32[256,256]{1,0:T(8,128)S(1)} collective-permute-done((f32[256,256]{1,0:T(8,128)S(1)}, f32[256,256]{1,0:T(8,128)S(1)}, u32[]{:S(2)}, u32[]{:S(2)}) %collective-permute-start.1) | collective-permute-done | bytes 262176 | tf_op jit(solution)/shard_map/ppermute | solution.py:28
  183.5 0.1 collective-permute-start.2
  183.6 7.2 %collective-permute-done.2 = f32[256,256]{1,0:T(8,128)S(1)} collective-permute-done((f32[256,256]{1,0:T(8,128)S(1)}, f32[256,256]{1,0:T(8,128)S(1)}, u32[]{:S(2)}, u32[]{:S(2)}) %collective-permute-start.2) | collective-permute-done | bytes 262176 | tf_op jit(solution)/shard_map/ppermute | solution.py:28
  190.9 3.9 collective-permute-start.3
  194.8 4.4 %collective-permute-done.3 = f32[256,256]{1,0:T(8,128)S(1)} collective-permute-done((f32[256,256]{1,0:T(8,128)S(1)}, f32[256,256]{1,0:T(8,128)S(1)}, u32[]{:S(2)}, u32[]{:S(2)}) %collective-permute-start.3) | collective-permute-done | bytes 262176 | tf_op jit(solution)/shard_map/ppermute | solution.py:28
  199.2 0.1 collective-permute-start.4
  199.3 1.5 collective-permute-done.4
  200.8 0.1 collective-permute-start.5
  200.9 8.3 %collective-permute-done.5 = f32[256,256]{1,0:T(8,128)S(1)} collective-permute-done((f32[256,256]{1,0:T(8,128)S(1)}, f32[256,256]{1,0:T(8,128)S(1)}, u32[]{:S(2)}, u32[]{:S(2)}) %collective-permute-start.5) | collective-permute-done | bytes 262176 | tf_op jit(solution)/shard_map/ppermute | solution.py:28
  209.3 1.3 collective-permute-start.6
  212.7 0.0 copy-done.1
  212.7 13.1 %all-gather = s32[8,16,8]{1,2,0:T(8,128)S(1)} all-gather(s32[1,16,8]{1,2,0:T(8,128)S(1)} %bitcast.61), channel_id=1, replica_groups=mesh['prow'=8,'pcol'=16] {'prow'}, dimensions={0}, use_global_device_ids=true | all-gather | bytes 4608 | tf_op jit(solution)/shard_map/all_gather | solution.py:74
  225.9 0.1 reshape.99
  225.9 22.8 %all_gather.7 = s32[128,128]{0,1:T(8,128)S(1)} all-gather(s32[128,8]{0,1:T(8,128)S(1)} %reshape.99), channel_id=1, replica_groups=mesh['prow'=8,'pcol'=16] {'pcol'}, dimensions={1}, use_global_device_ids=true | all-gather | bytes 69632 | tf_op jit(solution)/shard_map/all_gather | solution.py:73
  248.7 0.2 fusion.35
  248.9 0.1 broadcast_bitcast_fusion
  249.0 0.0 collective-permute-done.6
  249.0 0.4 fusion.15
  249.4 0.0 all-to-all-done.2
  249.4 1.1 dynamic-slice_bitcast_fusion
  250.5 0.3 fusion.17
  250.8 0.4 fusion.5
  251.2 0.3 fusion.13
  251.5 0.7 collective-permute-start.7
  252.2 0.0 collective-permute-done.7
  252.2 0.3 broadcast_in_dim.47
  252.4 51.6 %all_to_all.36 = f32[8,128,512]{2,1,0:T(8,128)S(1)} all-to-all(f32[8,128,512]{2,1,0:T(8,128)S(1)} %broadcast_in_dim.47), channel_id=1, replica_groups=mesh['prow'=8,'pcol'=16] {'prow'}, dimensions={0} | all-to-all | bytes 4194304 | tf_op jit(solution)/shard_map/all_to_all | solution.py:21
  304.0 2.5 broadcast_in_dim.46
  306.6 8.4 %all-to-all-start.3 = ((f32[16,128,512]{2,1,0:T(8,128)}), f32[16,128,512]{2,1,0:T(8,128)}, u32[]{:S(2)}, u32[]{:S(2)}) async-start(f32[16,128,512]{2,1,0:T(8,128)} %broadcast_in_dim.46), calls=%async_computation.3 | async-start | bytes 8388608 | tf_op jit(solution)/shard_map/all_to_all | solution.py:21
  315.0 0.1 copy.24
  315.0 62.5 %all-to-all-done.3 = f32[16,128,512]{2,1,0:T(8,128)} async-done(((f32[16,128,512]{2,1,0:T(8,128)}), f32[16,128,512]{2,1,0:T(8,128)}, u32[]{:S(2)}, u32[]{:S(2)}) %all-to-all-start.3) | async-done | bytes 4194336 | tf_op jit(solution)/shard_map/all_to_all | solution.py:21
  377.6 16.5 %broadcast_multiply_fusion = f32[16,128,8,128]{3,1,2,0:T(8,128)S(1)} fusion(f32[16,8]{1,0:T(8,128)S(1)} %copy.24, f32[16,128,512]{2,1,0:T(8,128)} %all-to-all-done.3, f32[8,128,512]{2,1,0:T(8,128)S(1)} %all_to_all.36), kind=kOutput, calls=%fused_computation.7 | convolution fusion | flops 12886999040 | bytes 14680576 | tf_op jit(solution)/shard_map/dot_general | solution.py:16
  394.1 9.8 %copy.25 = f32[16,128,8,128]{3,2,1,0:T(8,128)} copy(f32[16,128,8,128]{3,1,2,0:T(8,128)S(1)} %broadcast_multiply_fusion) | data formatting | bytes 16777216 | tf_op jit(solution)/shard_map/mul | solution.py:117
  403.8 12.3 %bitcast_subtract_fusion = f32[2048,1024]{1,0:T(8,128)} fusion(f32[2048,1024]{1,0:T(8,128)} %reshape.69, f32[256,8,8,128]{3,2,1,0:T(8,128)} %bitcast.56), kind=kLoop, calls=%fused_computation.3 | loop fusion | flops 2097152 | bytes 25165824 | tf_op jit(solution)/shard_map/sub | solution.py:118
  (15 shorter events, 0.3 us)
Async XLA Ops:
  2.0 37.9 %copy-start.2 = (s32[2]{0:T(128)S(1)}, s32[2]{0:T(128)}, u32[]{:S(2)}) copy-start(s32[2]{0:T(128)} %param.14) | copy-start | bytes 28
  11.8 20.6 %all-to-all-start = ((f32[128,24,1]{1,2,0:T(1,128)}), f32[128,24,1]{1,2,0:T(1,128)S(1)}, u32[]{:S(2)}, u32[]{:S(2)}) async-start(f32[128,24,1]{1,2,0:T(1,128)} %bitcast.5), calls=%async_computation | async-start | bytes 131072 | tf_op jit(solution)/shard_map/all_to_all | solution.py:54
  32.4 32.0 %all-to-all-start.1 = ((f32[128,24,128]{2,1,0:T(8,128)}), f32[128,24,128]{2,1,0:T(8,128)S(1)}, u32[]{:S(2)}, u32[]{:S(2)}) async-start(f32[128,24,128]{2,1,0:T(8,128)} %bitcast.7), calls=%async_computation.1 | async-start | bytes 3145728 | tf_op jit(solution)/shard_map/all_to_all | solution.py:53
  104.5 144.9 %all-to-all-start.2 = ((f32[16,128,512]{2,1,0:T(8,128)}), f32[16,128,512]{2,1,0:T(8,128)}, u32[]{:S(2)}, u32[]{:S(2)}) async-start(f32[16,128,512]{2,1,0:T(8,128)} %bitcast.57), calls=%async_computation.2 | async-start | bytes 8388608 | tf_op jit(solution)/shard_map/all_to_all | solution.py:90
  109.0 103.7 %copy-start.1 = (s32[16,8]{0,1:T(8,128)S(1)}, s32[16,8]{0,1:T(8,128)}, u32[]{:S(2)}) copy-start(s32[16,8]{0,1:T(8,128)} %param.9) | copy-start | bytes 1540
  109.0 140.0 %copy-start = (f32[2,256,256]{2,1,0:T(8,128)S(1)}, f32[2,256,256]{2,1,0:T(8,128)}, u32[]{:S(2)}) copy-start(f32[2,256,256]{2,1,0:T(8,128)} %param.15) | copy-start | bytes 1572868
  111.6 62.8 %collective-permute-start = (f32[256,256]{1,0:T(8,128)S(1)}, f32[256,256]{1,0:T(8,128)S(1)}, u32[]{:S(2)}, u32[]{:S(2)}) collective-permute-start(f32[256,256]{1,0:T(8,128)S(1)} %dynamic-slice_select_fusion), channel_id=1, source_target_pairs={{0,1},{1,0},{2,3},{3,2},{4,5},{5,4},{6,7},{7,6},{8,9},{9,8},{10,11... | collective-permute-start | bytes 786440 | tf_op jit(solution)/shard_map/ppermute | solution.py:28
  175.5 8.0 %collective-permute-start.1 = (f32[256,256]{1,0:T(8,128)S(1)}, f32[256,256]{1,0:T(8,128)S(1)}, u32[]{:S(2)}, u32[]{:S(2)}) collective-permute-start(f32[256,256]{1,0:T(8,128)S(1)} %fusion.40), channel_id=1, source_target_pairs={{0,2},{1,3},{2,0},{3,1},{4,6},{5,7},{6,4},{7,5},{8,10},{9,11},{10,... | collective-permute-start | bytes 786440 | tf_op jit(solution)/shard_map/ppermute | solution.py:28
  183.5 7.3 %collective-permute-start.2 = (f32[256,256]{1,0:T(8,128)S(1)}, f32[256,256]{1,0:T(8,128)S(1)}, u32[]{:S(2)}, u32[]{:S(2)}) collective-permute-start(f32[256,256]{1,0:T(8,128)S(1)} %add.119), channel_id=1, source_target_pairs={{0,4},{1,5},{2,6},{3,7},{4,0},{5,1},{6,2},{7,3},{8,12},{9,13},{10,... | collective-permute-start | bytes 786440 | tf_op jit(solution)/shard_map/ppermute | solution.py:28
  190.9 8.3 %collective-permute-start.3 = (f32[256,256]{1,0:T(8,128)S(1)}, f32[256,256]{1,0:T(8,128)S(1)}, u32[]{:S(2)}, u32[]{:S(2)}) collective-permute-start(f32[256,256]{1,0:T(8,128)S(1)} %add.120), channel_id=1, source_target_pairs={{0,8},{1,9},{2,10},{3,11},{4,12},{5,13},{6,14},{7,15},{8,0},{9,1},... | collective-permute-start | bytes 786440 | tf_op jit(solution)/shard_map/ppermute | solution.py:28
  199.2 1.6 collective-permute-start.4
  200.8 8.4 %collective-permute-start.5 = (f32[256,256]{1,0:T(8,128)S(1)}, f32[256,256]{1,0:T(8,128)S(1)}, u32[]{:S(2)}, u32[]{:S(2)}) collective-permute-start(f32[256,256]{1,0:T(8,128)S(1)} %add.122), channel_id=1, source_target_pairs={{0,32},{1,33},{2,34},{3,35},{4,36},{5,37},{6,38},{7,39},{8,40},{9,... | collective-permute-start | bytes 786440 | tf_op jit(solution)/shard_map/ppermute | solution.py:28
  209.3 39.7 %collective-permute-start.6 = (f32[256,256]{1,0:T(8,128)S(1)}, f32[256,256]{1,0:T(8,128)S(1)}, u32[]{:S(2)}, u32[]{:S(2)}) collective-permute-start(f32[256,256]{1,0:T(8,128)S(1)} %add.123), channel_id=1, source_target_pairs={{0,64},{1,65},{2,66},{3,67},{4,68},{5,69},{6,70},{7,71},{8,72},{9,... | collective-permute-start | bytes 786440 | tf_op jit(solution)/shard_map/ppermute | solution.py:28
  251.5 0.7 collective-permute-start.7
  306.6 71.0 %all-to-all-start.3 = ((f32[16,128,512]{2,1,0:T(8,128)}), f32[16,128,512]{2,1,0:T(8,128)}, u32[]{:S(2)}, u32[]{:S(2)}) async-start(f32[16,128,512]{2,1,0:T(8,128)} %broadcast_in_dim.46), calls=%async_computation.3 | async-start | bytes 8388608 | tf_op jit(solution)/shard_map/all_to_all | solution.py:21

commit v3 on v2

--- a/solution.py
+++ b/solution.py
@@ -70,10 +70,6 @@
     r = lax.axis_index("prow")
     c = lax.axis_index("pcol")
 
-    mask_all = lax.all_gather(
-        lax.all_gather(fill_blocks, "prow", axis=0, tiled=True), "pcol", axis=1, tiled=True
-    ).astype(jnp.float32)
-
     assembled = assemble(front, seg_values, seg_row, seg_block, seg_live, n_prow, n_pcol)
 
     owner = [panel_start[k] // blocks_local for k in range(PANELS)]
@@ -86,16 +82,20 @@
     x_mine = jnp.where((r == src_row) & (c == owner[0]), x_local, 0.0)
     x_cols = spread(x_mine, n_prow * n_pcol)
 
+    mask_local = fill_blocks.astype(jnp.float32)
+    mask_two = lax.dynamic_slice_in_dim(mask_local, offset[1] // 128, pw // 128, 1)
+    mask_two = jnp.repeat(mask_two.reshape(n_pcol, piece_rows // 128, pw // 128), 128, axis=2)
+    mask_two = jnp.pad(mask_two.reshape(n_pcol, 1, pw), ((0, 0), (0, 0), (0, (PANELS - 1) * pw)))
     send = jnp.concatenate(cols, axis=1).reshape(n_pcol, piece_rows, PANELS * pw)
+    send = jnp.concatenate([send, mask_two], axis=1)
     recv = lax.all_to_all(send, "pcol", 0, 0, tiled=False)
-    piece0 = lax.dynamic_index_in_dim(recv, owner[0], 0, keepdims=False)[:, :pw]
-    piece1 = lax.dynamic_index_in_dim(recv, owner[1], 0, keepdims=False)[:, pw:]
+    piece0 = lax.dynamic_index_in_dim(recv, owner[0], 0, keepdims=False)[:piece_rows, :pw]
+    from_two = lax.dynamic_index_in_dim(recv, owner[1], 0, keepdims=False)
+    piece1 = from_two[:piece_rows, pw:]
+    m_piece = from_two[piece_rows:, :pw]
 
     left0 = dot(piece0, panel_inverse[0])
     left0_x = dot(x_cols, panel_inverse[0])
-    piece_block = (r * rows_local + c * piece_rows) // 128
-    m_row = lax.dynamic_slice(mask_all, (piece_block, panel_start[1]), (1, pw // 128))
-    m_piece = jnp.repeat(m_row, 128, axis=1)
     piece1 = piece1 - dot_t(left0, left0_x) * m_piece
     left1 = dot(piece1, panel_inverse[1])
     piece = jnp.concatenate([left0, left1], axis=1)
@@ -110,10 +110,9 @@
             dr = first % cols_local // piece_rows
             perm.append((sr * n_pcol + sc, dr * n_pcol + dc))
     moved = lax.ppermute(piece, ("prow", "pcol"), perm)
-    left_cols = gather_rows(moved, "prow", n_prow)
+    left_cols = lax.all_gather(moved, "prow", axis=0, tiled=True)
 
-    product = dot_t(left_rows, left_cols)
-    mask_local = fill_blocks.astype(jnp.float32)
+    product = dot(left_rows, left_cols.T)
     shaped = product.reshape(rows_local // 128, 128, blocks_local, 128) * mask_local[:, None, :, None]
     return assembled - shaped.reshape(rows_local, cols_local)
 

time: 417 us -> 365 us (0.88); the launches traced: 416 us -> 360 us
  blocking collectives: 87.5 us -> 0 us
  starting transfers between devices: 39.7 us -> 51.8 us
  between operations: 8.46 us -> 19.8 us
  waiting for transfers between devices: 165 us -> 171 us
    all_gather x0 -> x1, waiting for transfers between devices: none -> 62.4 us  [body(): left_cols = lax.all_gather(moved, 'prow', axis=0, tiled=True)]
    all_to_all x1, waiting for transfers between devices: 62.5 us -> 3.35 us  [gather_rows(): got = lax.all_to_all(spread, axis, 0, 0, tiled=False)]
    all_to_all x1 -> x0, blocking collectives: 51.6 us -> none  [gather_rows(): got = lax.all_to_all(spread, axis, 0, 0, tiled=False)]
    all_gather x2 -> x0, blocking collectives: 35.9 us -> none  [the longest x1 22.8 us: body(): lax.all_gather(lax.all_gather(fill_blocks, 'prow', axis=0, tiled=True), '...]
    dot_general x3 -> x4, matrix products: 0.95 us -> 18 us  [dot(): return jnp.dot(a, b, precision=HIGHEST, preferred_element_type=jnp.float32)]
    dot_general x2 -> x1, matrix products: 16.9 us -> 0.4 us  [dot_t(): lax.dot_general(a, b, dims, precision=HIGHEST, preferred_element_type=jnp...]
    ppermute x7, starting transfers between devices: 7.44 us -> 20.3 us  [spread(): x = x + lax.ppermute(x, ('prow', 'pcol'), pairs)]
  transfers between devices with their start and end apart: 12 -> 13, of which waited for: 9 -> 11; matrix products, arithmetic and copies ran while one was open for 5% -> 6% of each run, Pallas kernels for 0% -> 0%
where the time goes in v3:
time: 365 us; the launch traced here: 360 us
  waiting for transfers between devices  171 us (47%)
  local copies, waits for them, and re-layouts  52.5 us (14%)
  starting transfers between devices  51.8 us (14%)
  other arithmetic  46 us (13%)
  between operations  19.8 us (5%)
  matrix products  18.4 us (5%)
    ppermute x7, waiting for transfers between devices, spread(): x = x + lax.ppermute(x, ('prow', 'pcol'), pairs)  92.5 us
    all_gather x1, waiting for transfers between devices, body(): left_cols = lax.all_gather(moved, 'prow', axis=0, tiled=True)  62.4 us
    scatter-add x1, other arithmetic, assemble(): flat = front.reshape(rows_local * blocks_local, 128).at[got_place.astype(...  26 us
    ppermute x7, starting transfers between devices, spread(): x = x + lax.ppermute(x, ('prow', 'pcol'), pairs)  20.3 us
    dot_general x4, matrix products, dot(): return jnp.dot(a, b, precision=HIGHEST, preferred_element_type=jnp.float32)  18 us
    sub x1, other arithmetic, body(): return assembled - shaped.reshape(rows_local, cols_local)  12.3 us
    all_to_all x1, starting transfers between devices, assemble(): got_place = lax.all_to_all(send_place, ('prow', 'pcol'), 0, 0, tiled=True)  11.2 us
    all_to_all x1, waiting for transfers between devices, assemble(): got_values = lax.all_to_all(send_values, ('prow', 'pcol'), 0, 0, tiled=True)  10.6 us
  transfers between devices with their start and end apart: 13, of which 11 were waited for; matrix products, arithmetic and copies ran while one was open for 6% of the time, Pallas kernels for 0%

profile of v3, /device:TPU:0, one launch (start us, length us, event | category | flops | bytes accessed | tf_op | source)
XLA Modules:
  0.0 359.8 jit_solution(17256498540148943174)
XLA Ops:
  7.2 0.7 fusion.27
  7.9 0.1 copy.16
  8.0 0.3 fusion.7
  8.4 0.1 broadcast_add_fusion
  8.5 0.0 copy-start.3
  8.5 0.0 copy-start.2
  8.5 0.3 copy.17
  8.9 0.6 fusion.6
  9.5 8.1 %scatter_custom_fusion = f32[3072]{0:T(1024)S(1)} fusion(s32[2048]{0:T(1024)S(1)} %compare_select_fusion.1, f32[2048]{0:T(1024)S(1)} %get-tuple-element.9, f32[]{:T(128)} %constant.125.clone.1), kind=kCustom, calls=%fused_computation.62 | custom fusion | bytes 12292 | tf_op jit(solution)/shard_map/scatter | solution.py:51
  17.6 0.7 all_to_all.20
  18.3 11.2 %all-to-all-start = ((f32[128,24,1]{1,2,0:T(1,128)}), f32[128,24,1]{1,2,0:T(1,128)S(1)}, u32[]{:S(2)}, u32[]{:S(2)}) async-start(f32[128,24,1]{1,2,0:T(1,128)} %bitcast.5), calls=%async_computation | async-start | bytes 131072 | tf_op jit(solution)/shard_map/all_to_all | solution.py:54
  29.5 7.2 %scatter_custom_fusion.1 = f32[3072,128]{1,0:T(8,128)} fusion(s32[2048]{0:T(1024)S(1)} %compare_select_fusion.1, f32[2048,128]{1,0:T(8,128)} %param.10, f32[]{:T(128)} %constant.125.clone.1), kind=kCustom, calls=%fused_computation.19 | custom fusion | bytes 1573376 | tf_op jit(solution)/shard_map/scatter | solution.py:48
  36.6 2.3 all-to-all-done
  38.9 7.5 %all-to-all-start.1 = ((f32[128,24,128]{2,1,0:T(8,128)}), f32[128,24,128]{2,1,0:T(8,128)S(1)}, u32[]{:S(2)}, u32[]{:S(2)}) async-start(f32[128,24,128]{2,1,0:T(8,128)} %bitcast.7), calls=%async_computation.1 | async-start | bytes 3145728 | tf_op jit(solution)/shard_map/all_to_all | solution.py:53
  46.4 0.0 copy-done.3
  46.4 0.6 fusion.34
  50.6 0.1 copy.19
  50.7 9.2 %reshape.64 = f32[16384,128]{1,0:T(8,128)} reshape(f32[2048,1024]{1,0:T(8,128)} %param.8) | data formatting | bytes 16777216 | tf_op jit(solution)/shard_map/reshape | solution.py:56
  59.9 0.2 convert_reduce_fusion
  60.1 0.1 convert_element_type.32
  60.3 10.6 %all-to-all-done.1 = f32[128,24,128]{2,1,0:T(8,128)S(1)} async-done(((f32[128,24,128]{2,1,0:T(8,128)}), f32[128,24,128]{2,1,0:T(8,128)S(1)}, u32[]{:S(2)}, u32[]{:S(2)}) %all-to-all-start.1) | async-done | bytes 1572896 | tf_op jit(solution)/shard_map/all_to_all | solution.py:53
  70.9 26.0 %scatter_fusion = f32[16384,128]{1,0:T(8,128)} fusion(f32[16384,128]{1,0:T(8,128)} %reshape.64, s32[3072]{0:T(1024)S(1)} %bitcast.60, f32[3072,128]{1,0:T(8,128)S(1)} %bitcast.56), kind=kCustom, calls=%fused_computation.2 | custom fusion | flops 393216 | bytes 4730880 | tf_op jit(solution)/shard_map/scatter-add | solution.py:58
  96.9 9.3 %reshape.66 = f32[2048,1024]{1,0:T(8,128)} reshape(f32[16384,128]{1,0:T(8,128)} %scatter_fusion) | data formatting | bytes 16777216 | tf_op jit(solution)/shard_map/reshape | solution.py:60
  106.1 2.5 constant_dynamic-slice_fusion.2
  108.7 0.6 pad_maximum_fusion
  109.3 0.1 broadcast_in_dim.37
  109.4 2.6 select_maximum_fusion
  112.0 4.6 %all-to-all-start.2 = ((f32[16,129,512]{2,1,0:T(8,128)}), f32[16,129,512]{2,1,0:T(8,128)}, u32[]{:S(2)}, u32[]{:S(2)}) async-start(f32[16,129,512]{2,1,0:T(8,128)} %select_maximum_fusion), calls=%async_computation.2 | async-start | bytes 8912896 | tf_op jit(solution)/shard_map/all_to_all | solution.py:91
  116.6 0.0 copy-start
  117.9 1.1 dynamic-slice_select_fusion
  119.1 1.8 collective-permute-start
  120.9 60.2 %collective-permute-done = f32[256,256]{1,0:T(8,128)S(1)} collective-permute-done((f32[256,256]{1,0:T(8,128)S(1)}, f32[256,256]{1,0:T(8,128)S(1)}, u32[]{:S(2)}, u32[]{:S(2)}) %collective-permute-start) | collective-permute-done | bytes 262176 | tf_op jit(solution)/shard_map/ppermute | solution.py:28
  181.0 1.1 fusion.39
  182.2 3.4 collective-permute-start.1
  185.6 4.5 %collective-permute-done.1 = f32[256,256]{1,0:T(8,128)S(1)} collective-permute-done((f32[256,256]{1,0:T(8,128)S(1)}, f32[256,256]{1,0:T(8,128)S(1)}, u32[]{:S(2)}, u32[]{:S(2)}) %collective-permute-start.1) | collective-permute-done | bytes 262176 | tf_op jit(solution)/shard_map/ppermute | solution.py:28
  190.2 0.5 collective-permute-start.2
  190.7 6.7 %collective-permute-done.2 = f32[256,256]{1,0:T(8,128)S(1)} collective-permute-done((f32[256,256]{1,0:T(8,128)S(1)}, f32[256,256]{1,0:T(8,128)S(1)}, u32[]{:S(2)}, u32[]{:S(2)}) %collective-permute-start.2) | collective-permute-done | bytes 262176 | tf_op jit(solution)/shard_map/ppermute | solution.py:28
  197.5 5.5 %collective-permute-start.3 = (f32[256,256]{1,0:T(8,128)S(1)}, f32[256,256]{1,0:T(8,128)S(1)}, u32[]{:S(2)}, u32[]{:S(2)}) collective-permute-start(f32[256,256]{1,0:T(8,128)S(1)} %add.117), channel_id=1, source_target_pairs={{0,8},{1,9},{2,10},{3,11},{4,12},{5,13},{6,14},{7,15},{8,0},{9,1},... | collective-permute-start | bytes 786440 | tf_op jit(solution)/shard_map/ppermute | solution.py:28
  203.0 4.4 %collective-permute-done.3 = f32[256,256]{1,0:T(8,128)S(1)} collective-permute-done((f32[256,256]{1,0:T(8,128)S(1)}, f32[256,256]{1,0:T(8,128)S(1)}, u32[]{:S(2)}, u32[]{:S(2)}) %collective-permute-start.3) | collective-permute-done | bytes 262176 | tf_op jit(solution)/shard_map/ppermute | solution.py:28
  207.4 0.1 collective-permute-start.4
  207.5 1.5 collective-permute-done.4
  209.0 8.6 %collective-permute-start.5 = (f32[256,256]{1,0:T(8,128)S(1)}, f32[256,256]{1,0:T(8,128)S(1)}, u32[]{:S(2)}, u32[]{:S(2)}) collective-permute-start(f32[256,256]{1,0:T(8,128)S(1)} %add.119), channel_id=1, source_target_pairs={{0,32},{1,33},{2,34},{3,35},{4,36},{5,37},{6,38},{7,39},{8,40},{9,... | collective-permute-start | bytes 786440 | tf_op jit(solution)/shard_map/ppermute | solution.py:28
  217.6 6.6 %collective-permute-done.5 = f32[256,256]{1,0:T(8,128)S(1)} collective-permute-done((f32[256,256]{1,0:T(8,128)S(1)}, f32[256,256]{1,0:T(8,128)S(1)}, u32[]{:S(2)}, u32[]{:S(2)}) %collective-permute-start.5) | collective-permute-done | bytes 262176 | tf_op jit(solution)/shard_map/ppermute | solution.py:28
  224.3 0.3 collective-permute-start.6
  225.1 8.7 %collective-permute-done.6 = f32[256,256]{1,0:T(8,128)S(1)} collective-permute-done((f32[256,256]{1,0:T(8,128)S(1)}, f32[256,256]{1,0:T(8,128)S(1)}, u32[]{:S(2)}, u32[]{:S(2)}) %collective-permute-start.6) | collective-permute-done | bytes 262176 | tf_op jit(solution)/shard_map/ppermute | solution.py:28
  233.8 0.4 fusion.14
  234.2 0.0 all-to-all-done.2
  234.2 1.1 dynamic-slice_bitcast_fusion
  235.3 0.3 fusion.16
  235.6 0.4 fusion.4
  236.0 0.3 fusion.12
  236.3 0.7 collective-permute-start.7
  237.0 2.5 broadcast_in_dim.40
  239.5 7.6 %all-to-all-start.3 = ((f32[16,128,512]{2,1,0:T(8,128)}), f32[16,128,512]{2,1,0:T(8,128)}, u32[]{:S(2)}, u32[]{:S(2)}) async-start(f32[16,128,512]{2,1,0:T(8,128)} %broadcast_in_dim.40), calls=%async_computation.3 | async-start | bytes 8388608 | tf_op jit(solution)/shard_map/all_to_all | solution.py:21
  247.1 0.0 all-gather.2.cloned.1.call-start
  247.2 0.0 collective-permute-done.7
  247.2 0.7 copy-done.1
  247.9 0.0 all-gather.2.cloned.1.call-update
  247.9 0.1 copy.20
  248.0 62.4 %all-gather.2.cloned.1.call-done = f32[1024,512]{1,0:T(8,128)} async-done(((f32[128,512]{1,0:T(8,128)}), f32[1024,512]{1,0:T(8,128)}) %all-gather.2.cloned.1.call-update) | async-done | bytes 2097168 | tf_op jit(solution)/shard_map/all_gather | solution.py:113
  310.4 3.4 all-to-all-done.3
  313.8 17.1 %broadcast_multiply_fusion = f32[16,128,8,128]{3,1,2,0:T(8,128)S(1)} fusion(f32[16,8]{1,0:T(8,128)S(1)} %copy.20, f32[8,128,512,1]{2,1,0,3:T(8,128)} %bitcast.57, f32[16,128,512]{2,1,0:T(8,128)} %all-to-all-done.3), kind=kOutput, calls=%fused_computation.9 | convolution fusion | flops 12886999040 | bytes 14680576 | tf_op jit(solution)/shard_map/dot_general | solution.py:11
  330.9 9.8 %copy.21 = f32[16,128,8,128]{3,2,1,0:T(8,128)} copy(f32[16,128,8,128]{3,1,2,0:T(8,128)S(1)} %broadcast_multiply_fusion) | data formatting | bytes 16777216 | tf_op jit(solution)/shard_map/mul | solution.py:116
  340.6 12.3 %bitcast_subtract_fusion = f32[2048,1024]{1,0:T(8,128)} fusion(f32[2048,1024]{1,0:T(8,128)} %reshape.66, f32[256,8,8,128]{3,2,1,0:T(8,128)} %bitcast.54), kind=kLoop, calls=%fused_computation.3 | loop fusion | flops 2097152 | bytes 25165824 | tf_op jit(solution)/shard_map/sub | solution.py:117
  (17 shorter events, 0.3 us)
Async XLA Ops:
  8.5 37.9 %copy-start.3 = (s32[2]{0:T(128)S(1)}, s32[2]{0:T(128)}, u32[]{:S(2)}) copy-start(s32[2]{0:T(128)} %param.14) | copy-start | bytes 28
  8.5 42.1 %copy-start.2 = (s32[16,8]{0,1:T(8,128)S(1)}, s32[16,8]{0,1:T(8,128)}, u32[]{:S(2)}) copy-start(s32[16,8]{0,1:T(8,128)} %param.9) | copy-start | bytes 1540
  18.3 20.6 %all-to-all-start = ((f32[128,24,1]{1,2,0:T(1,128)}), f32[128,24,1]{1,2,0:T(1,128)S(1)}, u32[]{:S(2)}, u32[]{:S(2)}) async-start(f32[128,24,1]{1,2,0:T(1,128)} %bitcast.5), calls=%async_computation | async-start | bytes 131072 | tf_op jit(solution)/shard_map/all_to_all | solution.py:54
  38.9 32.0 %all-to-all-start.1 = ((f32[128,24,128]{2,1,0:T(8,128)}), f32[128,24,128]{2,1,0:T(8,128)S(1)}, u32[]{:S(2)}, u32[]{:S(2)}) async-start(f32[128,24,128]{2,1,0:T(8,128)} %bitcast.7), calls=%async_computation.1 | async-start | bytes 3145728 | tf_op jit(solution)/shard_map/all_to_all | solution.py:53
  112.0 122.2 %all-to-all-start.2 = ((f32[16,129,512]{2,1,0:T(8,128)}), f32[16,129,512]{2,1,0:T(8,128)}, u32[]{:S(2)}, u32[]{:S(2)}) async-start(f32[16,129,512]{2,1,0:T(8,128)} %select_maximum_fusion), calls=%async_computation.2 | async-start | bytes 8912896 | tf_op jit(solution)/shard_map/all_to_all | solution.py:91
  116.6 117.2 %copy-start = (f32[2,256,256]{2,1,0:T(8,128)S(1)}, f32[2,256,256]{2,1,0:T(8,128)}, u32[]{:S(2)}) copy-start(f32[2,256,256]{2,1,0:T(8,128)} %param.15) | copy-start | bytes 1572868
  119.1 62.0 %collective-permute-start = (f32[256,256]{1,0:T(8,128)S(1)}, f32[256,256]{1,0:T(8,128)S(1)}, u32[]{:S(2)}, u32[]{:S(2)}) collective-permute-start(f32[256,256]{1,0:T(8,128)S(1)} %dynamic-slice_select_fusion), channel_id=1, source_target_pairs={{0,1},{1,0},{2,3},{3,2},{4,5},{5,4},{6,7},{7,6},{8,9},{9,8},{10,11... | collective-permute-start | bytes 786440 | tf_op jit(solution)/shard_map/ppermute | solution.py:28
  182.2 8.0 %collective-permute-start.1 = (f32[256,256]{1,0:T(8,128)S(1)}, f32[256,256]{1,0:T(8,128)S(1)}, u32[]{:S(2)}, u32[]{:S(2)}) collective-permute-start(f32[256,256]{1,0:T(8,128)S(1)} %fusion.39), channel_id=1, source_target_pairs={{0,2},{1,3},{2,0},{3,1},{4,6},{5,7},{6,4},{7,5},{8,10},{9,11},{10,... | collective-permute-start | bytes 786440 | tf_op jit(solution)/shard_map/ppermute | solution.py:28
  190.2 7.2 %collective-permute-start.2 = (f32[256,256]{1,0:T(8,128)S(1)}, f32[256,256]{1,0:T(8,128)S(1)}, u32[]{:S(2)}, u32[]{:S(2)}) collective-permute-start(f32[256,256]{1,0:T(8,128)S(1)} %add.116), channel_id=1, source_target_pairs={{0,4},{1,5},{2,6},{3,7},{4,0},{5,1},{6,2},{7,3},{8,12},{9,13},{10,... | collective-permute-start | bytes 786440 | tf_op jit(solution)/shard_map/ppermute | solution.py:28
  197.5 9.9 %collective-permute-start.3 = (f32[256,256]{1,0:T(8,128)S(1)}, f32[256,256]{1,0:T(8,128)S(1)}, u32[]{:S(2)}, u32[]{:S(2)}) collective-permute-start(f32[256,256]{1,0:T(8,128)S(1)} %add.117), channel_id=1, source_target_pairs={{0,8},{1,9},{2,10},{3,11},{4,12},{5,13},{6,14},{7,15},{8,0},{9,1},... | collective-permute-start | bytes 786440 | tf_op jit(solution)/shard_map/ppermute | solution.py:28
  207.4 1.6 collective-permute-start.4
  209.0 15.2 %collective-permute-start.5 = (f32[256,256]{1,0:T(8,128)S(1)}, f32[256,256]{1,0:T(8,128)S(1)}, u32[]{:S(2)}, u32[]{:S(2)}) collective-permute-start(f32[256,256]{1,0:T(8,128)S(1)} %add.119), channel_id=1, source_target_pairs={{0,32},{1,33},{2,34},{3,35},{4,36},{5,37},{6,38},{7,39},{8,40},{9,... | collective-permute-start | bytes 786440 | tf_op jit(solution)/shard_map/ppermute | solution.py:28
  224.3 9.5 %collective-permute-start.6 = (f32[256,256]{1,0:T(8,128)S(1)}, f32[256,256]{1,0:T(8,128)S(1)}, u32[]{:S(2)}, u32[]{:S(2)}) collective-permute-start(f32[256,256]{1,0:T(8,128)S(1)} %add.120), channel_id=1, source_target_pairs={{0,64},{1,65},{2,66},{3,67},{4,68},{5,69},{6,70},{7,71},{8,72},{9,... | collective-permute-start | bytes 786440 | tf_op jit(solution)/shard_map/ppermute | solution.py:28
  236.3 10.9 %collective-permute-start.7 = (f32[128,512]{1,0:T(8,128)S(1)}, f32[128,512]{1,0:T(8,128)S(1)}, u32[]{:S(2)}, u32[]{:S(2)}) collective-permute-start(f32[128,512]{1,0:T(8,128)S(1)} %pad_maximum_fusion.1), channel_id=1, source_target_pairs={{0,0},{1,16},{2,32},{3,48},{4,64},{5,80},{6,96},{7,112},{8,1},{9,1... | collective-permute-start | bytes 786440 | tf_op jit(solution)/shard_map/ppermute | solution.py:112
  239.5 74.2 %all-to-all-start.3 = ((f32[16,128,512]{2,1,0:T(8,128)}), f32[16,128,512]{2,1,0:T(8,128)}, u32[]{:S(2)}, u32[]{:S(2)}) async-start(f32[16,128,512]{2,1,0:T(8,128)} %broadcast_in_dim.40), calls=%async_computation.3 | async-start | bytes 8388608 | tf_op jit(solution)/shard_map/all_to_all | solution.py:21
  247.1 63.3 %all-gather.2.cloned.1.call-start = ((), (), s32[]{:S(2)}) async-start(), calls=%async_computation.4 | async-start | bytes 2359296 | tf_op jit(solution)/shard_map/all_gather | solution.py:113
  247.2 0.7 copy-start.1
Sparse Core Ops, SparseCore 0:
  249.6 60.7 all-gather.1

commit v4 on v3

--- a/solution.py
+++ b/solution.py
@@ -113,8 +113,8 @@
     left_cols = lax.all_gather(moved, "prow", axis=0, tiled=True)
 
     product = dot(left_rows, left_cols.T)
-    shaped = product.reshape(rows_local // 128, 128, blocks_local, 128) * mask_local[:, None, :, None]
-    return assembled - shaped.reshape(rows_local, cols_local)
+    mask_full = jnp.repeat(jnp.repeat(mask_local, 128, axis=0), 128, axis=1)
+    return assembled - product * mask_full
 
 
 def solution(mesh):

time: 365 us -> 343 us (0.940)
  other arithmetic: 46 us -> 29.8 us
  local copies, waits for them, and re-layouts: 52.5 us -> 45.1 us
  waiting for transfers between devices: 171 us -> 178 us
  starting transfers between devices: 51.8 us -> 46.9 us
    all_gather x1, waiting for transfers between devices: 62.4 us -> 0.01 us  [body(): left_cols = lax.all_gather(moved, 'prow', axis=0, tiled=True)]
    all_to_all x1, waiting for transfers between devices: 3.35 us -> 64.3 us  [gather_rows(): got = lax.all_to_all(spread, axis, 0, 0, tiled=False)]
    sub x1 -> x0, other arithmetic: 12.3 us -> none  [body(): return assembled - shaped.reshape(rows_local, cols_local)]
    mul x1 -> x0, local copies, waits for them, and re-layouts: 9.77 us -> none  [body(): product.reshape(rows_local // 128, 128, blocks_local, 128)]
    ppermute x7, starting transfers between devices: 20.3 us -> 10.8 us  [spread(): x = x + lax.ppermute(x, ('prow', 'pcol'), pairs)]
    ppermute x7, waiting for transfers between devices: 92.5 us -> 101 us  [spread(): x = x + lax.ppermute(x, ('prow', 'pcol'), pairs)]
    scatter-add x1, other arithmetic: 26 us -> 22 us  [assemble(): flat = front.reshape(rows_local * blocks_local, 128).at[got_place.astype(...]
  transfers between devices with their start and end apart: 13 -> 13, of which waited for: 11 -> 10; matrix products, arithmetic and copies ran while one was open for 6% -> 7% of each run, Pallas kernels for 0% -> 0%
where the time goes in v4:
time: 343 us; the launch traced here: 340 us
  waiting for transfers between devices  178 us (52%)
  starting transfers between devices  46.9 us (14%)
  local copies, waits for them, and re-layouts  45.1 us (13%)
  other arithmetic  29.8 us (9%)
  matrix products  20.5 us (6%)
  between operations  20 us (6%)
    ppermute x7, waiting for transfers between devices, spread(): x = x + lax.ppermute(x, ('prow', 'pcol'), pairs)  101 us
    all_to_all x1, waiting for transfers between devices, gather_rows(): got = lax.all_to_all(spread, axis, 0, 0, tiled=False)  64.3 us
    scatter-add x1, other arithmetic, assemble(): flat = front.reshape(rows_local * blocks_local, 128).at[got_place.astype(...  22 us
    dot_general x4, matrix products, dot(): return jnp.dot(a, b, precision=HIGHEST, preferred_element_type=jnp.float32)  20.1 us
    all_to_all x1, starting transfers between devices, assemble(): got_place = lax.all_to_all(send_place, ('prow', 'pcol'), 0, 0, tiled=True)  11.2 us
    ppermute x7, starting transfers between devices, spread(): x = x + lax.ppermute(x, ('prow', 'pcol'), pairs)  10.8 us
    all_to_all x1, waiting for transfers between devices, assemble(): got_values = lax.all_to_all(send_values, ('prow', 'pcol'), 0, 0, tiled=True)  10.5 us
    all_to_all x1, starting transfers between devices, gather_rows(): got = lax.all_to_all(spread, axis, 0, 0, tiled=False)  9.78 us
  transfers between devices with their start and end apart: 13, of which 10 were waited for; matrix products, arithmetic and copies ran while one was open for 7% of the time, Pallas kernels for 0%

profile of v4, /device:TPU:0, one launch (start us, length us, event | category | flops | bytes accessed | tf_op | source)
XLA Modules:
  0.0 339.9 jit_solution(3767326333530477528)
XLA Ops:
  6.5 0.7 fusion.24
  7.3 0.1 copy.15
  7.4 0.3 fusion.4
  7.8 0.1 broadcast_add_fusion
  7.8 0.0 copy-start.4
  7.9 0.3 copy.16
  8.2 0.6 fusion.3
  9.5 8.1 %scatter_custom_fusion = f32[3072]{0:T(1024)S(1)} fusion(s32[2048]{0:T(1024)S(1)} %compare_select_fusion.1, f32[2048]{0:T(1024)S(1)} %get-tuple-element.9, f32[]{:T(128)} %constant.125.clone.1), kind=kCustom, calls=%fused_computation.60 | custom fusion | bytes 12292 | tf_op jit(solution)/shard_map/scatter | solution.py:51
  17.6 0.7 all_to_all.20
  18.3 11.2 %all-to-all-start = ((f32[128,24,1]{1,2,0:T(1,128)}), f32[128,24,1]{1,2,0:T(1,128)S(1)}, u32[]{:S(2)}, u32[]{:S(2)}) async-start(f32[128,24,1]{1,2,0:T(1,128)} %bitcast.5), calls=%async_computation | async-start | bytes 131072 | tf_op jit(solution)/shard_map/all_to_all | solution.py:54
  29.5 7.2 %scatter_custom_fusion.1 = f32[3072,128]{1,0:T(8,128)} fusion(s32[2048]{0:T(1024)S(1)} %compare_select_fusion.1, f32[2048,128]{1,0:T(8,128)} %param.10, f32[]{:T(128)} %constant.125.clone.1), kind=kCustom, calls=%fused_computation.17 | custom fusion | bytes 1573376 | tf_op jit(solution)/shard_map/scatter | solution.py:48
  36.6 2.3 all-to-all-done
  38.9 7.5 %all-to-all-start.1 = ((f32[128,24,128]{2,1,0:T(8,128)}), f32[128,24,128]{2,1,0:T(8,128)S(1)}, u32[]{:S(2)}, u32[]{:S(2)}) async-start(f32[128,24,128]{2,1,0:T(8,128)} %bitcast.7), calls=%async_computation.1 | async-start | bytes 3145728 | tf_op jit(solution)/shard_map/all_to_all | solution.py:53
  46.4 0.6 fusion.31
  50.7 0.0 copy-start.3
  50.7 9.3 %reshape.64 = f32[16384,128]{1,0:T(8,128)} reshape(f32[2048,1024]{1,0:T(8,128)} %param.8) | data formatting | bytes 16777216 | tf_op jit(solution)/shard_map/reshape | solution.py:56
  59.9 0.0 copy-done.3
  59.9 0.1 copy.18
  60.0 0.2 convert_reduce_fusion
  60.2 0.1 convert_element_type.32
  60.4 10.5 %all-to-all-done.1 = f32[128,24,128]{2,1,0:T(8,128)S(1)} async-done(((f32[128,24,128]{2,1,0:T(8,128)}), f32[128,24,128]{2,1,0:T(8,128)S(1)}, u32[]{:S(2)}, u32[]{:S(2)}) %all-to-all-start.1) | async-done | bytes 1572896 | tf_op jit(solution)/shard_map/all_to_all | solution.py:53
  70.9 22.0 %scatter_fusion = f32[16384,128]{1,0:T(8,128)} fusion(f32[16384,128]{1,0:T(8,128)} %reshape.64, s32[3072]{0:T(1024)S(1)} %bitcast.52, f32[3072,128]{1,0:T(8,128)S(1)} %bitcast.48), kind=kCustom, calls=%fused_computation.2 | custom fusion | flops 393216 | bytes 4730880 | tf_op jit(solution)/shard_map/scatter-add | solution.py:58
  92.9 9.3 %reshape.66 = f32[2048,1024]{1,0:T(8,128)} reshape(f32[16384,128]{1,0:T(8,128)} %scatter_fusion) | data formatting | bytes 16777216 | tf_op jit(solution)/shard_map/reshape | solution.py:60
  102.1 2.5 constant_dynamic-slice_fusion.2
  104.7 0.6 pad_maximum_fusion
  105.3 0.1 broadcast_in_dim.42
  105.4 2.6 select_maximum_fusion
  108.0 6.9 %all-to-all-start.2 = ((f32[16,129,512]{2,1,0:T(8,128)}), f32[16,129,512]{2,1,0:T(8,128)}, u32[]{:S(2)}, u32[]{:S(2)}) async-start(f32[16,129,512]{2,1,0:T(8,128)} %select_maximum_fusion), calls=%async_computation.2 | async-start | bytes 8912896 | tf_op jit(solution)/shard_map/all_to_all | solution.py:91
  115.0 0.0 copy-start.1
  116.3 1.1 dynamic-slice_select_fusion
  117.4 2.0 collective-permute-start
  119.4 66.7 %collective-permute-done = f32[256,256]{1,0:T(8,128)S(1)} collective-permute-done((f32[256,256]{1,0:T(8,128)S(1)}, f32[256,256]{1,0:T(8,128)S(1)}, u32[]{:S(2)}, u32[]{:S(2)}) %collective-permute-start) | collective-permute-done | bytes 262176 | tf_op jit(solution)/shard_map/ppermute | solution.py:28
  186.1 1.1 fusion.37
  187.3 0.3 collective-permute-start.1
  187.6 8.4 %collective-permute-done.1 = f32[256,256]{1,0:T(8,128)S(1)} collective-permute-done((f32[256,256]{1,0:T(8,128)S(1)}, f32[256,256]{1,0:T(8,128)S(1)}, u32[]{:S(2)}, u32[]{:S(2)}) %collective-permute-start.1) | collective-permute-done | bytes 262176 | tf_op jit(solution)/shard_map/ppermute | solution.py:28
  196.0 0.6 collective-permute-start.2
  196.6 5.9 %collective-permute-done.2 = f32[256,256]{1,0:T(8,128)S(1)} collective-permute-done((f32[256,256]{1,0:T(8,128)S(1)}, f32[256,256]{1,0:T(8,128)S(1)}, u32[]{:S(2)}, u32[]{:S(2)}) %collective-permute-start.2) | collective-permute-done | bytes 262176 | tf_op jit(solution)/shard_map/ppermute | solution.py:28
  202.5 4.0 %collective-permute-start.3 = (f32[256,256]{1,0:T(8,128)S(1)}, f32[256,256]{1,0:T(8,128)S(1)}, u32[]{:S(2)}, u32[]{:S(2)}) collective-permute-start(f32[256,256]{1,0:T(8,128)S(1)} %add.117), channel_id=1, source_target_pairs={{0,8},{1,9},{2,10},{3,11},{4,12},{5,13},{6,14},{7,15},{8,0},{9,1},... | collective-permute-start | bytes 786440 | tf_op jit(solution)/shard_map/ppermute | solution.py:28
  206.5 4.4 %collective-permute-done.3 = f32[256,256]{1,0:T(8,128)S(1)} collective-permute-done((f32[256,256]{1,0:T(8,128)S(1)}, f32[256,256]{1,0:T(8,128)S(1)}, u32[]{:S(2)}, u32[]{:S(2)}) %collective-permute-start.3) | collective-permute-done | bytes 262176 | tf_op jit(solution)/shard_map/ppermute | solution.py:28
  210.9 0.1 collective-permute-start.4
  211.0 1.5 collective-permute-done.4
  212.6 0.3 collective-permute-start.5
  212.9 8.3 %collective-permute-done.5 = f32[256,256]{1,0:T(8,128)S(1)} collective-permute-done((f32[256,256]{1,0:T(8,128)S(1)}, f32[256,256]{1,0:T(8,128)S(1)}, u32[]{:S(2)}, u32[]{:S(2)}) %collective-permute-start.5) | collective-permute-done | bytes 262176 | tf_op jit(solution)/shard_map/ppermute | solution.py:28
  221.2 3.5 %collective-permute-start.6 = (f32[256,256]{1,0:T(8,128)S(1)}, f32[256,256]{1,0:T(8,128)S(1)}, u32[]{:S(2)}, u32[]{:S(2)}) collective-permute-start(f32[256,256]{1,0:T(8,128)S(1)} %add.120), channel_id=1, source_target_pairs={{0,64},{1,65},{2,66},{3,67},{4,68},{5,69},{6,70},{7,71},{8,72},{9,... | collective-permute-start | bytes 786440 | tf_op jit(solution)/shard_map/ppermute | solution.py:28
  225.4 5.4 %collective-permute-done.6 = f32[256,256]{1,0:T(8,128)S(1)} collective-permute-done((f32[256,256]{1,0:T(8,128)S(1)}, f32[256,256]{1,0:T(8,128)S(1)}, u32[]{:S(2)}, u32[]{:S(2)}) %collective-permute-start.6) | collective-permute-done | bytes 262176 | tf_op jit(solution)/shard_map/ppermute | solution.py:28
  230.8 0.4 fusion.11
  231.2 0.0 all-to-all-done.2
  231.2 1.1 dynamic-slice_bitcast_fusion
  232.3 0.3 fusion.13
  232.6 0.4 fusion.1
  233.0 0.3 fusion.9
  233.3 0.7 collective-permute-start.7
  234.0 2.5 broadcast_in_dim.45
  236.5 9.8 %all-to-all-start.3 = ((f32[16,128,512]{2,1,0:T(8,128)}), f32[16,128,512]{2,1,0:T(8,128)}, u32[]{:S(2)}, u32[]{:S(2)}) async-start(f32[16,128,512]{2,1,0:T(8,128)} %broadcast_in_dim.45), calls=%async_computation.3 | async-start | bytes 8388608 | tf_op jit(solution)/shard_map/all_to_all | solution.py:21
  246.3 0.0 all-gather.2.cloned.1.call-start
  246.4 0.0 collective-permute-done.7
  246.4 0.0 copy-start.2
  246.4 0.7 copy-done.2
  247.1 0.0 all-gather.2.cloned.1.call-update
  247.1 0.1 copy.19
  247.2 64.3 %all-to-all-done.3 = f32[16,128,512]{2,1,0:T(8,128)} async-done(((f32[16,128,512]{2,1,0:T(8,128)}), f32[16,128,512]{2,1,0:T(8,128)}, u32[]{:S(2)}, u32[]{:S(2)}) %all-to-all-start.3) | async-done | bytes 4194336 | tf_op jit(solution)/shard_map/all_to_all | solution.py:21
  311.5 0.1 broadcast_in_dim.46
  311.6 2.3 broadcast_in_dim.47
  314.0 19.1 %fusion = f32[2048,1024]{1,0:T(8,128)} fusion(f32[2048,1024]{1,0:T(8,128)} %reshape.66, f32[256,8,8,128]{3,2,1,0:T(8,128)S(1)} %bitcast.46, f32[2048,512]{1,0:T(8,128)} %bitcast.18, f32[1024,512]{1,0:T(8,128)S(1)} %copy-done), kind=kOutput, calls=%fused_computation.4 | convolution fusion | flops 12889096192 | bytes 31457280 | tf_op jit(solution)/shard_map/dot_general | solution.py:11
  (19 shorter events, 0.3 us)
Async XLA Ops:
  7.8 38.6 %copy-start.4 = (s32[2]{0:T(128)S(1)}, s32[2]{0:T(128)}, u32[]{:S(2)}) copy-start(s32[2]{0:T(128)} %param.14) | copy-start | bytes 28
  18.3 20.6 %all-to-all-start = ((f32[128,24,1]{1,2,0:T(1,128)}), f32[128,24,1]{1,2,0:T(1,128)S(1)}, u32[]{:S(2)}, u32[]{:S(2)}) async-start(f32[128,24,1]{1,2,0:T(1,128)} %bitcast.5), calls=%async_computation | async-start | bytes 131072 | tf_op jit(solution)/shard_map/all_to_all | solution.py:54
  38.9 32.0 %all-to-all-start.1 = ((f32[128,24,128]{2,1,0:T(8,128)}), f32[128,24,128]{2,1,0:T(8,128)S(1)}, u32[]{:S(2)}, u32[]{:S(2)}) async-start(f32[128,24,128]{2,1,0:T(8,128)} %bitcast.7), calls=%async_computation.1 | async-start | bytes 3145728 | tf_op jit(solution)/shard_map/all_to_all | solution.py:53
  50.7 9.3 %copy-start.3 = (s32[16,8]{0,1:T(8,128)S(1)}, s32[16,8]{0,1:T(8,128)}, u32[]{:S(2)}) copy-start(s32[16,8]{0,1:T(8,128)} %param.9) | copy-start | bytes 1540
  108.0 123.2 %all-to-all-start.2 = ((f32[16,129,512]{2,1,0:T(8,128)}), f32[16,129,512]{2,1,0:T(8,128)}, u32[]{:S(2)}, u32[]{:S(2)}) async-start(f32[16,129,512]{2,1,0:T(8,128)} %select_maximum_fusion), calls=%async_computation.2 | async-start | bytes 8912896 | tf_op jit(solution)/shard_map/all_to_all | solution.py:91
  115.0 115.8 %copy-start.1 = (f32[2,256,256]{2,1,0:T(8,128)S(1)}, f32[2,256,256]{2,1,0:T(8,128)}, u32[]{:S(2)}) copy-start(f32[2,256,256]{2,1,0:T(8,128)} %param.15) | copy-start | bytes 1572868
  117.4 68.7 %collective-permute-start = (f32[256,256]{1,0:T(8,128)S(1)}, f32[256,256]{1,0:T(8,128)S(1)}, u32[]{:S(2)}, u32[]{:S(2)}) collective-permute-start(f32[256,256]{1,0:T(8,128)S(1)} %dynamic-slice_select_fusion), channel_id=1, source_target_pairs={{0,1},{1,0},{2,3},{3,2},{4,5},{5,4},{6,7},{7,6},{8,9},{9,8},{10,11... | collective-permute-start | bytes 786440 | tf_op jit(solution)/shard_map/ppermute | solution.py:28
  187.3 8.7 %collective-permute-start.1 = (f32[256,256]{1,0:T(8,128)S(1)}, f32[256,256]{1,0:T(8,128)S(1)}, u32[]{:S(2)}, u32[]{:S(2)}) collective-permute-start(f32[256,256]{1,0:T(8,128)S(1)} %fusion.37), channel_id=1, source_target_pairs={{0,2},{1,3},{2,0},{3,1},{4,6},{5,7},{6,4},{7,5},{8,10},{9,11},{10,... | collective-permute-start | bytes 786440 | tf_op jit(solution)/shard_map/ppermute | solution.py:28
  196.0 6.5 %collective-permute-start.2 = (f32[256,256]{1,0:T(8,128)S(1)}, f32[256,256]{1,0:T(8,128)S(1)}, u32[]{:S(2)}, u32[]{:S(2)}) collective-permute-start(f32[256,256]{1,0:T(8,128)S(1)} %add.116), channel_id=1, source_target_pairs={{0,4},{1,5},{2,6},{3,7},{4,0},{5,1},{6,2},{7,3},{8,12},{9,13},{10,... | collective-permute-start | bytes 786440 | tf_op jit(solution)/shard_map/ppermute | solution.py:28
  202.5 8.4 %collective-permute-start.3 = (f32[256,256]{1,0:T(8,128)S(1)}, f32[256,256]{1,0:T(8,128)S(1)}, u32[]{:S(2)}, u32[]{:S(2)}) collective-permute-start(f32[256,256]{1,0:T(8,128)S(1)} %add.117), channel_id=1, source_target_pairs={{0,8},{1,9},{2,10},{3,11},{4,12},{5,13},{6,14},{7,15},{8,0},{9,1},... | collective-permute-start | bytes 786440 | tf_op jit(solution)/shard_map/ppermute | solution.py:28
  210.9 1.6 collective-permute-start.4
  212.6 8.6 %collective-permute-start.5 = (f32[256,256]{1,0:T(8,128)S(1)}, f32[256,256]{1,0:T(8,128)S(1)}, u32[]{:S(2)}, u32[]{:S(2)}) collective-permute-start(f32[256,256]{1,0:T(8,128)S(1)} %add.119), channel_id=1, source_target_pairs={{0,32},{1,33},{2,34},{3,35},{4,36},{5,37},{6,38},{7,39},{8,40},{9,... | collective-permute-start | bytes 786440 | tf_op jit(solution)/shard_map/ppermute | solution.py:28
  221.2 9.6 %collective-permute-start.6 = (f32[256,256]{1,0:T(8,128)S(1)}, f32[256,256]{1,0:T(8,128)S(1)}, u32[]{:S(2)}, u32[]{:S(2)}) collective-permute-start(f32[256,256]{1,0:T(8,128)S(1)} %add.120), channel_id=1, source_target_pairs={{0,64},{1,65},{2,66},{3,67},{4,68},{5,69},{6,70},{7,71},{8,72},{9,... | collective-permute-start | bytes 786440 | tf_op jit(solution)/shard_map/ppermute | solution.py:28
  233.3 13.1 %collective-permute-start.7 = (f32[128,512]{1,0:T(8,128)S(1)}, f32[128,512]{1,0:T(8,128)S(1)}, u32[]{:S(2)}, u32[]{:S(2)}) collective-permute-start(f32[128,512]{1,0:T(8,128)S(1)} %pad_maximum_fusion.1), channel_id=1, source_target_pairs={{0,0},{1,16},{2,32},{3,48},{4,64},{5,80},{6,96},{7,112},{8,1},{9,1... | collective-permute-start | bytes 786440 | tf_op jit(solution)/shard_map/ppermute | solution.py:112
  236.5 75.0 %all-to-all-start.3 = ((f32[16,128,512]{2,1,0:T(8,128)}), f32[16,128,512]{2,1,0:T(8,128)}, u32[]{:S(2)}, u32[]{:S(2)}) async-start(f32[16,128,512]{2,1,0:T(8,128)} %broadcast_in_dim.45), calls=%async_computation.3 | async-start | bytes 8388608 | tf_op jit(solution)/shard_map/all_to_all | solution.py:21
  246.3 65.2 %all-gather.2.cloned.1.call-start = ((), (), s32[]{:S(2)}) async-start(), calls=%async_computation.4 | async-start | bytes 2359296 | tf_op jit(solution)/shard_map/all_gather | solution.py:113
  246.4 0.7 copy-start.2
  311.6 2.3 copy-start
Sparse Core Ops, SparseCore 0:
  248.8 59.6 all-gather.1

commit v5 on v4

--- a/solution.py
+++ b/solution.py
@@ -80,7 +80,7 @@
     src_row = start2 // rows_local
     x_local = lax.dynamic_slice_in_dim(cols[0], start2 % rows_local, pw, 0)
     x_mine = jnp.where((r == src_row) & (c == owner[0]), x_local, 0.0)
-    x_cols = spread(x_mine, n_prow * n_pcol)
+    x_cols = lax.psum(lax.psum(x_mine, "pcol"), "prow")
 
     mask_local = fill_blocks.astype(jnp.float32)
     mask_two = lax.dynamic_slice_in_dim(mask_local, offset[1] // 128, pw // 128, 1)
@@ -112,7 +112,9 @@
     moved = lax.ppermute(piece, ("prow", "pcol"), perm)
     left_cols = lax.all_gather(moved, "prow", axis=0, tiled=True)
 
-    product = dot(left_rows, left_cols.T)
+    product = jnp.dot(
+        left_rows, left_cols.T, precision=lax.Precision.HIGH, preferred_element_type=jnp.float32
+    )
     mask_full = jnp.repeat(jnp.repeat(mask_local, 128, axis=0), 128, axis=1)
     return assembled - product * mask_full
 

time: 343 us -> 410 us (1.20)
  waiting for transfers between devices: 178 us -> 261 us
  starting transfers between devices: 46.9 us -> 36.4 us
    psum x0 -> x2, waiting for transfers between devices: none -> 183 us  [body(): x_cols = lax.psum(lax.psum(x_mine, 'pcol'), 'prow')]
    ppermute x7 -> x0, waiting for transfers between devices: 101 us -> none  [spread(): x = x + lax.ppermute(x, ('prow', 'pcol'), pairs)]
    dot_general x4 -> x3, matrix products: 20.1 us -> 1.89 us  [dot(): return jnp.dot(a, b, precision=HIGHEST, preferred_element_type=jnp.float32)]
    dot_general x0 -> x1, matrix products: none -> 14.6 us  [body(): jnp.dot(left_rows, left_cols.T, precision=lax.Precision.HIGH, preferred_e...]
    ppermute x7 -> x0, starting transfers between devices: 10.8 us -> none  [spread(): x = x + lax.ppermute(x, ('prow', 'pcol'), pairs)]
  transfers between devices with their start and end apart: 13 -> 8, of which waited for: 10 -> 6; matrix products, arithmetic and copies ran while one was open for 7% -> 6% of each run, Pallas kernels for 0% -> 0%
where the time goes in v5:
time: 410 us; the launch traced here: 409 us
  waiting for transfers between devices  261 us (64%)
  local copies, waits for them, and re-layouts  45.2 us (11%)
  starting transfers between devices  36.4 us (9%)
  other arithmetic  29.4 us (7%)
  between operations  19.8 us (5%)
  matrix products  16.9 us (4%)
    psum x2, waiting for transfers between devices, body(): x_cols = lax.psum(lax.psum(x_mine, 'pcol'), 'prow')  183 us
    all_to_all x1, waiting for transfers between devices, gather_rows(): got = lax.all_to_all(spread, axis, 0, 0, tiled=False)  62.7 us
    scatter-add x1, other arithmetic, assemble(): flat = front.reshape(rows_local * blocks_local, 128).at[got_place.astype(...  22.3 us
    dot_general x1, matrix products, body(): jnp.dot(left_rows, left_cols.T, precision=lax.Precision.HIGH, preferred_e...  14.6 us
    all_to_all x1, starting transfers between devices, assemble(): got_place = lax.all_to_all(send_place, ('prow', 'pcol'), 0, 0, tiled=True)  11.2 us
    all_to_all x1, waiting for transfers between devices, assemble(): got_values = lax.all_to_all(send_values, ('prow', 'pcol'), 0, 0, tiled=True)  10.3 us
    reshape x1, local copies, waits for them, and re-layouts, assemble(): return flat.reshape(rows_local, cols_local)  9.28 us
    reshape x1, local copies, waits for them, and re-layouts, assemble(): front.reshape(rows_local * blocks_local, 128)  9.25 us
  transfers between devices with their start and end apart: 8, of which 6 were waited for; matrix products, arithmetic and copies ran while one was open for 6% of the time, Pallas kernels for 0%

profile of v5, /device:TPU:0, one launch (start us, length us, event | category | flops | bytes accessed | tf_op | source)
XLA Modules:
  0.0 408.6 jit_solution(14854385177909925650)
XLA Ops:
  6.5 0.7 fusion.23
  7.3 0.1 copy.15
  7.4 0.3 fusion.4
  7.8 0.1 broadcast_add_fusion
  7.8 0.0 copy-start.4
  7.9 0.3 copy.16
  8.2 0.6 fusion.3
  9.5 8.1 %scatter_custom_fusion = f32[3072]{0:T(1024)S(1)} fusion(s32[2048]{0:T(1024)S(1)} %compare_select_fusion.1, f32[2048]{0:T(1024)S(1)} %get-tuple-element.9, f32[]{:T(128)} %constant.125.clone.1), kind=kCustom, calls=%fused_computation.59 | custom fusion | bytes 12292 | tf_op jit(solution)/shard_map/scatter | solution.py:51
  17.6 0.7 all_to_all.20
  18.3 11.2 %all-to-all-start = ((f32[128,24,1]{1,2,0:T(1,128)}), f32[128,24,1]{1,2,0:T(1,128)S(1)}, u32[]{:S(2)}, u32[]{:S(2)}) async-start(f32[128,24,1]{1,2,0:T(1,128)} %bitcast.5), calls=%async_computation | async-start | bytes 131072 | tf_op jit(solution)/shard_map/all_to_all | solution.py:54
  29.5 7.2 %scatter_custom_fusion.1 = f32[3072,128]{1,0:T(8,128)} fusion(s32[2048]{0:T(1024)S(1)} %compare_select_fusion.1, f32[2048,128]{1,0:T(8,128)} %param.10, f32[]{:T(128)} %constant.125.clone.1), kind=kCustom, calls=%fused_computation.17 | custom fusion | bytes 1573376 | tf_op jit(solution)/shard_map/scatter | solution.py:48
  36.7 2.2 all-to-all-done
  38.9 7.5 %all-to-all-start.1 = ((f32[128,24,128]{2,1,0:T(8,128)}), f32[128,24,128]{2,1,0:T(8,128)S(1)}, u32[]{:S(2)}, u32[]{:S(2)}) async-start(f32[128,24,128]{2,1,0:T(8,128)} %bitcast.7), calls=%async_computation.1 | async-start | bytes 3145728 | tf_op jit(solution)/shard_map/all_to_all | solution.py:53
  46.4 0.0 copy-done.4
  46.4 0.6 fusion.30
  50.9 0.0 copy-start.3
  50.9 9.3 %reshape.64 = f32[16384,128]{1,0:T(8,128)} reshape(f32[2048,1024]{1,0:T(8,128)} %param.8) | data formatting | bytes 16777216 | tf_op jit(solution)/shard_map/reshape | solution.py:56
  60.1 0.0 copy-done.3
  60.2 0.1 copy.18
  60.2 0.2 convert_reduce_fusion
  60.4 0.1 convert_element_type.32
  60.6 10.3 %all-to-all-done.1 = f32[128,24,128]{2,1,0:T(8,128)S(1)} async-done(((f32[128,24,128]{2,1,0:T(8,128)}), f32[128,24,128]{2,1,0:T(8,128)S(1)}, u32[]{:S(2)}, u32[]{:S(2)}) %all-to-all-start.1) | async-done | bytes 1572896 | tf_op jit(solution)/shard_map/all_to_all | solution.py:53
  70.9 22.3 %scatter_fusion = f32[16384,128]{1,0:T(8,128)} fusion(f32[16384,128]{1,0:T(8,128)} %reshape.64, s32[3072]{0:T(1024)S(1)} %bitcast.53, f32[3072,128]{1,0:T(8,128)S(1)} %bitcast.49), kind=kCustom, calls=%fused_computation.2 | custom fusion | flops 393216 | bytes 4730880 | tf_op jit(solution)/shard_map/scatter-add | solution.py:58
  93.2 9.3 %reshape.66 = f32[2048,1024]{1,0:T(8,128)} reshape(f32[16384,128]{1,0:T(8,128)} %scatter_fusion) | data formatting | bytes 16777216 | tf_op jit(solution)/shard_map/reshape | solution.py:60
  102.4 2.5 constant_dynamic-slice_fusion.2
  105.0 0.6 pad_maximum_fusion
  105.6 0.1 broadcast_in_dim.42
  105.7 2.6 select_maximum_fusion
  108.3 0.0 copy-start.1
  108.3 7.6 %all-to-all-start.2 = ((f32[16,129,512]{2,1,0:T(8,128)}), f32[16,129,512]{2,1,0:T(8,128)}, u32[]{:S(2)}, u32[]{:S(2)}) async-start(f32[16,129,512]{2,1,0:T(8,128)} %select_maximum_fusion), calls=%async_computation.2 | async-start | bytes 8912896 | tf_op jit(solution)/shard_map/all_to_all | solution.py:91
  116.0 0.0 all-reduce.4.cloned.1.call-start
  117.3 1.9 dynamic-slice_select_fusion
  119.2 0.0 all-reduce.4.cloned.1.call-update
  119.2 0.0 all-reduce.6.cloned.1.call-start
  119.3 121.6 %all-reduce.4.cloned.1.call-done = f32[256,256]{1,0:T(8,128)} async-done(((f32[256,256]{1,0:T(8,128)}), f32[256,256]{1,0:T(8,128)}) %all-reduce.4.cloned.1.call-update) | async-done | bytes 262160 | tf_op jit(solution)/shard_map/psum | solution.py:83
  240.9 0.0 all-reduce.6.cloned.1.call-update
  241.6 61.2 %all-reduce.6.cloned.1.call-done = f32[256,256]{1,0:T(8,128)} async-done(((f32[256,256]{1,0:T(8,128)}), f32[256,256]{1,0:T(8,128)}) %all-reduce.6.cloned.1.call-update) | async-done | bytes 262160 | tf_op jit(solution)/shard_map/psum | solution.py:83
  302.8 0.0 copy-done.1
  302.8 1.3 fusion.11
  304.1 0.0 all-to-all-done.2
  304.1 1.1 dynamic-slice_bitcast_fusion
  305.2 0.3 fusion.13
  305.5 0.4 fusion.1
  305.9 0.3 fusion.9
  306.2 0.7 collective-permute-start
  306.9 2.5 broadcast_in_dim.45
  309.5 9.1 %all-to-all-start.3 = ((f32[16,128,512]{2,1,0:T(8,128)}), f32[16,128,512]{2,1,0:T(8,128)}, u32[]{:S(2)}, u32[]{:S(2)}) async-start(f32[16,128,512]{2,1,0:T(8,128)} %broadcast_in_dim.45), calls=%async_computation.3 | async-start | bytes 8388608 | tf_op jit(solution)/shard_map/all_to_all | solution.py:21
  318.6 0.2 all-gather.2.cloned.1.call-start
  318.8 0.0 collective-permute-done
  318.8 0.0 copy-start.2
  318.9 0.7 copy-done.2
  319.6 0.0 all-gather.2.cloned.1.call-update
  319.6 0.1 copy.19
  319.7 62.7 %all-to-all-done.3 = f32[16,128,512]{2,1,0:T(8,128)} async-done(((f32[16,128,512]{2,1,0:T(8,128)}), f32[16,128,512]{2,1,0:T(8,128)}, u32[]{:S(2)}, u32[]{:S(2)}) %all-to-all-start.3) | async-done | bytes 4194336 | tf_op jit(solution)/shard_map/all_to_all | solution.py:21
  382.3 2.7 all-gather.2.cloned.1.call-done
  385.0 0.1 broadcast_in_dim.46
  385.1 0.0 copy-start
  385.1 2.3 broadcast_in_dim.47
  387.4 0.0 copy-done
  387.4 14.6 %fusion = f32[2048,1024]{1,0:T(8,128)} fusion(f32[2048,1024]{1,0:T(8,128)} %reshape.66, f32[256,8,8,128]{3,2,1,0:T(8,128)S(1)} %bitcast.47, f32[2048,512]{1,0:T(8,128)} %bitcast.18, f32[1024,512]{1,0:T(8,128)S(1)} %copy-done), kind=kOutput, calls=%fused_computation.4 | convolution fusion | flops 6446645248 | bytes 31457280 | tf_op jit(solution)/shard_map/dot_general | solution.py:115
  (9 shorter events, 0.1 us)
Async XLA Ops:
  7.8 38.6 %copy-start.4 = (s32[2]{0:T(128)S(1)}, s32[2]{0:T(128)}, u32[]{:S(2)}) copy-start(s32[2]{0:T(128)} %param.14) | copy-start | bytes 28
  18.3 20.6 %all-to-all-start = ((f32[128,24,1]{1,2,0:T(1,128)}), f32[128,24,1]{1,2,0:T(1,128)S(1)}, u32[]{:S(2)}, u32[]{:S(2)}) async-start(f32[128,24,1]{1,2,0:T(1,128)} %bitcast.5), calls=%async_computation | async-start | bytes 131072 | tf_op jit(solution)/shard_map/all_to_all | solution.py:54
  38.9 32.0 %all-to-all-start.1 = ((f32[128,24,128]{2,1,0:T(8,128)}), f32[128,24,128]{2,1,0:T(8,128)S(1)}, u32[]{:S(2)}, u32[]{:S(2)}) async-start(f32[128,24,128]{2,1,0:T(8,128)} %bitcast.7), calls=%async_computation.1 | async-start | bytes 3145728 | tf_op jit(solution)/shard_map/all_to_all | solution.py:53
  50.9 9.3 %copy-start.3 = (s32[16,8]{0,1:T(8,128)S(1)}, s32[16,8]{0,1:T(8,128)}, u32[]{:S(2)}) copy-start(s32[16,8]{0,1:T(8,128)} %param.9) | copy-start | bytes 1540
  108.3 194.5 %copy-start.1 = (f32[2,256,256]{2,1,0:T(8,128)S(1)}, f32[2,256,256]{2,1,0:T(8,128)}, u32[]{:S(2)}) copy-start(f32[2,256,256]{2,1,0:T(8,128)} %param.15) | copy-start | bytes 1572868
  108.3 195.8 %all-to-all-start.2 = ((f32[16,129,512]{2,1,0:T(8,128)}), f32[16,129,512]{2,1,0:T(8,128)}, u32[]{:S(2)}, u32[]{:S(2)}) async-start(f32[16,129,512]{2,1,0:T(8,128)} %select_maximum_fusion), calls=%async_computation.2 | async-start | bytes 8912896 | tf_op jit(solution)/shard_map/all_to_all | solution.py:91
  116.0 124.9 %all-reduce.4.cloned.1.call-start = ((), (), s32[]{:S(2)}) async-start(), calls=%async_computation.4 | async-start | bytes 524288 | tf_op jit(solution)/shard_map/psum | solution.py:83
  119.2 183.6 %all-reduce.6.cloned.1.call-start = ((), (), s32[]{:S(2)}) async-start(), calls=%async_computation.5 | async-start | bytes 524288 | tf_op jit(solution)/shard_map/psum | solution.py:83
  306.2 12.6 %collective-permute-start = (f32[128,512]{1,0:T(8,128)S(1)}, f32[128,512]{1,0:T(8,128)S(1)}, u32[]{:S(2)}, u32[]{:S(2)}) collective-permute-start(f32[128,512]{1,0:T(8,128)S(1)} %pad_maximum_fusion.1), channel_id=1, source_target_pairs={{0,0},{1,16},{2,32},{3,48},{4,64},{5,80},{6,96},{7,112},{8,1},{9,1... | collective-permute-start | bytes 786440 | tf_op jit(solution)/shard_map/ppermute | solution.py:112
  309.5 72.9 %all-to-all-start.3 = ((f32[16,128,512]{2,1,0:T(8,128)}), f32[16,128,512]{2,1,0:T(8,128)}, u32[]{:S(2)}, u32[]{:S(2)}) async-start(f32[16,128,512]{2,1,0:T(8,128)} %broadcast_in_dim.45), calls=%async_computation.3 | async-start | bytes 8388608 | tf_op jit(solution)/shard_map/all_to_all | solution.py:21
  318.6 66.4 %all-gather.2.cloned.1.call-start = ((), (), s32[]{:S(2)}) async-start(), calls=%async_computation.6 | async-start | bytes 2359296 | tf_op jit(solution)/shard_map/all_gather | solution.py:113
  318.8 0.7 copy-start.2
  385.1 2.3 copy-start
Sparse Core Ops, SparseCore 0:
  119.9 120.9 all-reduce.3
  243.2 59.5 all-reduce.5
  321.1 63.8 all-gather.1

commit v6 on v5

--- a/solution.py
+++ b/solution.py
@@ -80,7 +80,7 @@
     src_row = start2 // rows_local
     x_local = lax.dynamic_slice_in_dim(cols[0], start2 % rows_local, pw, 0)
     x_mine = jnp.where((r == src_row) & (c == owner[0]), x_local, 0.0)
-    x_cols = lax.psum(lax.psum(x_mine, "pcol"), "prow")
+    x_cols = spread(x_mine, n_prow * n_pcol)
 
     mask_local = fill_blocks.astype(jnp.float32)
     mask_two = lax.dynamic_slice_in_dim(mask_local, offset[1] // 128, pw // 128, 1)

time: 410 us -> 337 us (0.82)
  waiting for transfers between devices: 261 us -> 180 us
  starting transfers between devices: 36.4 us -> 41.8 us
    psum x2 -> x0, waiting for transfers between devices: 183 us -> none  [body(): x_cols = lax.psum(lax.psum(x_mine, 'pcol'), 'prow')]
    ppermute x0 -> x7, waiting for transfers between devices: none -> 102 us  [spread(): x = x + lax.ppermute(x, ('prow', 'pcol'), pairs)]
    ppermute x0 -> x7, starting transfers between devices: none -> 7.79 us  [spread(): x = x + lax.ppermute(x, ('prow', 'pcol'), pairs)]
  transfers between devices with their start and end apart: 8 -> 13, of which waited for: 6 -> 10; matrix products, arithmetic and copies ran while one was open for 6% -> 7% of each run, Pallas kernels for 0% -> 0%
where the time goes in v6:
time: 337 us; the launch traced here: 332 us
  waiting for transfers between devices  180 us (53%)
  local copies, waits for them, and re-layouts  45.1 us (13%)
  starting transfers between devices  41.8 us (12%)
  other arithmetic  29.8 us (9%)
  between operations  20 us (6%)
  matrix products  15.9 us (5%)
    ppermute x7, waiting for transfers between devices, spread(): x = x + lax.ppermute(x, ('prow', 'pcol'), pairs)  102 us
    all_to_all x1, waiting for transfers between devices, gather_rows(): got = lax.all_to_all(spread, axis, 0, 0, tiled=False)  64.8 us
    scatter-add x1, other arithmetic, assemble(): flat = front.reshape(rows_local * blocks_local, 128).at[got_place.astype(...  22 us
    dot_general x1, matrix products, body(): jnp.dot(left_rows, left_cols.T, precision=lax.Precision.HIGH, preferred_e...  14.6 us
    all_to_all x1, starting transfers between devices, assemble(): got_place = lax.all_to_all(send_place, ('prow', 'pcol'), 0, 0, tiled=True)  11.2 us
    all_to_all x1, waiting for transfers between devices, assemble(): got_values = lax.all_to_all(send_values, ('prow', 'pcol'), 0, 0, tiled=True)  10.5 us
    reshape x1, local copies, waits for them, and re-layouts, assemble(): return flat.reshape(rows_local, cols_local)  9.28 us
    reshape x1, local copies, waits for them, and re-layouts, assemble(): front.reshape(rows_local * blocks_local, 128)  9.25 us
  transfers between devices with their start and end apart: 13, of which 10 were waited for; matrix products, arithmetic and copies ran while one was open for 7% of the time, Pallas kernels for 0%

profile of v6, /device:TPU:0, one launch (start us, length us, event | category | flops | bytes accessed | tf_op | source)
XLA Modules:
  0.0 332.2 jit_solution(14828031351405054927)
XLA Ops:
  6.5 0.7 fusion.24
  7.3 0.1 copy.15
  7.4 0.3 fusion.4
  7.8 0.1 broadcast_add_fusion
  7.8 0.0 copy-start.4
  7.9 0.3 copy.16
  8.2 0.6 fusion.3
  9.5 8.1 %scatter_custom_fusion = f32[3072]{0:T(1024)S(1)} fusion(s32[2048]{0:T(1024)S(1)} %compare_select_fusion.1, f32[2048]{0:T(1024)S(1)} %get-tuple-element.9, f32[]{:T(128)} %constant.125.clone.1), kind=kCustom, calls=%fused_computation.60 | custom fusion | bytes 12292 | tf_op jit(solution)/shard_map/scatter | solution.py:51
  17.6 0.7 all_to_all.20
  18.3 11.2 %all-to-all-start = ((f32[128,24,1]{1,2,0:T(1,128)}), f32[128,24,1]{1,2,0:T(1,128)S(1)}, u32[]{:S(2)}, u32[]{:S(2)}) async-start(f32[128,24,1]{1,2,0:T(1,128)} %bitcast.5), calls=%async_computation | async-start | bytes 131072 | tf_op jit(solution)/shard_map/all_to_all | solution.py:54
  29.5 7.2 %scatter_custom_fusion.1 = f32[3072,128]{1,0:T(8,128)} fusion(s32[2048]{0:T(1024)S(1)} %compare_select_fusion.1, f32[2048,128]{1,0:T(8,128)} %param.10, f32[]{:T(128)} %constant.125.clone.1), kind=kCustom, calls=%fused_computation.17 | custom fusion | bytes 1573376 | tf_op jit(solution)/shard_map/scatter | solution.py:48
  36.6 2.3 all-to-all-done
  38.9 7.5 %all-to-all-start.1 = ((f32[128,24,128]{2,1,0:T(8,128)}), f32[128,24,128]{2,1,0:T(8,128)S(1)}, u32[]{:S(2)}, u32[]{:S(2)}) async-start(f32[128,24,128]{2,1,0:T(8,128)} %bitcast.7), calls=%async_computation.1 | async-start | bytes 3145728 | tf_op jit(solution)/shard_map/all_to_all | solution.py:53
  46.4 0.0 copy-done.4
  46.4 0.6 fusion.31
  50.7 0.0 copy-start.3
  50.7 9.3 %reshape.64 = f32[16384,128]{1,0:T(8,128)} reshape(f32[2048,1024]{1,0:T(8,128)} %param.8) | data formatting | bytes 16777216 | tf_op jit(solution)/shard_map/reshape | solution.py:56
  59.9 0.0 copy-done.3
  59.9 0.1 copy.18
  60.0 0.2 convert_reduce_fusion
  60.2 0.1 convert_element_type.32
  60.4 10.5 %all-to-all-done.1 = f32[128,24,128]{2,1,0:T(8,128)S(1)} async-done(((f32[128,24,128]{2,1,0:T(8,128)}), f32[128,24,128]{2,1,0:T(8,128)S(1)}, u32[]{:S(2)}, u32[]{:S(2)}) %all-to-all-start.1) | async-done | bytes 1572896 | tf_op jit(solution)/shard_map/all_to_all | solution.py:53
  70.9 22.0 %scatter_fusion = f32[16384,128]{1,0:T(8,128)} fusion(f32[16384,128]{1,0:T(8,128)} %reshape.64, s32[3072]{0:T(1024)S(1)} %bitcast.52, f32[3072,128]{1,0:T(8,128)S(1)} %bitcast.48), kind=kCustom, calls=%fused_computation.2 | custom fusion | flops 393216 | bytes 4730880 | tf_op jit(solution)/shard_map/scatter-add | solution.py:58
  92.9 9.3 %reshape.66 = f32[2048,1024]{1,0:T(8,128)} reshape(f32[16384,128]{1,0:T(8,128)} %scatter_fusion) | data formatting | bytes 16777216 | tf_op jit(solution)/shard_map/reshape | solution.py:60
  102.2 2.5 constant_dynamic-slice_fusion.2
  104.7 0.6 pad_maximum_fusion
  105.3 0.1 broadcast_in_dim.42
  105.4 2.6 select_maximum_fusion
  108.0 7.2 %all-to-all-start.2 = ((f32[16,129,512]{2,1,0:T(8,128)}), f32[16,129,512]{2,1,0:T(8,128)}, u32[]{:S(2)}, u32[]{:S(2)}) async-start(f32[16,129,512]{2,1,0:T(8,128)} %select_maximum_fusion), calls=%async_computation.2 | async-start | bytes 8912896 | tf_op jit(solution)/shard_map/all_to_all | solution.py:91
  115.2 0.0 copy-start.1
  116.6 1.1 dynamic-slice_select_fusion
  117.7 2.0 collective-permute-start
  119.7 65.7 %collective-permute-done = f32[256,256]{1,0:T(8,128)S(1)} collective-permute-done((f32[256,256]{1,0:T(8,128)S(1)}, f32[256,256]{1,0:T(8,128)S(1)}, u32[]{:S(2)}, u32[]{:S(2)}) %collective-permute-start) | collective-permute-done | bytes 262176 | tf_op jit(solution)/shard_map/ppermute | solution.py:28
  185.4 1.1 fusion.37
  186.6 0.2 collective-permute-start.1
  186.8 8.1 %collective-permute-done.1 = f32[256,256]{1,0:T(8,128)S(1)} collective-permute-done((f32[256,256]{1,0:T(8,128)S(1)}, f32[256,256]{1,0:T(8,128)S(1)}, u32[]{:S(2)}, u32[]{:S(2)}) %collective-permute-start.1) | collective-permute-done | bytes 262176 | tf_op jit(solution)/shard_map/ppermute | solution.py:28
  194.9 0.4 collective-permute-start.2
  195.2 6.3 %collective-permute-done.2 = f32[256,256]{1,0:T(8,128)S(1)} collective-permute-done((f32[256,256]{1,0:T(8,128)S(1)}, f32[256,256]{1,0:T(8,128)S(1)}, u32[]{:S(2)}, u32[]{:S(2)}) %collective-permute-start.2) | collective-permute-done | bytes 262176 | tf_op jit(solution)/shard_map/ppermute | solution.py:28
  201.6 4.1 %collective-permute-start.3 = (f32[256,256]{1,0:T(8,128)S(1)}, f32[256,256]{1,0:T(8,128)S(1)}, u32[]{:S(2)}, u32[]{:S(2)}) collective-permute-start(f32[256,256]{1,0:T(8,128)S(1)} %add.117), channel_id=1, source_target_pairs={{0,8},{1,9},{2,10},{3,11},{4,12},{5,13},{6,14},{7,15},{8,0},{9,1},... | collective-permute-start | bytes 786440 | tf_op jit(solution)/shard_map/ppermute | solution.py:28
  205.7 4.4 %collective-permute-done.3 = f32[256,256]{1,0:T(8,128)S(1)} collective-permute-done((f32[256,256]{1,0:T(8,128)S(1)}, f32[256,256]{1,0:T(8,128)S(1)}, u32[]{:S(2)}, u32[]{:S(2)}) %collective-permute-start.3) | collective-permute-done | bytes 262176 | tf_op jit(solution)/shard_map/ppermute | solution.py:28
  210.1 0.1 collective-permute-start.4
  210.2 1.5 collective-permute-done.4
  211.8 0.3 collective-permute-start.5
  212.0 8.3 %collective-permute-done.5 = f32[256,256]{1,0:T(8,128)S(1)} collective-permute-done((f32[256,256]{1,0:T(8,128)S(1)}, f32[256,256]{1,0:T(8,128)S(1)}, u32[]{:S(2)}, u32[]{:S(2)}) %collective-permute-start.5) | collective-permute-done | bytes 262176 | tf_op jit(solution)/shard_map/ppermute | solution.py:28
  220.4 0.8 collective-permute-start.6
  221.9 7.6 %collective-permute-done.6 = f32[256,256]{1,0:T(8,128)S(1)} collective-permute-done((f32[256,256]{1,0:T(8,128)S(1)}, f32[256,256]{1,0:T(8,128)S(1)}, u32[]{:S(2)}, u32[]{:S(2)}) %collective-permute-start.6) | collective-permute-done | bytes 262176 | tf_op jit(solution)/shard_map/ppermute | solution.py:28
  229.5 0.4 fusion.11
  229.9 0.0 all-to-all-done.2
  229.9 1.1 dynamic-slice_bitcast_fusion
  231.0 0.3 fusion.13
  231.3 0.4 fusion.1
  231.7 0.3 fusion.9
  232.0 0.7 collective-permute-start.7
  232.7 2.5 broadcast_in_dim.45
  235.2 7.4 %all-to-all-start.3 = ((f32[16,128,512]{2,1,0:T(8,128)}), f32[16,128,512]{2,1,0:T(8,128)}, u32[]{:S(2)}, u32[]{:S(2)}) async-start(f32[16,128,512]{2,1,0:T(8,128)} %broadcast_in_dim.45), calls=%async_computation.3 | async-start | bytes 8388608 | tf_op jit(solution)/shard_map/all_to_all | solution.py:21
  242.7 0.0 all-gather.2.cloned.1.call-start
  242.7 0.0 collective-permute-done.7
  242.8 0.7 copy-done.2
  243.5 0.0 all-gather.2.cloned.1.call-update
  243.5 0.1 copy.19
  243.6 64.8 %all-to-all-done.3 = f32[16,128,512]{2,1,0:T(8,128)} async-done(((f32[16,128,512]{2,1,0:T(8,128)}), f32[16,128,512]{2,1,0:T(8,128)}, u32[]{:S(2)}, u32[]{:S(2)}) %all-to-all-start.3) | async-done | bytes 4194336 | tf_op jit(solution)/shard_map/all_to_all | solution.py:21
  308.3 0.1 broadcast_in_dim.46
  308.4 2.3 broadcast_in_dim.47
  310.7 14.6 %fusion = f32[2048,1024]{1,0:T(8,128)} fusion(f32[2048,1024]{1,0:T(8,128)} %reshape.66, f32[256,8,8,128]{3,2,1,0:T(8,128)S(1)} %bitcast.46, f32[2048,512]{1,0:T(8,128)} %bitcast.18, f32[1024,512]{1,0:T(8,128)S(1)} %copy-done), kind=kOutput, calls=%fused_computation.4 | convolution fusion | flops 6446645248 | bytes 31457280 | tf_op jit(solution)/shard_map/dot_general | solution.py:115
  (19 shorter events, 0.3 us)
Async XLA Ops:
  7.8 38.6 %copy-start.4 = (s32[2]{0:T(128)S(1)}, s32[2]{0:T(128)}, u32[]{:S(2)}) copy-start(s32[2]{0:T(128)} %param.14) | copy-start | bytes 28
  18.3 20.6 %all-to-all-start = ((f32[128,24,1]{1,2,0:T(1,128)}), f32[128,24,1]{1,2,0:T(1,128)S(1)}, u32[]{:S(2)}, u32[]{:S(2)}) async-start(f32[128,24,1]{1,2,0:T(1,128)} %bitcast.5), calls=%async_computation | async-start | bytes 131072 | tf_op jit(solution)/shard_map/all_to_all | solution.py:54
  38.9 32.0 %all-to-all-start.1 = ((f32[128,24,128]{2,1,0:T(8,128)}), f32[128,24,128]{2,1,0:T(8,128)S(1)}, u32[]{:S(2)}, u32[]{:S(2)}) async-start(f32[128,24,128]{2,1,0:T(8,128)} %bitcast.7), calls=%async_computation.1 | async-start | bytes 3145728 | tf_op jit(solution)/shard_map/all_to_all | solution.py:53
  50.7 9.3 %copy-start.3 = (s32[16,8]{0,1:T(8,128)S(1)}, s32[16,8]{0,1:T(8,128)}, u32[]{:S(2)}) copy-start(s32[16,8]{0,1:T(8,128)} %param.9) | copy-start | bytes 1540
  108.0 121.8 %all-to-all-start.2 = ((f32[16,129,512]{2,1,0:T(8,128)}), f32[16,129,512]{2,1,0:T(8,128)}, u32[]{:S(2)}, u32[]{:S(2)}) async-start(f32[16,129,512]{2,1,0:T(8,128)} %select_maximum_fusion), calls=%async_computation.2 | async-start | bytes 8912896 | tf_op jit(solution)/shard_map/all_to_all | solution.py:91
  115.2 114.3 %copy-start.1 = (f32[2,256,256]{2,1,0:T(8,128)S(1)}, f32[2,256,256]{2,1,0:T(8,128)}, u32[]{:S(2)}) copy-start(f32[2,256,256]{2,1,0:T(8,128)} %param.15) | copy-start | bytes 1572868
  117.7 67.7 %collective-permute-start = (f32[256,256]{1,0:T(8,128)S(1)}, f32[256,256]{1,0:T(8,128)S(1)}, u32[]{:S(2)}, u32[]{:S(2)}) collective-permute-start(f32[256,256]{1,0:T(8,128)S(1)} %dynamic-slice_select_fusion), channel_id=1, source_target_pairs={{0,1},{1,0},{2,3},{3,2},{4,5},{5,4},{6,7},{7,6},{8,9},{9,8},{10,11... | collective-permute-start | bytes 786440 | tf_op jit(solution)/shard_map/ppermute | solution.py:28
  186.6 8.3 %collective-permute-start.1 = (f32[256,256]{1,0:T(8,128)S(1)}, f32[256,256]{1,0:T(8,128)S(1)}, u32[]{:S(2)}, u32[]{:S(2)}) collective-permute-start(f32[256,256]{1,0:T(8,128)S(1)} %fusion.37), channel_id=1, source_target_pairs={{0,2},{1,3},{2,0},{3,1},{4,6},{5,7},{6,4},{7,5},{8,10},{9,11},{10,... | collective-permute-start | bytes 786440 | tf_op jit(solution)/shard_map/ppermute | solution.py:28
  194.9 6.7 %collective-permute-start.2 = (f32[256,256]{1,0:T(8,128)S(1)}, f32[256,256]{1,0:T(8,128)S(1)}, u32[]{:S(2)}, u32[]{:S(2)}) collective-permute-start(f32[256,256]{1,0:T(8,128)S(1)} %add.116), channel_id=1, source_target_pairs={{0,4},{1,5},{2,6},{3,7},{4,0},{5,1},{6,2},{7,3},{8,12},{9,13},{10,... | collective-permute-start | bytes 786440 | tf_op jit(solution)/shard_map/ppermute | solution.py:28
  201.6 8.5 %collective-permute-start.3 = (f32[256,256]{1,0:T(8,128)S(1)}, f32[256,256]{1,0:T(8,128)S(1)}, u32[]{:S(2)}, u32[]{:S(2)}) collective-permute-start(f32[256,256]{1,0:T(8,128)S(1)} %add.117), channel_id=1, source_target_pairs={{0,8},{1,9},{2,10},{3,11},{4,12},{5,13},{6,14},{7,15},{8,0},{9,1},... | collective-permute-start | bytes 786440 | tf_op jit(solution)/shard_map/ppermute | solution.py:28
  210.1 1.6 collective-permute-start.4
  211.8 8.6 %collective-permute-start.5 = (f32[256,256]{1,0:T(8,128)S(1)}, f32[256,256]{1,0:T(8,128)S(1)}, u32[]{:S(2)}, u32[]{:S(2)}) collective-permute-start(f32[256,256]{1,0:T(8,128)S(1)} %add.119), channel_id=1, source_target_pairs={{0,32},{1,33},{2,34},{3,35},{4,36},{5,37},{6,38},{7,39},{8,40},{9,... | collective-permute-start | bytes 786440 | tf_op jit(solution)/shard_map/ppermute | solution.py:28
  220.4 9.1 %collective-permute-start.6 = (f32[256,256]{1,0:T(8,128)S(1)}, f32[256,256]{1,0:T(8,128)S(1)}, u32[]{:S(2)}, u32[]{:S(2)}) collective-permute-start(f32[256,256]{1,0:T(8,128)S(1)} %add.120), channel_id=1, source_target_pairs={{0,64},{1,65},{2,66},{3,67},{4,68},{5,69},{6,70},{7,71},{8,72},{9,... | collective-permute-start | bytes 786440 | tf_op jit(solution)/shard_map/ppermute | solution.py:28
  232.0 10.7 %collective-permute-start.7 = (f32[128,512]{1,0:T(8,128)S(1)}, f32[128,512]{1,0:T(8,128)S(1)}, u32[]{:S(2)}, u32[]{:S(2)}) collective-permute-start(f32[128,512]{1,0:T(8,128)S(1)} %pad_maximum_fusion.1), channel_id=1, source_target_pairs={{0,0},{1,16},{2,32},{3,48},{4,64},{5,80},{6,96},{7,112},{8,1},{9,1... | collective-permute-start | bytes 786440 | tf_op jit(solution)/shard_map/ppermute | solution.py:112
  235.2 73.1 %all-to-all-start.3 = ((f32[16,128,512]{2,1,0:T(8,128)}), f32[16,128,512]{2,1,0:T(8,128)}, u32[]{:S(2)}, u32[]{:S(2)}) async-start(f32[16,128,512]{2,1,0:T(8,128)} %broadcast_in_dim.45), calls=%async_computation.3 | async-start | bytes 8388608 | tf_op jit(solution)/shard_map/all_to_all | solution.py:21
  242.7 65.7 %all-gather.2.cloned.1.call-start = ((), (), s32[]{:S(2)}) async-start(), calls=%async_computation.4 | async-start | bytes 2359296 | tf_op jit(solution)/shard_map/all_gather | solution.py:113
  242.7 0.7 copy-start.2
  308.4 2.3 copy-start
Sparse Core Ops, SparseCore 0:
  245.2 62.4 all-gather.1

commit v7 on v6

--- a/solution.py
+++ b/solution.py
@@ -23,9 +23,17 @@
 
 
 def spread(x, total):
-    for bit in range(total.bit_length() - 1):
-        pairs = [(i, i ^ (1 << bit)) for i in range(total)]
-        x = x + lax.ppermute(x, ("prow", "pcol"), pairs)
+    bits = total.bit_length() - 1
+    low = 0
+    while low < bits:
+        width = min(2, bits - low)
+        got = []
+        for k in range(1, 1 << width):
+            pairs = [(i, i ^ (k << low)) for i in range(total)]
+            got.append(lax.ppermute(x, ("prow", "pcol"), pairs))
+        for part in got:
+            x = x + part
+        low += width
     return x
 
 

time: 337 us -> 343 us (1.018)
  waiting for transfers between devices: 180 us -> 186 us
    ppermute x7 -> x10, waiting for transfers between devices: 102 us -> 107 us  [spread(): got.append(lax.ppermute(x, ('prow', 'pcol'), pairs))]
    ppermute x7 -> x10, starting transfers between devices: 7.79 us -> 11.7 us  [spread(): got.append(lax.ppermute(x, ('prow', 'pcol'), pairs))]
  transfers between devices with their start and end apart: 13 -> 16, of which waited for: 10 -> 11; matrix products, arithmetic and copies ran while one was open for 7% -> 7% of each run, Pallas kernels for 0% -> 0%
where the time goes in v7:
time: 343 us; the launch traced here: 341 us
  waiting for transfers between devices  186 us (54%)
  local copies, waits for them, and re-layouts  45.1 us (13%)
  starting transfers between devices  43.9 us (13%)
  other arithmetic  29.9 us (9%)
  between operations  20.1 us (6%)
  matrix products  15.9 us (5%)
    ppermute x10, waiting for transfers between devices, spread(): got.append(lax.ppermute(x, ('prow', 'pcol'), pairs))  107 us
    all_to_all x1, waiting for transfers between devices, gather_rows(): got = lax.all_to_all(spread, axis, 0, 0, tiled=False)  66.7 us
    scatter-add x1, other arithmetic, assemble(): flat = front.reshape(rows_local * blocks_local, 128).at[got_place.astype(...  22.1 us
    dot_general x1, matrix products, body(): jnp.dot(left_rows, left_cols.T, precision=lax.Precision.HIGH, preferred_e...  14.6 us
    ppermute x10, starting transfers between devices, spread(): got.append(lax.ppermute(x, ('prow', 'pcol'), pairs))  11.7 us
    all_to_all x1, starting transfers between devices, assemble(): got_place = lax.all_to_all(send_place, ('prow', 'pcol'), 0, 0, tiled=True)  11.2 us
    all_to_all x1, waiting for transfers between devices, assemble(): got_values = lax.all_to_all(send_values, ('prow', 'pcol'), 0, 0, tiled=True)  10.4 us
    reshape x1, local copies, waits for them, and re-layouts, assemble(): return flat.reshape(rows_local, cols_local)  9.27 us
  transfers between devices with their start and end apart: 16, of which 11 were waited for; matrix products, arithmetic and copies ran while one was open for 7% of the time, Pallas kernels for 0%

profile of v7, /device:TPU:0, one launch (start us, length us, event | category | flops | bytes accessed | tf_op | source)
XLA Modules:
  0.0 341.0 jit_solution(14904883908101438645)
XLA Ops:
  6.5 0.7 fusion.24
  7.3 0.1 copy.15
  7.4 0.3 fusion.4
  7.8 0.1 broadcast_add_fusion
  7.9 0.3 copy.16
  8.2 0.6 fusion.3
  9.5 8.1 %scatter_custom_fusion = f32[3072]{0:T(1024)S(1)} fusion(s32[2048]{0:T(1024)S(1)} %compare_select_fusion.1, f32[2048]{0:T(1024)S(1)} %get-tuple-element.9, f32[]{:T(128)} %constant.125.clone.1), kind=kCustom, calls=%fused_computation.63 | custom fusion | bytes 12292 | tf_op jit(solution)/shard_map/scatter | solution.py:59
  17.6 0.7 all_to_all.20
  18.3 11.2 %all-to-all-start = ((f32[128,24,1]{1,2,0:T(1,128)}), f32[128,24,1]{1,2,0:T(1,128)S(1)}, u32[]{:S(2)}, u32[]{:S(2)}) async-start(f32[128,24,1]{1,2,0:T(1,128)} %bitcast.5), calls=%async_computation | async-start | bytes 131072 | tf_op jit(solution)/shard_map/all_to_all | solution.py:62
  29.5 7.2 %scatter_custom_fusion.1 = f32[3072,128]{1,0:T(8,128)} fusion(s32[2048]{0:T(1024)S(1)} %compare_select_fusion.1, f32[2048,128]{1,0:T(8,128)} %param.10, f32[]{:T(128)} %constant.125.clone.1), kind=kCustom, calls=%fused_computation.17 | custom fusion | bytes 1573376 | tf_op jit(solution)/shard_map/scatter | solution.py:56
  36.7 2.2 all-to-all-done
  38.9 7.5 %all-to-all-start.1 = ((f32[128,24,128]{2,1,0:T(8,128)}), f32[128,24,128]{2,1,0:T(8,128)S(1)}, u32[]{:S(2)}, u32[]{:S(2)}) async-start(f32[128,24,128]{2,1,0:T(8,128)} %bitcast.7), calls=%async_computation.1 | async-start | bytes 3145728 | tf_op jit(solution)/shard_map/all_to_all | solution.py:61
  46.4 0.6 fusion.31
  50.8 0.0 copy-start.3
  50.8 9.3 %reshape.64 = f32[16384,128]{1,0:T(8,128)} reshape(f32[2048,1024]{1,0:T(8,128)} %param.8) | data formatting | bytes 16777216 | tf_op jit(solution)/shard_map/reshape | solution.py:64
  60.1 0.1 copy.18
  60.2 0.2 convert_reduce_fusion
  60.4 0.1 convert_element_type.32
  60.5 10.4 %all-to-all-done.1 = f32[128,24,128]{2,1,0:T(8,128)S(1)} async-done(((f32[128,24,128]{2,1,0:T(8,128)}), f32[128,24,128]{2,1,0:T(8,128)S(1)}, u32[]{:S(2)}, u32[]{:S(2)}) %all-to-all-start.1) | async-done | bytes 1572896 | tf_op jit(solution)/shard_map/all_to_all | solution.py:61
  70.9 22.1 %scatter_fusion = f32[16384,128]{1,0:T(8,128)} fusion(f32[16384,128]{1,0:T(8,128)} %reshape.64, s32[3072]{0:T(1024)S(1)} %bitcast.52, f32[3072,128]{1,0:T(8,128)S(1)} %bitcast.48), kind=kCustom, calls=%fused_computation.2 | custom fusion | flops 393216 | bytes 4730880 | tf_op jit(solution)/shard_map/scatter-add | solution.py:66
  93.0 9.3 %reshape.66 = f32[2048,1024]{1,0:T(8,128)} reshape(f32[16384,128]{1,0:T(8,128)} %scatter_fusion) | data formatting | bytes 16777216 | tf_op jit(solution)/shard_map/reshape | solution.py:68
  102.3 2.5 constant_dynamic-slice_fusion.2
  104.8 0.6 pad_maximum_fusion
  105.5 0.1 broadcast_in_dim.42
  105.6 2.6 select_maximum_fusion
  108.2 6.5 %all-to-all-start.2 = ((f32[16,129,512]{2,1,0:T(8,128)}), f32[16,129,512]{2,1,0:T(8,128)}, u32[]{:S(2)}, u32[]{:S(2)}) async-start(f32[16,129,512]{2,1,0:T(8,128)} %select_maximum_fusion), calls=%async_computation.2 | async-start | bytes 8912896 | tf_op jit(solution)/shard_map/all_to_all | solution.py:99
  116.0 1.1 dynamic-slice_select_fusion
  117.2 2.0 collective-permute-start
  119.1 2.7 collective-permute-start.1
  121.8 0.1 collective-permute-start.2
  122.0 65.9 %collective-permute-done = f32[256,256]{1,0:T(8,128)S(1)} collective-permute-done((f32[256,256]{1,0:T(8,128)S(1)}, f32[256,256]{1,0:T(8,128)S(1)}, u32[]{:S(2)}, u32[]{:S(2)}) %collective-permute-start) | collective-permute-done | bytes 262176 | tf_op jit(solution)/shard_map/ppermute | solution.py:33
  187.9 6.3 %collective-permute-done.1 = f32[256,256]{1,0:T(8,128)S(1)} collective-permute-done((f32[256,256]{1,0:T(8,128)S(1)}, f32[256,256]{1,0:T(8,128)S(1)}, u32[]{:S(2)}, u32[]{:S(2)}) %collective-permute-start.1) | collective-permute-done | bytes 262176 | tf_op jit(solution)/shard_map/ppermute | solution.py:33
  194.2 1.1 add_add_fusion.2
  195.4 0.6 collective-permute-start.3
  196.0 3.0 collective-permute-start.4
  199.0 1.1 collective-permute-start.5
  200.1 4.5 %collective-permute-done.3 = f32[256,256]{1,0:T(8,128)S(1)} collective-permute-done((f32[256,256]{1,0:T(8,128)S(1)}, f32[256,256]{1,0:T(8,128)S(1)}, u32[]{:S(2)}, u32[]{:S(2)}) %collective-permute-start.3) | collective-permute-done | bytes 262176 | tf_op jit(solution)/shard_map/ppermute | solution.py:33
  204.6 6.0 %collective-permute-done.4 = f32[256,256]{1,0:T(8,128)S(1)} collective-permute-done((f32[256,256]{1,0:T(8,128)S(1)}, f32[256,256]{1,0:T(8,128)S(1)}, u32[]{:S(2)}, u32[]{:S(2)}) %collective-permute-start.4) | collective-permute-done | bytes 262176 | tf_op jit(solution)/shard_map/ppermute | solution.py:33
  210.7 2.6 collective-permute-done.5
  213.2 0.1 add_add_fusion.1
  213.3 0.3 collective-permute-start.6
  213.6 0.1 collective-permute-start.7
  213.7 1.8 collective-permute-start.8
  215.4 7.4 %collective-permute-done.7 = f32[256,256]{1,0:T(8,128)S(1)} collective-permute-done((f32[256,256]{1,0:T(8,128)S(1)}, f32[256,256]{1,0:T(8,128)S(1)}, u32[]{:S(2)}, u32[]{:S(2)}) %collective-permute-start.7) | collective-permute-done | bytes 262176 | tf_op jit(solution)/shard_map/ppermute | solution.py:33
  222.8 4.5 %collective-permute-done.8 = f32[256,256]{1,0:T(8,128)S(1)} collective-permute-done((f32[256,256]{1,0:T(8,128)S(1)}, f32[256,256]{1,0:T(8,128)S(1)}, u32[]{:S(2)}, u32[]{:S(2)}) %collective-permute-start.8) | collective-permute-done | bytes 262176 | tf_op jit(solution)/shard_map/ppermute | solution.py:33
  227.4 0.1 add_add_fusion
  227.4 0.1 collective-permute-start.9
  228.1 9.5 %collective-permute-done.9 = f32[256,256]{1,0:T(8,128)S(1)} collective-permute-done((f32[256,256]{1,0:T(8,128)S(1)}, f32[256,256]{1,0:T(8,128)S(1)}, u32[]{:S(2)}, u32[]{:S(2)}) %collective-permute-start.9) | collective-permute-done | bytes 262176 | tf_op jit(solution)/shard_map/ppermute | solution.py:33
  237.6 0.4 fusion.11
  238.0 1.1 dynamic-slice_bitcast_fusion
  239.1 0.3 fusion.13
  239.4 0.4 fusion.1
  239.8 0.3 fusion.9
  240.1 0.7 collective-permute-start.10
  240.8 2.5 broadcast_in_dim.45
  243.3 6.3 %all-to-all-start.3 = ((f32[16,128,512]{2,1,0:T(8,128)}), f32[16,128,512]{2,1,0:T(8,128)}, u32[]{:S(2)}, u32[]{:S(2)}) async-start(f32[16,128,512]{2,1,0:T(8,128)} %broadcast_in_dim.45), calls=%async_computation.3 | async-start | bytes 8388608 | tf_op jit(solution)/shard_map/all_to_all | solution.py:21
  249.6 0.0 all-gather.2.cloned.1.call-start
  249.7 0.7 copy-done.2
  250.4 0.0 all-gather.2.cloned.1.call-update
  250.4 0.1 copy.19
  250.5 66.7 %all-to-all-done.3 = f32[16,128,512]{2,1,0:T(8,128)} async-done(((f32[16,128,512]{2,1,0:T(8,128)}), f32[16,128,512]{2,1,0:T(8,128)}, u32[]{:S(2)}, u32[]{:S(2)}) %all-to-all-start.3) | async-done | bytes 4194336 | tf_op jit(solution)/shard_map/all_to_all | solution.py:21
  317.1 0.1 broadcast_in_dim.46
  317.2 2.3 broadcast_in_dim.47
  319.5 14.6 %fusion = f32[2048,1024]{1,0:T(8,128)} fusion(f32[2048,1024]{1,0:T(8,128)} %reshape.66, f32[256,8,8,128]{3,2,1,0:T(8,128)S(1)} %bitcast.46, f32[2048,512]{1,0:T(8,128)} %bitcast.18, f32[1024,512]{1,0:T(8,128)S(1)} %copy-done), kind=kOutput, calls=%fused_computation.4 | convolution fusion | flops 6446645248 | bytes 31457280 | tf_op jit(solution)/shard_map/dot_general | solution.py:123
  (22 shorter events, 0.1 us)
Async XLA Ops:
  7.8 38.6 %copy-start.4 = (s32[2]{0:T(128)S(1)}, s32[2]{0:T(128)}, u32[]{:S(2)}) copy-start(s32[2]{0:T(128)} %param.14) | copy-start | bytes 28
  18.3 20.6 %all-to-all-start = ((f32[128,24,1]{1,2,0:T(1,128)}), f32[128,24,1]{1,2,0:T(1,128)S(1)}, u32[]{:S(2)}, u32[]{:S(2)}) async-start(f32[128,24,1]{1,2,0:T(1,128)} %bitcast.5), calls=%async_computation | async-start | bytes 131072 | tf_op jit(solution)/shard_map/all_to_all | solution.py:62
  38.9 32.0 %all-to-all-start.1 = ((f32[128,24,128]{2,1,0:T(8,128)}), f32[128,24,128]{2,1,0:T(8,128)S(1)}, u32[]{:S(2)}, u32[]{:S(2)}) async-start(f32[128,24,128]{2,1,0:T(8,128)} %bitcast.7), calls=%async_computation.1 | async-start | bytes 3145728 | tf_op jit(solution)/shard_map/all_to_all | solution.py:61
  50.8 9.3 %copy-start.3 = (s32[16,8]{0,1:T(8,128)S(1)}, s32[16,8]{0,1:T(8,128)}, u32[]{:S(2)}) copy-start(s32[16,8]{0,1:T(8,128)} %param.9) | copy-start | bytes 1540
  108.2 129.8 %all-to-all-start.2 = ((f32[16,129,512]{2,1,0:T(8,128)}), f32[16,129,512]{2,1,0:T(8,128)}, u32[]{:S(2)}, u32[]{:S(2)}) async-start(f32[16,129,512]{2,1,0:T(8,128)} %select_maximum_fusion), calls=%async_computation.2 | async-start | bytes 8912896 | tf_op jit(solution)/shard_map/all_to_all | solution.py:99
  114.7 122.9 %copy-start.1 = (f32[2,256,256]{2,1,0:T(8,128)S(1)}, f32[2,256,256]{2,1,0:T(8,128)}, u32[]{:S(2)}) copy-start(f32[2,256,256]{2,1,0:T(8,128)} %param.15) | copy-start | bytes 1572868
  117.2 70.7 %collective-permute-start = (f32[256,256]{1,0:T(8,128)S(1)}, f32[256,256]{1,0:T(8,128)S(1)}, u32[]{:S(2)}, u32[]{:S(2)}) collective-permute-start(f32[256,256]{1,0:T(8,128)S(1)} %dynamic-slice_select_fusion), channel_id=1, source_target_pairs={{0,1},{1,0},{2,3},{3,2},{4,5},{5,4},{6,7},{7,6},{8,9},{9,8},{10,11... | collective-permute-start | bytes 786440 | tf_op jit(solution)/shard_map/ppermute | solution.py:33
  119.1 75.1 %collective-permute-start.1 = (f32[256,256]{1,0:T(8,128)S(1)}, f32[256,256]{1,0:T(8,128)S(1)}, u32[]{:S(2)}, u32[]{:S(2)}) collective-permute-start(f32[256,256]{1,0:T(8,128)S(1)} %dynamic-slice_select_fusion), channel_id=1, source_target_pairs={{0,2},{1,3},{2,0},{3,1},{4,6},{5,7},{6,4},{7,5},{8,10},{9,11},{10,... | collective-permute-start | bytes 786440 | tf_op jit(solution)/shard_map/ppermute | solution.py:33
  121.8 72.4 %collective-permute-start.2 = (f32[256,256]{1,0:T(8,128)S(1)}, f32[256,256]{1,0:T(8,128)S(1)}, u32[]{:S(2)}, u32[]{:S(2)}) collective-permute-start(f32[256,256]{1,0:T(8,128)S(1)} %dynamic-slice_select_fusion), channel_id=1, source_target_pairs={{0,3},{1,2},{2,1},{3,0},{4,7},{5,6},{6,5},{7,4},{8,11},{9,10},{10,... | collective-permute-start | bytes 786440 | tf_op jit(solution)/shard_map/ppermute | solution.py:33
  195.4 9.3 %collective-permute-start.3 = (f32[256,256]{1,0:T(8,128)S(1)}, f32[256,256]{1,0:T(8,128)S(1)}, u32[]{:S(2)}, u32[]{:S(2)}) collective-permute-start(f32[256,256]{1,0:T(8,128)S(1)} %add_add_fusion.2), channel_id=1, source_target_pairs={{0,4},{1,5},{2,6},{3,7},{4,0},{5,1},{6,2},{7,3},{8,12},{9,13},{10,... | collective-permute-start | bytes 786440 | tf_op jit(solution)/shard_map/ppermute | solution.py:33
  196.0 14.7 %collective-permute-start.4 = (f32[256,256]{1,0:T(8,128)S(1)}, f32[256,256]{1,0:T(8,128)S(1)}, u32[]{:S(2)}, u32[]{:S(2)}) collective-permute-start(f32[256,256]{1,0:T(8,128)S(1)} %add_add_fusion.2), channel_id=1, source_target_pairs={{0,8},{1,9},{2,10},{3,11},{4,12},{5,13},{6,14},{7,15},{8,0},{9,1},... | collective-permute-start | bytes 786440 | tf_op jit(solution)/shard_map/ppermute | solution.py:33
  199.0 14.2 %collective-permute-start.5 = (f32[256,256]{1,0:T(8,128)S(1)}, f32[256,256]{1,0:T(8,128)S(1)}, u32[]{:S(2)}, u32[]{:S(2)}) collective-permute-start(f32[256,256]{1,0:T(8,128)S(1)} %add_add_fusion.2), channel_id=1, source_target_pairs={{0,12},{1,13},{2,14},{3,15},{4,8},{5,9},{6,10},{7,11},{8,4},{9,5},... | collective-permute-start | bytes 786440 | tf_op jit(solution)/shard_map/ppermute | solution.py:33
  213.3 2.1 collective-permute-start.6
  213.6 9.3 %collective-permute-start.7 = (f32[256,256]{1,0:T(8,128)S(1)}, f32[256,256]{1,0:T(8,128)S(1)}, u32[]{:S(2)}, u32[]{:S(2)}) collective-permute-start(f32[256,256]{1,0:T(8,128)S(1)} %add_add_fusion.1), channel_id=1, source_target_pairs={{0,32},{1,33},{2,34},{3,35},{4,36},{5,37},{6,38},{7,39},{8,40},{9,... | collective-permute-start | bytes 786440 | tf_op jit(solution)/shard_map/ppermute | solution.py:33
  213.7 13.7 %collective-permute-start.8 = (f32[256,256]{1,0:T(8,128)S(1)}, f32[256,256]{1,0:T(8,128)S(1)}, u32[]{:S(2)}, u32[]{:S(2)}) collective-permute-start(f32[256,256]{1,0:T(8,128)S(1)} %add_add_fusion.1), channel_id=1, source_target_pairs={{0,48},{1,49},{2,50},{3,51},{4,52},{5,53},{6,54},{7,55},{8,56},{9,... | collective-permute-start | bytes 786440 | tf_op jit(solution)/shard_map/ppermute | solution.py:33
  227.4 10.2 %collective-permute-start.9 = (f32[256,256]{1,0:T(8,128)S(1)}, f32[256,256]{1,0:T(8,128)S(1)}, u32[]{:S(2)}, u32[]{:S(2)}) collective-permute-start(f32[256,256]{1,0:T(8,128)S(1)} %add_add_fusion), channel_id=1, source_target_pairs={{0,64},{1,65},{2,66},{3,67},{4,68},{5,69},{6,70},{7,71},{8,72},{9,... | collective-permute-start | bytes 786440 | tf_op jit(solution)/shard_map/ppermute | solution.py:33
  240.1 9.5 %collective-permute-start.10 = (f32[128,512]{1,0:T(8,128)S(1)}, f32[128,512]{1,0:T(8,128)S(1)}, u32[]{:S(2)}, u32[]{:S(2)}) collective-permute-start(f32[128,512]{1,0:T(8,128)S(1)} %pad_maximum_fusion.1), channel_id=1, source_target_pairs={{0,0},{1,16},{2,32},{3,48},{4,64},{5,80},{6,96},{7,112},{8,1},{9,1... | collective-permute-start | bytes 786440 | tf_op jit(solution)/shard_map/ppermute | solution.py:120
  243.3 73.8 %all-to-all-start.3 = ((f32[16,128,512]{2,1,0:T(8,128)}), f32[16,128,512]{2,1,0:T(8,128)}, u32[]{:S(2)}, u32[]{:S(2)}) async-start(f32[16,128,512]{2,1,0:T(8,128)} %broadcast_in_dim.45), calls=%async_computation.3 | async-start | bytes 8388608 | tf_op jit(solution)/shard_map/all_to_all | solution.py:21
  249.6 67.5 %all-gather.2.cloned.1.call-start = ((), (), s32[]{:S(2)}) async-start(), calls=%async_computation.4 | async-start | bytes 2359296 | tf_op jit(solution)/shard_map/all_gather | solution.py:121
  249.7 0.7 copy-start.2
  317.2 2.3 copy-start
Sparse Core Ops, SparseCore 0:
  252.1 62.3 all-gather.1

commit v8 on v6

--- a/solution.py
+++ b/solution.py
@@ -50,8 +50,11 @@
     send_place = (
         jnp.zeros((devices * capacity,), jnp.float32).at[slot].set(local_place, mode="drop")
     )
-    got_values = lax.all_to_all(send_values, ("prow", "pcol"), 0, 0, tiled=True)
-    got_place = lax.all_to_all(send_place, ("prow", "pcol"), 0, 0, tiled=True)
+    place_row = jnp.pad(send_place.reshape(devices, 1, capacity), ((0, 0), (0, 0), (0, 128 - capacity)))
+    send = jnp.concatenate([send_values.reshape(devices, capacity, 128), place_row], axis=1)
+    got = lax.all_to_all(send, ("prow", "pcol"), 0, 0, tiled=True)
+    got_values = got[:, :capacity, :].reshape(devices * capacity, 128)
+    got_place = got[:, capacity, :capacity].reshape(devices * capacity)
     flat = (
         front.reshape(rows_local * blocks_local, 128)
         .at[got_place.astype(jnp.int32)]

time: 337 us -> 335 us (level)
  other arithmetic: 29.8 us -> 36 us
  waiting for transfers between devices: 180 us -> 175 us
    ppermute x7, waiting for transfers between devices: 102 us -> 93.3 us  [spread(): x = x + lax.ppermute(x, ('prow', 'pcol'), pairs)]
    ppermute x7, starting transfers between devices: 7.79 us -> 15.6 us  [spread(): x = x + lax.ppermute(x, ('prow', 'pcol'), pairs)]
    all_to_all x2 -> x1, starting transfers between devices: 18.7 us -> 11.2 us  [assemble(): got = lax.all_to_all(send, ('prow', 'pcol'), 0, 0, tiled=True)]
    scatter-add x1, other arithmetic: 22 us -> 26.7 us  [assemble(): flat = front.reshape(rows_local * blocks_local, 128).at[got_place.astype(...]
    all_to_all x2 -> x1, waiting for transfers between devices: 12.8 us -> 15.9 us  [assemble(): got = lax.all_to_all(send, ('prow', 'pcol'), 0, 0, tiled=True)]
  transfers between devices with their start and end apart: 13 -> 12, of which waited for: 10 -> 9; matrix products, arithmetic and copies ran while one was open for 7% -> 5% of each run, Pallas kernels for 0% -> 0%
where the time goes in v8:
time: 335 us; the launch traced here: 334 us
  waiting for transfers between devices  175 us (52%)
  local copies, waits for them, and re-layouts  45 us (13%)
  starting transfers between devices  41.8 us (12%)
  other arithmetic  36 us (11%)
  between operations  20.3 us (6%)
  matrix products  15.9 us (5%)
    ppermute x7, waiting for transfers between devices, spread(): x = x + lax.ppermute(x, ('prow', 'pcol'), pairs)  93.3 us
    all_to_all x1, waiting for transfers between devices, gather_rows(): got = lax.all_to_all(spread, axis, 0, 0, tiled=False)  65.3 us
    scatter-add x1, other arithmetic, assemble(): flat = front.reshape(rows_local * blocks_local, 128).at[got_place.astype(...  26.7 us
    all_to_all x1, waiting for transfers between devices, assemble(): got = lax.all_to_all(send, ('prow', 'pcol'), 0, 0, tiled=True)  15.9 us
    ppermute x7, starting transfers between devices, spread(): x = x + lax.ppermute(x, ('prow', 'pcol'), pairs)  15.6 us
    dot_general x1, matrix products, body(): jnp.dot(left_rows, left_cols.T, precision=lax.Precision.HIGH, preferred_e...  14.6 us
    all_to_all x1, starting transfers between devices, assemble(): got = lax.all_to_all(send, ('prow', 'pcol'), 0, 0, tiled=True)  11.2 us
    all_to_all x1, starting transfers between devices, gather_rows(): got = lax.all_to_all(spread, axis, 0, 0, tiled=False)  9.77 us
  transfers between devices with their start and end apart: 12, of which 9 were waited for; matrix products, arithmetic and copies ran while one was open for 5% of the time, Pallas kernels for 0%

profile of v8, /device:TPU:0, one launch (start us, length us, event | category | flops | bytes accessed | tf_op | source)
XLA Modules:
  0.0 333.5 jit_solution(14120162967641343595)
XLA Ops:
  6.5 0.7 fusion.25
  7.3 0.1 copy.16
  7.4 0.3 fusion.4
  7.8 0.1 broadcast_add_fusion
  7.8 0.3 copy.17
  8.2 0.6 fusion.3
  9.5 8.1 %scatter_custom_fusion.1 = f32[3072]{0:T(1024)S(1)} fusion(s32[2048]{0:T(1024)S(1)} %compare_select_fusion.1, f32[2048]{0:T(1024)S(1)} %get-tuple-element.9, f32[]{:T(128)} %constant.125.clone.1), kind=kCustom, calls=%fused_computation.62 | custom fusion | bytes 12292 | tf_op jit(solution)/shard_map/scatter | solution.py:51
  17.6 0.1 reshape.72
  17.7 6.4 %scatter_custom_fusion = f32[3072,128]{1,0:T(8,128)S(1)} fusion(s32[2048]{0:T(1024)S(1)} %compare_select_fusion.1, f32[2048,128]{1,0:T(8,128)} %param.10, f32[]{:T(128)} %constant.125.clone.1), kind=kCustom, calls=%fused_computation.18 | custom fusion | bytes 1573376 | tf_op jit(solution)/shard_map/scatter | solution.py:48
  24.0 0.0 copy-start.4
  24.0 1.6 pad_maximum_fusion.1
  25.6 11.2 %all-to-all-start = ((f32[128,25,128]{2,1,0:T(8,128)}), f32[128,25,128]{2,1,0:T(8,128)S(1)}, u32[]{:S(2)}, u32[]{:S(2)}) async-start(f32[128,25,128]{2,1,0:T(8,128)} %pad_maximum_fusion.1), calls=%async_computation | async-start | bytes 4194304 | tf_op jit(solution)/shard_map/all_to_all | solution.py:55
  36.8 0.0 copy-done.4
  36.8 0.6 fusion.32
  41.3 0.0 copy-start.3
  41.3 9.3 %reshape.69 = f32[16384,128]{1,0:T(8,128)} reshape(f32[2048,1024]{1,0:T(8,128)} %param.8) | data formatting | bytes 16777216 | tf_op jit(solution)/shard_map/reshape | solution.py:59
  50.6 0.1 copy.19
  50.7 15.9 %all-to-all-done = f32[128,25,128]{2,1,0:T(8,128)S(1)} async-done(((f32[128,25,128]{2,1,0:T(8,128)}), f32[128,25,128]{2,1,0:T(8,128)S(1)}, u32[]{:S(2)}, u32[]{:S(2)}) %all-to-all-start) | async-done | bytes 1638432 | tf_op jit(solution)/shard_map/all_to_all | solution.py:55
  66.6 0.2 fusion.20
  66.8 0.1 convert_element_type.34
  66.9 1.3 slice.51
  68.2 26.7 %scatter_fusion = f32[16384,128]{1,0:T(8,128)} fusion(f32[16384,128]{1,0:T(8,128)} %reshape.69, s32[3072]{0:T(1024)S(1)} %bitcast.54, f32[3072,128]{1,0:T(8,128)} %bitcast.49), kind=kCustom, calls=%fused_computation.2 | custom fusion | flops 393216 | bytes 4730880 | tf_op jit(solution)/shard_map/scatter-add | solution.py:61
  94.9 9.3 %reshape.74 = f32[2048,1024]{1,0:T(8,128)} reshape(f32[16384,128]{1,0:T(8,128)} %scatter_fusion) | data formatting | bytes 16777216 | tf_op jit(solution)/shard_map/reshape | solution.py:63
  104.2 2.5 constant_dynamic-slice_fusion.2
  106.7 0.6 pad_maximum_fusion
  107.4 0.1 broadcast_in_dim.42
  107.4 2.6 select_maximum_fusion
  110.1 4.6 %all-to-all-start.1 = ((f32[16,129,512]{2,1,0:T(8,128)}), f32[16,129,512]{2,1,0:T(8,128)}, u32[]{:S(2)}, u32[]{:S(2)}) async-start(f32[16,129,512]{2,1,0:T(8,128)} %select_maximum_fusion), calls=%async_computation.1 | async-start | bytes 8912896 | tf_op jit(solution)/shard_map/all_to_all | solution.py:94
  114.6 0.0 copy-start.1
  116.1 1.1 dynamic-slice_select_fusion
  117.2 1.8 collective-permute-start
  119.0 61.7 %collective-permute-done = f32[256,256]{1,0:T(8,128)S(1)} collective-permute-done((f32[256,256]{1,0:T(8,128)S(1)}, f32[256,256]{1,0:T(8,128)S(1)}, u32[]{:S(2)}, u32[]{:S(2)}) %collective-permute-start) | collective-permute-done | bytes 262176 | tf_op jit(solution)/shard_map/ppermute | solution.py:28
  180.7 1.1 fusion.38
  181.8 1.9 collective-permute-start.1
  183.8 6.0 %collective-permute-done.1 = f32[256,256]{1,0:T(8,128)S(1)} collective-permute-done((f32[256,256]{1,0:T(8,128)S(1)}, f32[256,256]{1,0:T(8,128)S(1)}, u32[]{:S(2)}, u32[]{:S(2)}) %collective-permute-start.1) | collective-permute-done | bytes 262176 | tf_op jit(solution)/shard_map/ppermute | solution.py:28
  189.8 0.1 collective-permute-start.2
  189.9 7.7 %collective-permute-done.2 = f32[256,256]{1,0:T(8,128)S(1)} collective-permute-done((f32[256,256]{1,0:T(8,128)S(1)}, f32[256,256]{1,0:T(8,128)S(1)}, u32[]{:S(2)}, u32[]{:S(2)}) %collective-permute-start.2) | collective-permute-done | bytes 262176 | tf_op jit(solution)/shard_map/ppermute | solution.py:28
  197.7 4.3 %collective-permute-start.3 = (f32[256,256]{1,0:T(8,128)S(1)}, f32[256,256]{1,0:T(8,128)S(1)}, u32[]{:S(2)}, u32[]{:S(2)}) collective-permute-start(f32[256,256]{1,0:T(8,128)S(1)} %add.119), channel_id=1, source_target_pairs={{0,8},{1,9},{2,10},{3,11},{4,12},{5,13},{6,14},{7,15},{8,0},{9,1},... | collective-permute-start | bytes 786440 | tf_op jit(solution)/shard_map/ppermute | solution.py:28
  202.0 4.4 %collective-permute-done.3 = f32[256,256]{1,0:T(8,128)S(1)} collective-permute-done((f32[256,256]{1,0:T(8,128)S(1)}, f32[256,256]{1,0:T(8,128)S(1)}, u32[]{:S(2)}, u32[]{:S(2)}) %collective-permute-start.3) | collective-permute-done | bytes 262176 | tf_op jit(solution)/shard_map/ppermute | solution.py:28
  206.4 0.1 collective-permute-start.4
  206.4 1.5 collective-permute-done.4
  208.0 3.2 collective-permute-start.5
  211.2 6.6 %collective-permute-done.5 = f32[256,256]{1,0:T(8,128)S(1)} collective-permute-done((f32[256,256]{1,0:T(8,128)S(1)}, f32[256,256]{1,0:T(8,128)S(1)}, u32[]{:S(2)}, u32[]{:S(2)}) %collective-permute-start.5) | collective-permute-done | bytes 262176 | tf_op jit(solution)/shard_map/ppermute | solution.py:28
  217.8 4.1 %collective-permute-start.6 = (f32[256,256]{1,0:T(8,128)S(1)}, f32[256,256]{1,0:T(8,128)S(1)}, u32[]{:S(2)}, u32[]{:S(2)}) collective-permute-start(f32[256,256]{1,0:T(8,128)S(1)} %add.122), channel_id=1, source_target_pairs={{0,64},{1,65},{2,66},{3,67},{4,68},{5,69},{6,70},{7,71},{8,72},{9,... | collective-permute-start | bytes 786440 | tf_op jit(solution)/shard_map/ppermute | solution.py:28
  222.6 5.4 %collective-permute-done.6 = f32[256,256]{1,0:T(8,128)S(1)} collective-permute-done((f32[256,256]{1,0:T(8,128)S(1)}, f32[256,256]{1,0:T(8,128)S(1)}, u32[]{:S(2)}, u32[]{:S(2)}) %collective-permute-start.6) | collective-permute-done | bytes 262176 | tf_op jit(solution)/shard_map/ppermute | solution.py:28
  228.0 0.4 fusion.11
  228.4 0.0 all-to-all-done.1
  228.4 1.1 dynamic-slice_bitcast_fusion
  229.5 0.3 fusion.13
  229.8 0.4 fusion.1
  230.2 0.3 fusion.9
  230.5 0.7 collective-permute-start.7
  231.2 2.5 broadcast_in_dim.45
  233.7 9.8 %all-to-all-start.2 = ((f32[16,128,512]{2,1,0:T(8,128)}), f32[16,128,512]{2,1,0:T(8,128)}, u32[]{:S(2)}, u32[]{:S(2)}) async-start(f32[16,128,512]{2,1,0:T(8,128)} %broadcast_in_dim.45), calls=%async_computation.2 | async-start | bytes 8388608 | tf_op jit(solution)/shard_map/all_to_all | solution.py:21
  243.5 0.0 all-gather.2.cloned.1.call-start
  243.6 0.0 collective-permute-done.7
  243.6 0.7 copy-done.2
  244.3 0.0 all-gather.2.cloned.1.call-update
  244.3 0.1 copy.20
  244.4 65.3 %all-to-all-done.2 = f32[16,128,512]{2,1,0:T(8,128)} async-done(((f32[16,128,512]{2,1,0:T(8,128)}), f32[16,128,512]{2,1,0:T(8,128)}, u32[]{:S(2)}, u32[]{:S(2)}) %all-to-all-start.2) | async-done | bytes 4194336 | tf_op jit(solution)/shard_map/all_to_all | solution.py:21
  309.7 0.1 broadcast_in_dim.46
  309.8 0.0 copy-start
  309.8 2.3 broadcast_in_dim.47
  312.1 14.6 %fusion = f32[2048,1024]{1,0:T(8,128)} fusion(f32[2048,1024]{1,0:T(8,128)} %reshape.74, f32[256,8,8,128]{3,2,1,0:T(8,128)S(1)} %bitcast.46, f32[2048,512]{1,0:T(8,128)} %bitcast.18, f32[1024,512]{1,0:T(8,128)S(1)} %copy-done), kind=kOutput, calls=%fused_computation.4 | convolution fusion | flops 6446645248 | bytes 31457280 | tf_op jit(solution)/shard_map/dot_general | solution.py:118
  (20 shorter events, 0.3 us)
Async XLA Ops:
  24.0 12.8 %copy-start.4 = (s32[2]{0:T(128)S(1)}, s32[2]{0:T(128)}, u32[]{:S(2)}) copy-start(s32[2]{0:T(128)} %param.14) | copy-start | bytes 28
  25.6 41.0 %all-to-all-start = ((f32[128,25,128]{2,1,0:T(8,128)}), f32[128,25,128]{2,1,0:T(8,128)S(1)}, u32[]{:S(2)}, u32[]{:S(2)}) async-start(f32[128,25,128]{2,1,0:T(8,128)} %pad_maximum_fusion.1), calls=%async_computation | async-start | bytes 4194304 | tf_op jit(solution)/shard_map/all_to_all | solution.py:55
  41.3 9.3 %copy-start.3 = (s32[16,8]{0,1:T(8,128)S(1)}, s32[16,8]{0,1:T(8,128)}, u32[]{:S(2)}) copy-start(s32[16,8]{0,1:T(8,128)} %param.9) | copy-start | bytes 1540
  110.1 118.3 %all-to-all-start.1 = ((f32[16,129,512]{2,1,0:T(8,128)}), f32[16,129,512]{2,1,0:T(8,128)}, u32[]{:S(2)}, u32[]{:S(2)}) async-start(f32[16,129,512]{2,1,0:T(8,128)} %select_maximum_fusion), calls=%async_computation.1 | async-start | bytes 8912896 | tf_op jit(solution)/shard_map/all_to_all | solution.py:94
  114.6 113.3 %copy-start.1 = (f32[2,256,256]{2,1,0:T(8,128)S(1)}, f32[2,256,256]{2,1,0:T(8,128)}, u32[]{:S(2)}) copy-start(f32[2,256,256]{2,1,0:T(8,128)} %param.15) | copy-start | bytes 1572868
  117.2 63.6 %collective-permute-start = (f32[256,256]{1,0:T(8,128)S(1)}, f32[256,256]{1,0:T(8,128)S(1)}, u32[]{:S(2)}, u32[]{:S(2)}) collective-permute-start(f32[256,256]{1,0:T(8,128)S(1)} %dynamic-slice_select_fusion), channel_id=1, source_target_pairs={{0,1},{1,0},{2,3},{3,2},{4,5},{5,4},{6,7},{7,6},{8,9},{9,8},{10,11... | collective-permute-start | bytes 786440 | tf_op jit(solution)/shard_map/ppermute | solution.py:28
  181.8 8.0 %collective-permute-start.1 = (f32[256,256]{1,0:T(8,128)S(1)}, f32[256,256]{1,0:T(8,128)S(1)}, u32[]{:S(2)}, u32[]{:S(2)}) collective-permute-start(f32[256,256]{1,0:T(8,128)S(1)} %fusion.38), channel_id=1, source_target_pairs={{0,2},{1,3},{2,0},{3,1},{4,6},{5,7},{6,4},{7,5},{8,10},{9,11},{10,... | collective-permute-start | bytes 786440 | tf_op jit(solution)/shard_map/ppermute | solution.py:28
  189.8 7.8 %collective-permute-start.2 = (f32[256,256]{1,0:T(8,128)S(1)}, f32[256,256]{1,0:T(8,128)S(1)}, u32[]{:S(2)}, u32[]{:S(2)}) collective-permute-start(f32[256,256]{1,0:T(8,128)S(1)} %add.118), channel_id=1, source_target_pairs={{0,4},{1,5},{2,6},{3,7},{4,0},{5,1},{6,2},{7,3},{8,12},{9,13},{10,... | collective-permute-start | bytes 786440 | tf_op jit(solution)/shard_map/ppermute | solution.py:28
  197.7 8.7 %collective-permute-start.3 = (f32[256,256]{1,0:T(8,128)S(1)}, f32[256,256]{1,0:T(8,128)S(1)}, u32[]{:S(2)}, u32[]{:S(2)}) collective-permute-start(f32[256,256]{1,0:T(8,128)S(1)} %add.119), channel_id=1, source_target_pairs={{0,8},{1,9},{2,10},{3,11},{4,12},{5,13},{6,14},{7,15},{8,0},{9,1},... | collective-permute-start | bytes 786440 | tf_op jit(solution)/shard_map/ppermute | solution.py:28
  206.4 1.6 collective-permute-start.4
  208.0 9.8 %collective-permute-start.5 = (f32[256,256]{1,0:T(8,128)S(1)}, f32[256,256]{1,0:T(8,128)S(1)}, u32[]{:S(2)}, u32[]{:S(2)}) collective-permute-start(f32[256,256]{1,0:T(8,128)S(1)} %add.121), channel_id=1, source_target_pairs={{0,32},{1,33},{2,34},{3,35},{4,36},{5,37},{6,38},{7,39},{8,40},{9,... | collective-permute-start | bytes 786440 | tf_op jit(solution)/shard_map/ppermute | solution.py:28
  217.8 10.2 %collective-permute-start.6 = (f32[256,256]{1,0:T(8,128)S(1)}, f32[256,256]{1,0:T(8,128)S(1)}, u32[]{:S(2)}, u32[]{:S(2)}) collective-permute-start(f32[256,256]{1,0:T(8,128)S(1)} %add.122), channel_id=1, source_target_pairs={{0,64},{1,65},{2,66},{3,67},{4,68},{5,69},{6,70},{7,71},{8,72},{9,... | collective-permute-start | bytes 786440 | tf_op jit(solution)/shard_map/ppermute | solution.py:28
  230.5 13.1 %collective-permute-start.7 = (f32[128,512]{1,0:T(8,128)S(1)}, f32[128,512]{1,0:T(8,128)S(1)}, u32[]{:S(2)}, u32[]{:S(2)}) collective-permute-start(f32[128,512]{1,0:T(8,128)S(1)} %pad_maximum_fusion.2), channel_id=1, source_target_pairs={{0,0},{1,16},{2,32},{3,48},{4,64},{5,80},{6,96},{7,112},{8,1},{9,1... | collective-permute-start | bytes 786440 | tf_op jit(solution)/shard_map/ppermute | solution.py:115
  233.7 76.0 %all-to-all-start.2 = ((f32[16,128,512]{2,1,0:T(8,128)}), f32[16,128,512]{2,1,0:T(8,128)}, u32[]{:S(2)}, u32[]{:S(2)}) async-start(f32[16,128,512]{2,1,0:T(8,128)} %broadcast_in_dim.45), calls=%async_computation.2 | async-start | bytes 8388608 | tf_op jit(solution)/shard_map/all_to_all | solution.py:21
  243.5 66.2 %all-gather.2.cloned.1.call-start = ((), (), s32[]{:S(2)}) async-start(), calls=%async_computation.3 | async-start | bytes 2359296 | tf_op jit(solution)/shard_map/all_gather | solution.py:116
  243.6 0.7 copy-start.2
  309.8 2.3 copy-start
Sparse Core Ops, SparseCore 0:
  246.0 59.7 all-gather.1

commit v9 on v6

--- a/solution.py
+++ b/solution.py
@@ -57,7 +57,7 @@
         .at[got_place.astype(jnp.int32)]
         .add(got_values)
     )
-    return flat.reshape(rows_local, cols_local)
+    return flat.reshape(rows_local, cols_local), flat.reshape(rows_local, blocks_local, 128)
 
 
 def body(front, fill_blocks, seg_values, seg_row, seg_block, seg_live, panel_start, panel_inverse):
@@ -70,11 +70,14 @@
     r = lax.axis_index("prow")
     c = lax.axis_index("pcol")
 
-    assembled = assemble(front, seg_values, seg_row, seg_block, seg_live, n_prow, n_pcol)
+    assembled, by_block = assemble(front, seg_values, seg_row, seg_block, seg_live, n_prow, n_pcol)
 
     owner = [panel_start[k] // blocks_local for k in range(PANELS)]
     offset = [panel_start[k] % blocks_local * 128 for k in range(PANELS)]
-    cols = [lax.dynamic_slice_in_dim(assembled, offset[k], pw, 1) for k in range(PANELS)]
+    cols = [
+        lax.dynamic_slice_in_dim(by_block, offset[k] // 128, pw // 128, 1).reshape(rows_local, pw)
+        for k in range(PANELS)
+    ]
 
     start2 = panel_start[1] * 128
     src_row = start2 // rows_local

time: 337 us -> 342 us (1.015)
  local copies, waits for them, and re-layouts: 45.1 us -> 59.2 us
  waiting for transfers between devices: 180 us -> 167 us
  starting transfers between devices: 41.8 us -> 48.5 us
    all_to_all x1, waiting for transfers between devices: 64.8 us -> 54.9 us  [gather_rows(): got = lax.all_to_all(spread, axis, 0, 0, tiled=False)]
    concatenate x0 -> x2, local copies, waits for them, and re-layouts: none -> 6.66 us  [body(): jnp.concatenate(cols, axis=1).reshape(n_pcol, piece_rows, PANELS * pw)]
    dynamic_slice x1, local copies, waits for them, and re-layouts: 2.51 us -> 8.23 us  [body(): lax.dynamic_slice_in_dim(by_block, offset[k] // 128, pw // 128, 1)]
    ppermute x7, starting transfers between devices: 7.79 us -> 12.7 us  [spread(): x = x + lax.ppermute(x, ('prow', 'pcol'), pairs)]
  transfers between devices with their start and end apart: 13 -> 13, of which waited for: 10 -> 10; matrix products, arithmetic and copies ran while one was open for 7% -> 9% of each run, Pallas kernels for 0% -> 0%
where the time goes in v9:
time: 342 us; the launch traced here: 338 us
  waiting for transfers between devices  167 us (49%)
  local copies, waits for them, and re-layouts  59.2 us (17%)
  starting transfers between devices  48.5 us (14%)
  other arithmetic  29.2 us (9%)
  between operations  20.4 us (6%)
  matrix products  13.7 us (4%)
    ppermute x7, waiting for transfers between devices, spread(): x = x + lax.ppermute(x, ('prow', 'pcol'), pairs)  100 us
    all_to_all x1, waiting for transfers between devices, gather_rows(): got = lax.all_to_all(spread, axis, 0, 0, tiled=False)  54.9 us
    scatter-add x1, other arithmetic, assemble(): flat = front.reshape(rows_local * blocks_local, 128).at[got_place.astype(...  22 us
    ppermute x7, starting transfers between devices, spread(): x = x + lax.ppermute(x, ('prow', 'pcol'), pairs)  12.7 us
    dot_general x1, matrix products, body(): jnp.dot(left_rows, left_cols.T, precision=lax.Precision.HIGH, preferred_e...  12.4 us
    all_to_all x1, starting transfers between devices, assemble(): got_place = lax.all_to_all(send_place, ('prow', 'pcol'), 0, 0, tiled=True)  11.2 us
    all_to_all x1, waiting for transfers between devices, assemble(): got_values = lax.all_to_all(send_values, ('prow', 'pcol'), 0, 0, tiled=True)  10.1 us
    reshape x1, local copies, waits for them, and re-layouts, assemble(): flat.reshape(rows_local, cols_local)  9.28 us
  transfers between devices with their start and end apart: 13, of which 10 were waited for; matrix products, arithmetic and copies ran while one was open for 9% of the time, Pallas kernels for 0%

profile of v9, /device:TPU:0, one launch (start us, length us, event | category | flops | bytes accessed | tf_op | source)
XLA Modules:
  0.0 338.4 jit_solution(3406067284405617833)
XLA Ops:
  6.5 0.7 fusion.24
  7.3 0.1 copy.15
  7.4 0.3 fusion.4
  7.8 0.1 broadcast_add_fusion
  7.8 0.0 copy-start.5
  7.9 0.3 copy.16
  8.2 0.6 fusion.3
  9.5 8.1 %scatter_custom_fusion = f32[3072]{0:T(1024)S(1)} fusion(s32[2048]{0:T(1024)S(1)} %compare_select_fusion.1, f32[2048]{0:T(1024)S(1)} %get-tuple-element.9, f32[]{:T(128)} %constant.123.clone.1), kind=kCustom, calls=%fused_computation.60 | custom fusion | bytes 12292 | tf_op jit(solution)/shard_map/scatter | solution.py:51
  17.6 0.7 all_to_all.20
  18.3 11.2 %all-to-all-start = ((f32[128,24,1]{1,2,0:T(1,128)}), f32[128,24,1]{1,2,0:T(1,128)S(1)}, u32[]{:S(2)}, u32[]{:S(2)}) async-start(f32[128,24,1]{1,2,0:T(1,128)} %bitcast.5), calls=%async_computation | async-start | bytes 131072 | tf_op jit(solution)/shard_map/all_to_all | solution.py:54
  29.5 7.2 %scatter_custom_fusion.1 = f32[3072,128]{1,0:T(8,128)} fusion(s32[2048]{0:T(1024)S(1)} %compare_select_fusion.1, f32[2048,128]{1,0:T(8,128)} %param.10, f32[]{:T(128)} %constant.123.clone.1), kind=kCustom, calls=%fused_computation.17 | custom fusion | bytes 1573376 | tf_op jit(solution)/shard_map/scatter | solution.py:48
  36.6 2.3 all-to-all-done
  38.9 7.5 %all-to-all-start.1 = ((f32[128,24,128]{2,1,0:T(8,128)}), f32[128,24,128]{2,1,0:T(8,128)S(1)}, u32[]{:S(2)}, u32[]{:S(2)}) async-start(f32[128,24,128]{2,1,0:T(8,128)} %bitcast.7), calls=%async_computation.1 | async-start | bytes 3145728 | tf_op jit(solution)/shard_map/all_to_all | solution.py:53
  46.4 0.6 fusion.31
  51.1 0.0 copy-start.4
  51.1 9.3 %reshape.73 = f32[16384,128]{1,0:T(8,128)} reshape(f32[2048,1024]{1,0:T(8,128)} %param.8) | data formatting | bytes 16777216 | tf_op jit(solution)/shard_map/reshape | solution.py:56
  60.3 0.0 copy-done.4
  60.4 0.1 copy.18
  60.4 0.2 convert_reduce_fusion
  60.6 0.1 convert_element_type.32
  60.8 10.1 %all-to-all-done.1 = f32[128,24,128]{2,1,0:T(8,128)S(1)} async-done(((f32[128,24,128]{2,1,0:T(8,128)}), f32[128,24,128]{2,1,0:T(8,128)S(1)}, u32[]{:S(2)}, u32[]{:S(2)}) %all-to-all-start.1) | async-done | bytes 1572896 | tf_op jit(solution)/shard_map/all_to_all | solution.py:53
  70.9 22.0 %scatter_fusion = f32[16384,128]{1,0:T(8,128)} fusion(f32[16384,128]{1,0:T(8,128)} %reshape.73, s32[3072]{0:T(1024)S(1)} %bitcast.59, f32[3072,128]{1,0:T(8,128)S(1)} %bitcast.53), kind=kCustom, calls=%fused_computation.2 | custom fusion | flops 393216 | bytes 4730880 | tf_op jit(solution)/shard_map/scatter-add | solution.py:58
  92.8 8.2 %constant_dynamic-slice_fusion.2 = (f32[2048,2,128]{2,1,0:T(2,128)S(1)}, f32[2048,2,128]{2,1,0:T(2,128)}) fusion(f32[2048,8,128]{2,1,0:T(8,128)} %bitcast.50, s32[]{:T(128)S(6)} %select_n.102, s32[]{:T(128)S(6)} %select_n.105), kind=kLoop, calls=%fused_computation.66 | loop fusion | bytes 8388616 | tf_op jit(solution)/shard_map/dynamic_slice | solution.py:78
  101.1 2.8 concatenate.14
  103.8 3.9 %concatenate.15 = f32[16,128,256]{2,1,0:T(8,128)} reshape(f32[2048,2,128]{2,1,0:T(2,128)} %get-tuple-element.6) | data formatting | bytes 4194304 | tf_op jit(solution)/shard_map/concatenate | solution.py:92
  107.7 0.1 broadcast_in_dim.42
  107.8 4.9 %select_maximum_fusion = f32[16,129,512]{2,1,0:T(8,128)} fusion(f32[16,1,256]{2,1,0:T(1,128)S(1)} %bitcast.58, f32[16,128,256]{2,1,0:T(8,128)} %concatenate.15, f32[16,128,256]{2,1,0:T(8,128)} %concatenate.14), kind=kLoop, calls=%fused_computation.5 | loop fusion | flops 4227072 | bytes 8437760 | tf_op jit(solution)/shard_map/concatenate | solution.py:93
  112.7 7.3 %all-to-all-start.2 = ((f32[16,129,512]{2,1,0:T(8,128)}), f32[16,129,512]{2,1,0:T(8,128)}, u32[]{:S(2)}, u32[]{:S(2)}) async-start(f32[16,129,512]{2,1,0:T(8,128)} %select_maximum_fusion), calls=%async_computation.2 | async-start | bytes 8912896 | tf_op jit(solution)/shard_map/all_to_all | solution.py:94
  121.4 0.0 copy-start.2
  121.4 0.1 copy.24
  121.6 2.7 collective-permute-start
  124.2 67.3 %collective-permute-done = f32[256,256]{1,0:T(8,128)S(1)} collective-permute-done((f32[256,256]{1,0:T(8,128)S(1)}, f32[256,256]{1,0:T(8,128)S(1)}, u32[]{:S(2)}, u32[]{:S(2)}) %collective-permute-start) | collective-permute-done | bytes 262176 | tf_op jit(solution)/shard_map/ppermute | solution.py:28
  191.6 0.1 collective-permute-start.1
  191.7 8.3 %collective-permute-done.1 = f32[256,256]{1,0:T(8,128)S(1)} collective-permute-done((f32[256,256]{1,0:T(8,128)S(1)}, f32[256,256]{1,0:T(8,128)S(1)}, u32[]{:S(2)}, u32[]{:S(2)}) %collective-permute-start.1) | collective-permute-done | bytes 262176 | tf_op jit(solution)/shard_map/ppermute | solution.py:28
  200.0 0.8 collective-permute-start.2
  200.8 5.6 %collective-permute-done.2 = f32[256,256]{1,0:T(8,128)S(1)} collective-permute-done((f32[256,256]{1,0:T(8,128)S(1)}, f32[256,256]{1,0:T(8,128)S(1)}, u32[]{:S(2)}, u32[]{:S(2)}) %collective-permute-start.2) | collective-permute-done | bytes 262176 | tf_op jit(solution)/shard_map/ppermute | solution.py:28
  206.5 4.0 %collective-permute-start.3 = (f32[256,256]{1,0:T(8,128)S(1)}, f32[256,256]{1,0:T(8,128)S(1)}, u32[]{:S(2)}, u32[]{:S(2)}) collective-permute-start(f32[256,256]{1,0:T(8,128)S(1)} %add.113), channel_id=1, source_target_pairs={{0,8},{1,9},{2,10},{3,11},{4,12},{5,13},{6,14},{7,15},{8,0},{9,1},... | collective-permute-start | bytes 786440 | tf_op jit(solution)/shard_map/ppermute | solution.py:28
  210.5 4.4 %collective-permute-done.3 = f32[256,256]{1,0:T(8,128)S(1)} collective-permute-done((f32[256,256]{1,0:T(8,128)S(1)}, f32[256,256]{1,0:T(8,128)S(1)}, u32[]{:S(2)}, u32[]{:S(2)}) %collective-permute-start.3) | collective-permute-done | bytes 262176 | tf_op jit(solution)/shard_map/ppermute | solution.py:28
  214.8 0.1 collective-permute-start.4
  214.9 1.5 collective-permute-done.4
  216.5 0.5 collective-permute-start.5
  217.0 8.0 %collective-permute-done.5 = f32[256,256]{1,0:T(8,128)S(1)} collective-permute-done((f32[256,256]{1,0:T(8,128)S(1)}, f32[256,256]{1,0:T(8,128)S(1)}, u32[]{:S(2)}, u32[]{:S(2)}) %collective-permute-start.5) | collective-permute-done | bytes 262176 | tf_op jit(solution)/shard_map/ppermute | solution.py:28
  225.0 4.6 %collective-permute-start.6 = (f32[256,256]{1,0:T(8,128)S(1)}, f32[256,256]{1,0:T(8,128)S(1)}, u32[]{:S(2)}, u32[]{:S(2)}) collective-permute-start(f32[256,256]{1,0:T(8,128)S(1)} %add.116), channel_id=1, source_target_pairs={{0,64},{1,65},{2,66},{3,67},{4,68},{5,69},{6,70},{7,71},{8,72},{9,... | collective-permute-start | bytes 786440 | tf_op jit(solution)/shard_map/ppermute | solution.py:28
  230.3 5.0 %collective-permute-done.6 = f32[256,256]{1,0:T(8,128)S(1)} collective-permute-done((f32[256,256]{1,0:T(8,128)S(1)}, f32[256,256]{1,0:T(8,128)S(1)}, u32[]{:S(2)}, u32[]{:S(2)}) %collective-permute-start.6) | collective-permute-done | bytes 262176 | tf_op jit(solution)/shard_map/ppermute | solution.py:28
  235.4 0.4 fusion.11
  235.7 0.0 all-to-all-done.2
  235.8 1.1 dynamic-slice_bitcast_fusion
  236.8 0.3 fusion.13
  237.1 0.4 fusion.1
  237.6 0.3 fusion.9
  237.9 0.7 collective-permute-start.7
  238.6 2.5 broadcast_in_dim.45
  241.0 9.1 %all-to-all-start.3 = ((f32[16,128,512]{2,1,0:T(8,128)}), f32[16,128,512]{2,1,0:T(8,128)}, u32[]{:S(2)}, u32[]{:S(2)}) async-start(f32[16,128,512]{2,1,0:T(8,128)} %broadcast_in_dim.45), calls=%async_computation.3 | async-start | bytes 8388608 | tf_op jit(solution)/shard_map/all_to_all | solution.py:21
  250.1 0.0 all-gather.2.cloned.1.call-start
  250.1 0.0 collective-permute-done.7
  250.2 0.7 copy-done.3
  250.8 0.0 all-gather.2.cloned.1.call-update
  250.9 0.1 copy.19
  250.9 9.3 %reshape.75 = f32[2048,1024]{1,0:T(8,128)} reshape(f32[16384,128]{1,0:T(8,128)} %scatter_fusion) | data formatting | bytes 16777216 | tf_op jit(solution)/shard_map/reshape | solution.py:60
  260.2 54.9 %all-to-all-done.3 = f32[16,128,512]{2,1,0:T(8,128)} async-done(((f32[16,128,512]{2,1,0:T(8,128)}), f32[16,128,512]{2,1,0:T(8,128)}, u32[]{:S(2)}, u32[]{:S(2)}) %all-to-all-start.3) | async-done | bytes 4194336 | tf_op jit(solution)/shard_map/all_to_all | solution.py:21
  315.2 0.1 broadcast_in_dim.46
  315.2 2.3 broadcast_in_dim.47
  317.6 1.6 copy-done
  319.2 12.4 %fusion = f32[2048,1024]{1,0:T(8,128)} fusion(f32[2048,1024]{1,0:T(8,128)S(1)} %copy-done, f32[256,8,8,128]{3,2,1,0:T(8,128)S(1)} %bitcast.51, f32[2048,512]{1,0:T(8,128)} %bitcast.18, f32[1024,512]{1,0:T(8,128)S(1)} %copy-done.1), kind=kOutput, calls=%fused_computation.4 | convolution fusion | flops 6446645248 | bytes 31457280 | tf_op jit(solution)/shard_map/dot_general | solution.py:118
  (23 shorter events, 0.3 us)
Async XLA Ops:
  7.8 38.6 %copy-start.5 = (s32[2]{0:T(128)S(1)}, s32[2]{0:T(128)}, u32[]{:S(2)}) copy-start(s32[2]{0:T(128)} %param.14) | copy-start | bytes 28
  18.3 20.6 %all-to-all-start = ((f32[128,24,1]{1,2,0:T(1,128)}), f32[128,24,1]{1,2,0:T(1,128)S(1)}, u32[]{:S(2)}, u32[]{:S(2)}) async-start(f32[128,24,1]{1,2,0:T(1,128)} %bitcast.5), calls=%async_computation | async-start | bytes 131072 | tf_op jit(solution)/shard_map/all_to_all | solution.py:54
  38.9 32.0 %all-to-all-start.1 = ((f32[128,24,128]{2,1,0:T(8,128)}), f32[128,24,128]{2,1,0:T(8,128)S(1)}, u32[]{:S(2)}, u32[]{:S(2)}) async-start(f32[128,24,128]{2,1,0:T(8,128)} %bitcast.7), calls=%async_computation.1 | async-start | bytes 3145728 | tf_op jit(solution)/shard_map/all_to_all | solution.py:53
  51.1 9.3 %copy-start.4 = (s32[16,8]{0,1:T(8,128)S(1)}, s32[16,8]{0,1:T(8,128)}, u32[]{:S(2)}) copy-start(s32[16,8]{0,1:T(8,128)} %param.9) | copy-start | bytes 1540
  112.7 123.0 %all-to-all-start.2 = ((f32[16,129,512]{2,1,0:T(8,128)}), f32[16,129,512]{2,1,0:T(8,128)}, u32[]{:S(2)}, u32[]{:S(2)}) async-start(f32[16,129,512]{2,1,0:T(8,128)} %select_maximum_fusion), calls=%async_computation.2 | async-start | bytes 8912896 | tf_op jit(solution)/shard_map/all_to_all | solution.py:94
  121.4 114.0 %copy-start.2 = (f32[2,256,256]{2,1,0:T(8,128)S(1)}, f32[2,256,256]{2,1,0:T(8,128)}, u32[]{:S(2)}) copy-start(f32[2,256,256]{2,1,0:T(8,128)} %param.15) | copy-start | bytes 1572868
  121.6 70.0 %collective-permute-start = (f32[256,256]{1,0:T(8,128)S(1)}, f32[256,256]{1,0:T(8,128)S(1)}, u32[]{:S(2)}, u32[]{:S(2)}) collective-permute-start(f32[256,256]{1,0:T(8,128)S(1)} %dynamic-slice_select_fusion), channel_id=1, source_target_pairs={{0,1},{1,0},{2,3},{3,2},{4,5},{5,4},{6,7},{7,6},{8,9},{9,8},{10,11... | collective-permute-start | bytes 786440 | tf_op jit(solution)/shard_map/ppermute | solution.py:28
  191.6 8.4 %collective-permute-start.1 = (f32[256,256]{1,0:T(8,128)S(1)}, f32[256,256]{1,0:T(8,128)S(1)}, u32[]{:S(2)}, u32[]{:S(2)}) collective-permute-start(f32[256,256]{1,0:T(8,128)S(1)} %fusion.37), channel_id=1, source_target_pairs={{0,2},{1,3},{2,0},{3,1},{4,6},{5,7},{6,4},{7,5},{8,10},{9,11},{10,... | collective-permute-start | bytes 786440 | tf_op jit(solution)/shard_map/ppermute | solution.py:28
  200.0 6.5 %collective-permute-start.2 = (f32[256,256]{1,0:T(8,128)S(1)}, f32[256,256]{1,0:T(8,128)S(1)}, u32[]{:S(2)}, u32[]{:S(2)}) collective-permute-start(f32[256,256]{1,0:T(8,128)S(1)} %add.112), channel_id=1, source_target_pairs={{0,4},{1,5},{2,6},{3,7},{4,0},{5,1},{6,2},{7,3},{8,12},{9,13},{10,... | collective-permute-start | bytes 786440 | tf_op jit(solution)/shard_map/ppermute | solution.py:28
  206.5 8.3 %collective-permute-start.3 = (f32[256,256]{1,0:T(8,128)S(1)}, f32[256,256]{1,0:T(8,128)S(1)}, u32[]{:S(2)}, u32[]{:S(2)}) collective-permute-start(f32[256,256]{1,0:T(8,128)S(1)} %add.113), channel_id=1, source_target_pairs={{0,8},{1,9},{2,10},{3,11},{4,12},{5,13},{6,14},{7,15},{8,0},{9,1},... | collective-permute-start | bytes 786440 | tf_op jit(solution)/shard_map/ppermute | solution.py:28
  214.8 1.6 collective-permute-start.4
  216.5 8.4 %collective-permute-start.5 = (f32[256,256]{1,0:T(8,128)S(1)}, f32[256,256]{1,0:T(8,128)S(1)}, u32[]{:S(2)}, u32[]{:S(2)}) collective-permute-start(f32[256,256]{1,0:T(8,128)S(1)} %add.115), channel_id=1, source_target_pairs={{0,32},{1,33},{2,34},{3,35},{4,36},{5,37},{6,38},{7,39},{8,40},{9,... | collective-permute-start | bytes 786440 | tf_op jit(solution)/shard_map/ppermute | solution.py:28
  225.0 10.4 %collective-permute-start.6 = (f32[256,256]{1,0:T(8,128)S(1)}, f32[256,256]{1,0:T(8,128)S(1)}, u32[]{:S(2)}, u32[]{:S(2)}) collective-permute-start(f32[256,256]{1,0:T(8,128)S(1)} %add.116), channel_id=1, source_target_pairs={{0,64},{1,65},{2,66},{3,67},{4,68},{5,69},{6,70},{7,71},{8,72},{9,... | collective-permute-start | bytes 786440 | tf_op jit(solution)/shard_map/ppermute | solution.py:28
  237.9 12.3 %collective-permute-start.7 = (f32[128,512]{1,0:T(8,128)S(1)}, f32[128,512]{1,0:T(8,128)S(1)}, u32[]{:S(2)}, u32[]{:S(2)}) collective-permute-start(f32[128,512]{1,0:T(8,128)S(1)} %pad_maximum_fusion), channel_id=1, source_target_pairs={{0,0},{1,16},{2,32},{3,48},{4,64},{5,80},{6,96},{7,112},{8,1},{9,1... | collective-permute-start | bytes 786440 | tf_op jit(solution)/shard_map/ppermute | solution.py:115
  241.0 74.1 %all-to-all-start.3 = ((f32[16,128,512]{2,1,0:T(8,128)}), f32[16,128,512]{2,1,0:T(8,128)}, u32[]{:S(2)}, u32[]{:S(2)}) async-start(f32[16,128,512]{2,1,0:T(8,128)} %broadcast_in_dim.45), calls=%async_computation.3 | async-start | bytes 8388608 | tf_op jit(solution)/shard_map/all_to_all | solution.py:21
  250.1 65.1 %all-gather.2.cloned.1.call-start = ((), (), s32[]{:S(2)}) async-start(), calls=%async_computation.4 | async-start | bytes 2359296 | tf_op jit(solution)/shard_map/all_gather | solution.py:116
  250.1 0.7 copy-start.3
  315.2 2.4 copy-start.1
  315.2 4.0 %copy-start = (f32[2048,1024]{1,0:T(8,128)S(1)}, f32[2048,1024]{1,0:T(8,128)}, u32[]{:S(2)}) copy-start(f32[2048,1024]{1,0:T(8,128)} %reshape.75) | copy-start | bytes 25165828
Sparse Core Ops, SparseCore 0:
  252.6 61.8 all-gather.1

commit v10 on v6

--- a/solution.py
+++ b/solution.py
@@ -4,7 +4,7 @@
 from jax.sharding import PartitionSpec as P
 
 PANELS = 2
-HIGHEST = lax.Precision.HIGHEST
+HIGHEST = lax.Precision.HIGH
 
 
 def dot(a, b):

time: 337 us -> 342 us (1.015)
  no operation moved by 1% of the time
where the time goes in v10:
time: 342 us; the launch traced here: 337 us
  waiting for transfers between devices  180 us (53%)
  local copies, waits for them, and re-layouts  45.1 us (13%)
  starting transfers between devices  44.2 us (13%)
  other arithmetic  31.4 us (9%)
  between operations  20 us (6%)
  matrix products  15.6 us (5%)
    ppermute x7, waiting for transfers between devices, spread(): x = x + lax.ppermute(x, ('prow', 'pcol'), pairs)  104 us
    all_to_all x1, waiting for transfers between devices, gather_rows(): got = lax.all_to_all(spread, axis, 0, 0, tiled=False)  63.3 us
    scatter-add x1, other arithmetic, assemble(): flat = front.reshape(rows_local * blocks_local, 128).at[got_place.astype(...  23.7 us
    dot_general x1, matrix products, body(): jnp.dot(left_rows, left_cols.T, precision=lax.Precision.HIGH, preferred_e...  14.6 us
    all_to_all x1, starting transfers between devices, assemble(): got_place = lax.all_to_all(send_place, ('prow', 'pcol'), 0, 0, tiled=True)  11.2 us
    all_to_all x1, waiting for transfers between devices, assemble(): got_values = lax.all_to_all(send_values, ('prow', 'pcol'), 0, 0, tiled=True)  10.5 us
    ppermute x7, starting transfers between devices, spread(): x = x + lax.ppermute(x, ('prow', 'pcol'), pairs)  10 us
    reshape x1, local copies, waits for them, and re-layouts, assemble(): return flat.reshape(rows_local, cols_local)  9.28 us
  transfers between devices with their start and end apart: 13, of which 10 were waited for; matrix products, arithmetic and copies ran while one was open for 7% of the time, Pallas kernels for 0%

profile of v10, /device:TPU:0, one launch (start us, length us, event | category | flops | bytes accessed | tf_op | source)
XLA Modules:
  0.0 336.5 jit_solution(16804006270596208084)
XLA Ops:
  6.5 0.7 fusion.24
  7.3 0.1 copy.15
  7.4 0.3 fusion.4
  7.8 0.1 broadcast_add_fusion
  7.8 0.0 copy-start.4
  7.9 0.3 copy.16
  8.2 0.6 fusion.3
  9.5 8.1 %scatter_custom_fusion = f32[3072]{0:T(1024)S(1)} fusion(s32[2048]{0:T(1024)S(1)} %compare_select_fusion.1, f32[2048]{0:T(1024)S(1)} %get-tuple-element.9, f32[]{:T(128)} %constant.125.clone.1), kind=kCustom, calls=%fused_computation.60 | custom fusion | bytes 12292 | tf_op jit(solution)/shard_map/scatter | solution.py:51
  17.6 0.7 all_to_all.20
  18.3 11.2 %all-to-all-start = ((f32[128,24,1]{1,2,0:T(1,128)}), f32[128,24,1]{1,2,0:T(1,128)S(1)}, u32[]{:S(2)}, u32[]{:S(2)}) async-start(f32[128,24,1]{1,2,0:T(1,128)} %bitcast.5), calls=%async_computation | async-start | bytes 131072 | tf_op jit(solution)/shard_map/all_to_all | solution.py:54
  29.5 7.2 %scatter_custom_fusion.1 = f32[3072,128]{1,0:T(8,128)} fusion(s32[2048]{0:T(1024)S(1)} %compare_select_fusion.1, f32[2048,128]{1,0:T(8,128)} %param.10, f32[]{:T(128)} %constant.125.clone.1), kind=kCustom, calls=%fused_computation.17 | custom fusion | bytes 1573376 | tf_op jit(solution)/shard_map/scatter | solution.py:48
  36.6 2.3 all-to-all-done
  38.9 7.5 %all-to-all-start.1 = ((f32[128,24,128]{2,1,0:T(8,128)}), f32[128,24,128]{2,1,0:T(8,128)S(1)}, u32[]{:S(2)}, u32[]{:S(2)}) async-start(f32[128,24,128]{2,1,0:T(8,128)} %bitcast.7), calls=%async_computation.1 | async-start | bytes 3145728 | tf_op jit(solution)/shard_map/all_to_all | solution.py:53
  46.4 0.0 copy-done.4
  46.4 0.6 fusion.31
  50.7 0.0 copy-start.3
  50.7 9.3 %reshape.64 = f32[16384,128]{1,0:T(8,128)} reshape(f32[2048,1024]{1,0:T(8,128)} %param.8) | data formatting | bytes 16777216 | tf_op jit(solution)/shard_map/reshape | solution.py:56
  59.9 0.1 copy.18
  60.0 0.2 convert_reduce_fusion
  60.2 0.1 convert_element_type.32
  60.4 10.5 %all-to-all-done.1 = f32[128,24,128]{2,1,0:T(8,128)S(1)} async-done(((f32[128,24,128]{2,1,0:T(8,128)}), f32[128,24,128]{2,1,0:T(8,128)S(1)}, u32[]{:S(2)}, u32[]{:S(2)}) %all-to-all-start.1) | async-done | bytes 1572896 | tf_op jit(solution)/shard_map/all_to_all | solution.py:53
  70.9 23.7 %scatter_fusion = f32[16384,128]{1,0:T(8,128)} fusion(f32[16384,128]{1,0:T(8,128)} %reshape.64, s32[3072]{0:T(1024)S(1)} %bitcast.52, f32[3072,128]{1,0:T(8,128)S(1)} %bitcast.48), kind=kCustom, calls=%fused_computation.2 | custom fusion | flops 393216 | bytes 4730880 | tf_op jit(solution)/shard_map/scatter-add | solution.py:58
  94.6 9.3 %reshape.66 = f32[2048,1024]{1,0:T(8,128)} reshape(f32[16384,128]{1,0:T(8,128)} %scatter_fusion) | data formatting | bytes 16777216 | tf_op jit(solution)/shard_map/reshape | solution.py:60
  103.8 2.5 constant_dynamic-slice_fusion.2
  106.4 0.6 pad_maximum_fusion
  107.0 0.1 broadcast_in_dim.42
  107.1 2.6 select_maximum_fusion
  109.7 5.8 %all-to-all-start.2 = ((f32[16,129,512]{2,1,0:T(8,128)}), f32[16,129,512]{2,1,0:T(8,128)}, u32[]{:S(2)}, u32[]{:S(2)}) async-start(f32[16,129,512]{2,1,0:T(8,128)} %select_maximum_fusion), calls=%async_computation.2 | async-start | bytes 8912896 | tf_op jit(solution)/shard_map/all_to_all | solution.py:91
  115.6 0.0 copy-start.1
  116.9 1.1 dynamic-slice_select_fusion
  118.0 2.0 collective-permute-start
  120.0 68.6 %collective-permute-done = f32[256,256]{1,0:T(8,128)S(1)} collective-permute-done((f32[256,256]{1,0:T(8,128)S(1)}, f32[256,256]{1,0:T(8,128)S(1)}, u32[]{:S(2)}, u32[]{:S(2)}) %collective-permute-start) | collective-permute-done | bytes 262176 | tf_op jit(solution)/shard_map/ppermute | solution.py:28
  188.6 1.1 fusion.37
  189.8 0.5 collective-permute-start.1
  190.2 9.2 %collective-permute-done.1 = f32[256,256]{1,0:T(8,128)S(1)} collective-permute-done((f32[256,256]{1,0:T(8,128)S(1)}, f32[256,256]{1,0:T(8,128)S(1)}, u32[]{:S(2)}, u32[]{:S(2)}) %collective-permute-start.1) | collective-permute-done | bytes 262176 | tf_op jit(solution)/shard_map/ppermute | solution.py:28
  199.4 0.7 collective-permute-start.2
  200.1 6.6 %collective-permute-done.2 = f32[256,256]{1,0:T(8,128)S(1)} collective-permute-done((f32[256,256]{1,0:T(8,128)S(1)}, f32[256,256]{1,0:T(8,128)S(1)}, u32[]{:S(2)}, u32[]{:S(2)}) %collective-permute-start.2) | collective-permute-done | bytes 262176 | tf_op jit(solution)/shard_map/ppermute | solution.py:28
  206.8 3.0 collective-permute-start.3
  209.7 5.0 %collective-permute-done.3 = f32[256,256]{1,0:T(8,128)S(1)} collective-permute-done((f32[256,256]{1,0:T(8,128)S(1)}, f32[256,256]{1,0:T(8,128)S(1)}, u32[]{:S(2)}, u32[]{:S(2)}) %collective-permute-start.3) | collective-permute-done | bytes 262176 | tf_op jit(solution)/shard_map/ppermute | solution.py:28
  214.8 0.1 collective-permute-start.4
  214.8 1.5 collective-permute-done.4
  216.4 1.6 collective-permute-start.5
  218.0 7.0 %collective-permute-done.5 = f32[256,256]{1,0:T(8,128)S(1)} collective-permute-done((f32[256,256]{1,0:T(8,128)S(1)}, f32[256,256]{1,0:T(8,128)S(1)}, u32[]{:S(2)}, u32[]{:S(2)}) %collective-permute-start.5) | collective-permute-done | bytes 262176 | tf_op jit(solution)/shard_map/ppermute | solution.py:28
  225.1 2.2 collective-permute-start.6
  228.0 6.2 %collective-permute-done.6 = f32[256,256]{1,0:T(8,128)S(1)} collective-permute-done((f32[256,256]{1,0:T(8,128)S(1)}, f32[256,256]{1,0:T(8,128)S(1)}, u32[]{:S(2)}, u32[]{:S(2)}) %collective-permute-start.6) | collective-permute-done | bytes 262176 | tf_op jit(solution)/shard_map/ppermute | solution.py:28
  234.1 0.3 fusion.11
  234.4 0.0 all-to-all-done.2
  234.4 1.1 dynamic-slice_bitcast_fusion
  235.5 0.2 fusion.13
  235.8 0.3 fusion.1
  236.1 0.2 fusion.9
  236.3 0.7 collective-permute-start.7
  237.0 2.5 broadcast_in_dim.45
  239.6 9.0 %all-to-all-start.3 = ((f32[16,128,512]{2,1,0:T(8,128)}), f32[16,128,512]{2,1,0:T(8,128)}, u32[]{:S(2)}, u32[]{:S(2)}) async-start(f32[16,128,512]{2,1,0:T(8,128)} %broadcast_in_dim.45), calls=%async_computation.3 | async-start | bytes 8388608 | tf_op jit(solution)/shard_map/all_to_all | solution.py:21
  248.6 0.0 all-gather.2.cloned.1.call-start
  248.6 0.0 collective-permute-done.7
  248.6 0.7 copy-done.2
  249.3 0.0 all-gather.2.cloned.1.call-update
  249.3 0.1 copy.19
  249.4 63.3 %all-to-all-done.3 = f32[16,128,512]{2,1,0:T(8,128)} async-done(((f32[16,128,512]{2,1,0:T(8,128)}), f32[16,128,512]{2,1,0:T(8,128)}, u32[]{:S(2)}, u32[]{:S(2)}) %all-to-all-start.3) | async-done | bytes 4194336 | tf_op jit(solution)/shard_map/all_to_all | solution.py:21
  312.7 0.1 broadcast_in_dim.46
  312.8 0.0 copy-start
  312.8 2.3 broadcast_in_dim.47
  315.1 14.6 %fusion = f32[2048,1024]{1,0:T(8,128)} fusion(f32[2048,1024]{1,0:T(8,128)} %reshape.66, f32[256,8,8,128]{3,2,1,0:T(8,128)S(1)} %bitcast.46, f32[2048,512]{1,0:T(8,128)} %bitcast.18, f32[1024,512]{1,0:T(8,128)S(1)} %copy-done), kind=kOutput, calls=%fused_computation.4 | convolution fusion | flops 6446645248 | bytes 31457280 | tf_op jit(solution)/shard_map/dot_general | solution.py:115
  (19 shorter events, 0.3 us)
Async XLA Ops:
  7.8 38.6 %copy-start.4 = (s32[2]{0:T(128)S(1)}, s32[2]{0:T(128)}, u32[]{:S(2)}) copy-start(s32[2]{0:T(128)} %param.14) | copy-start | bytes 28
  18.3 20.6 %all-to-all-start = ((f32[128,24,1]{1,2,0:T(1,128)}), f32[128,24,1]{1,2,0:T(1,128)S(1)}, u32[]{:S(2)}, u32[]{:S(2)}) async-start(f32[128,24,1]{1,2,0:T(1,128)} %bitcast.5), calls=%async_computation | async-start | bytes 131072 | tf_op jit(solution)/shard_map/all_to_all | solution.py:54
  38.9 32.0 %all-to-all-start.1 = ((f32[128,24,128]{2,1,0:T(8,128)}), f32[128,24,128]{2,1,0:T(8,128)S(1)}, u32[]{:S(2)}, u32[]{:S(2)}) async-start(f32[128,24,128]{2,1,0:T(8,128)} %bitcast.7), calls=%async_computation.1 | async-start | bytes 3145728 | tf_op jit(solution)/shard_map/all_to_all | solution.py:53
  50.7 9.3 %copy-start.3 = (s32[16,8]{0,1:T(8,128)S(1)}, s32[16,8]{0,1:T(8,128)}, u32[]{:S(2)}) copy-start(s32[16,8]{0,1:T(8,128)} %param.9) | copy-start | bytes 1540
  109.7 124.7 %all-to-all-start.2 = ((f32[16,129,512]{2,1,0:T(8,128)}), f32[16,129,512]{2,1,0:T(8,128)}, u32[]{:S(2)}, u32[]{:S(2)}) async-start(f32[16,129,512]{2,1,0:T(8,128)} %select_maximum_fusion), calls=%async_computation.2 | async-start | bytes 8912896 | tf_op jit(solution)/shard_map/all_to_all | solution.py:91
  115.6 118.6 %copy-start.1 = (f32[2,256,256]{2,1,0:T(8,128)S(1)}, f32[2,256,256]{2,1,0:T(8,128)}, u32[]{:S(2)}) copy-start(f32[2,256,256]{2,1,0:T(8,128)} %param.15) | copy-start | bytes 1572868
  118.0 70.6 %collective-permute-start = (f32[256,256]{1,0:T(8,128)S(1)}, f32[256,256]{1,0:T(8,128)S(1)}, u32[]{:S(2)}, u32[]{:S(2)}) collective-permute-start(f32[256,256]{1,0:T(8,128)S(1)} %dynamic-slice_select_fusion), channel_id=1, source_target_pairs={{0,1},{1,0},{2,3},{3,2},{4,5},{5,4},{6,7},{7,6},{8,9},{9,8},{10,11... | collective-permute-start | bytes 786440 | tf_op jit(solution)/shard_map/ppermute | solution.py:28
  189.8 9.6 %collective-permute-start.1 = (f32[256,256]{1,0:T(8,128)S(1)}, f32[256,256]{1,0:T(8,128)S(1)}, u32[]{:S(2)}, u32[]{:S(2)}) collective-permute-start(f32[256,256]{1,0:T(8,128)S(1)} %fusion.37), channel_id=1, source_target_pairs={{0,2},{1,3},{2,0},{3,1},{4,6},{5,7},{6,4},{7,5},{8,10},{9,11},{10,... | collective-permute-start | bytes 786440 | tf_op jit(solution)/shard_map/ppermute | solution.py:28
  199.4 7.3 %collective-permute-start.2 = (f32[256,256]{1,0:T(8,128)S(1)}, f32[256,256]{1,0:T(8,128)S(1)}, u32[]{:S(2)}, u32[]{:S(2)}) collective-permute-start(f32[256,256]{1,0:T(8,128)S(1)} %add.116), channel_id=1, source_target_pairs={{0,4},{1,5},{2,6},{3,7},{4,0},{5,1},{6,2},{7,3},{8,12},{9,13},{10,... | collective-permute-start | bytes 786440 | tf_op jit(solution)/shard_map/ppermute | solution.py:28
  206.8 8.0 %collective-permute-start.3 = (f32[256,256]{1,0:T(8,128)S(1)}, f32[256,256]{1,0:T(8,128)S(1)}, u32[]{:S(2)}, u32[]{:S(2)}) collective-permute-start(f32[256,256]{1,0:T(8,128)S(1)} %add.117), channel_id=1, source_target_pairs={{0,8},{1,9},{2,10},{3,11},{4,12},{5,13},{6,14},{7,15},{8,0},{9,1},... | collective-permute-start | bytes 786440 | tf_op jit(solution)/shard_map/ppermute | solution.py:28
  214.8 1.6 collective-permute-start.4
  216.4 8.6 %collective-permute-start.5 = (f32[256,256]{1,0:T(8,128)S(1)}, f32[256,256]{1,0:T(8,128)S(1)}, u32[]{:S(2)}, u32[]{:S(2)}) collective-permute-start(f32[256,256]{1,0:T(8,128)S(1)} %add.119), channel_id=1, source_target_pairs={{0,32},{1,33},{2,34},{3,35},{4,36},{5,37},{6,38},{7,39},{8,40},{9,... | collective-permute-start | bytes 786440 | tf_op jit(solution)/shard_map/ppermute | solution.py:28
  225.1 9.1 %collective-permute-start.6 = (f32[256,256]{1,0:T(8,128)S(1)}, f32[256,256]{1,0:T(8,128)S(1)}, u32[]{:S(2)}, u32[]{:S(2)}) collective-permute-start(f32[256,256]{1,0:T(8,128)S(1)} %add.120), channel_id=1, source_target_pairs={{0,64},{1,65},{2,66},{3,67},{4,68},{5,69},{6,70},{7,71},{8,72},{9,... | collective-permute-start | bytes 786440 | tf_op jit(solution)/shard_map/ppermute | solution.py:28
  236.3 12.3 %collective-permute-start.7 = (f32[128,512]{1,0:T(8,128)S(1)}, f32[128,512]{1,0:T(8,128)S(1)}, u32[]{:S(2)}, u32[]{:S(2)}) collective-permute-start(f32[128,512]{1,0:T(8,128)S(1)} %pad_maximum_fusion.1), channel_id=1, source_target_pairs={{0,0},{1,16},{2,32},{3,48},{4,64},{5,80},{6,96},{7,112},{8,1},{9,1... | collective-permute-start | bytes 786440 | tf_op jit(solution)/shard_map/ppermute | solution.py:112
  239.6 73.1 %all-to-all-start.3 = ((f32[16,128,512]{2,1,0:T(8,128)}), f32[16,128,512]{2,1,0:T(8,128)}, u32[]{:S(2)}, u32[]{:S(2)}) async-start(f32[16,128,512]{2,1,0:T(8,128)} %broadcast_in_dim.45), calls=%async_computation.3 | async-start | bytes 8388608 | tf_op jit(solution)/shard_map/all_to_all | solution.py:21
  248.6 64.1 %all-gather.2.cloned.1.call-start = ((), (), s32[]{:S(2)}) async-start(), calls=%async_computation.4 | async-start | bytes 2359296 | tf_op jit(solution)/shard_map/all_gather | solution.py:113
  248.6 0.7 copy-start.2
  312.8 2.3 copy-start
Sparse Core Ops, SparseCore 0:
  251.1 60.9 all-gather.1

commit v11 on v6

--- a/solution.py
+++ b/solution.py
@@ -85,14 +85,12 @@
     mask_local = fill_blocks.astype(jnp.float32)
     mask_two = lax.dynamic_slice_in_dim(mask_local, offset[1] // 128, pw // 128, 1)
     mask_two = jnp.repeat(mask_two.reshape(n_pcol, piece_rows // 128, pw // 128), 128, axis=2)
-    mask_two = jnp.pad(mask_two.reshape(n_pcol, 1, pw), ((0, 0), (0, 0), (0, (PANELS - 1) * pw)))
+    recv_mask = lax.all_to_all(mask_two.reshape(n_pcol, 1, pw), "pcol", 0, 0, tiled=False)
     send = jnp.concatenate(cols, axis=1).reshape(n_pcol, piece_rows, PANELS * pw)
-    send = jnp.concatenate([send, mask_two], axis=1)
     recv = lax.all_to_all(send, "pcol", 0, 0, tiled=False)
-    piece0 = lax.dynamic_index_in_dim(recv, owner[0], 0, keepdims=False)[:piece_rows, :pw]
-    from_two = lax.dynamic_index_in_dim(recv, owner[1], 0, keepdims=False)
-    piece1 = from_two[:piece_rows, pw:]
-    m_piece = from_two[piece_rows:, :pw]
+    piece0 = lax.dynamic_index_in_dim(recv, owner[0], 0, keepdims=False)[:, :pw]
+    piece1 = lax.dynamic_index_in_dim(recv, owner[1], 0, keepdims=False)[:, pw:]
+    m_piece = lax.dynamic_index_in_dim(recv_mask, owner[1], 0, keepdims=False)
 
     left0 = dot(piece0, panel_inverse[0])
     left0_x = dot(x_cols, panel_inverse[0])

time: 337 us -> 342 us (1.015)
  starting transfers between devices: 41.8 us -> 50.6 us
  waiting for transfers between devices: 180 us -> 176 us
    ppermute x7, starting transfers between devices: 7.79 us -> 12.5 us  [spread(): x = x + lax.ppermute(x, ('prow', 'pcol'), pairs)]
    ppermute x7, waiting for transfers between devices: 102 us -> 97.5 us  [spread(): x = x + lax.ppermute(x, ('prow', 'pcol'), pairs)]
    all_to_all x0 -> x1, starting transfers between devices: none -> 3.5 us  [body(): lax.all_to_all(mask_two.reshape(n_pcol, 1, pw), 'pcol', 0, 0, tiled=False)]
  transfers between devices with their start and end apart: 13 -> 14, of which waited for: 10 -> 10; matrix products, arithmetic and copies ran while one was open for 7% -> 18% of each run, Pallas kernels for 0% -> 0%
where the time goes in v11:
time: 342 us; the launch traced here: 339 us
  waiting for transfers between devices  176 us (51%)
  starting transfers between devices  50.6 us (15%)
  local copies, waits for them, and re-layouts  45.7 us (13%)
  other arithmetic  30.6 us (9%)
  between operations  20.2 us (6%)
  matrix products  15.9 us (5%)
    ppermute x7, waiting for transfers between devices, spread(): x = x + lax.ppermute(x, ('prow', 'pcol'), pairs)  97.5 us
    all_to_all x1, waiting for transfers between devices, gather_rows(): got = lax.all_to_all(spread, axis, 0, 0, tiled=False)  65.7 us
    scatter-add x1, other arithmetic, assemble(): flat = front.reshape(rows_local * blocks_local, 128).at[got_place.astype(...  23.5 us
    dot_general x1, matrix products, body(): jnp.dot(left_rows, left_cols.T, precision=lax.Precision.HIGH, preferred_e...  14.6 us
    ppermute x7, starting transfers between devices, spread(): x = x + lax.ppermute(x, ('prow', 'pcol'), pairs)  12.5 us
    all_to_all x1, starting transfers between devices, assemble(): got_place = lax.all_to_all(send_place, ('prow', 'pcol'), 0, 0, tiled=True)  11.2 us
    all_to_all x1, waiting for transfers between devices, assemble(): got_values = lax.all_to_all(send_values, ('prow', 'pcol'), 0, 0, tiled=True)  10.3 us
    reshape x1, local copies, waits for them, and re-layouts, assemble(): return flat.reshape(rows_local, cols_local)  9.28 us
  transfers between devices with their start and end apart: 14, of which 10 were waited for; matrix products, arithmetic and copies ran while one was open for 18% of the time, Pallas kernels for 0%

profile of v11, /device:TPU:0, one launch (start us, length us, event | category | flops | bytes accessed | tf_op | source)
XLA Modules:
  0.0 338.9 jit_solution(8282750294408035833)
XLA Ops:
  6.5 0.7 fusion.24
  7.3 0.1 copy.15
  7.4 0.3 fusion.4
  7.8 0.1 broadcast_add_fusion
  7.8 0.0 copy-start.4
  7.9 0.3 copy.16
  8.2 0.6 fusion.3
  9.5 8.1 %scatter_custom_fusion = f32[3072]{0:T(1024)S(1)} fusion(s32[2048]{0:T(1024)S(1)} %compare_select_fusion.1, f32[2048]{0:T(1024)S(1)} %get-tuple-element.9, f32[]{:T(128)} %constant.128.clone.1), kind=kCustom, calls=%fused_computation.58 | custom fusion | bytes 12292 | tf_op jit(solution)/shard_map/scatter | solution.py:51
  17.6 0.7 all_to_all.23
  18.3 11.2 %all-to-all-start = ((f32[128,24,1]{1,2,0:T(1,128)}), f32[128,24,1]{1,2,0:T(1,128)S(1)}, u32[]{:S(2)}, u32[]{:S(2)}) async-start(f32[128,24,1]{1,2,0:T(1,128)} %bitcast.5), calls=%async_computation | async-start | bytes 131072 | tf_op jit(solution)/shard_map/all_to_all | solution.py:54
  29.5 7.2 %scatter_custom_fusion.1 = f32[3072,128]{1,0:T(8,128)} fusion(s32[2048]{0:T(1024)S(1)} %compare_select_fusion.1, f32[2048,128]{1,0:T(8,128)} %param.10, f32[]{:T(128)} %constant.128.clone.1), kind=kCustom, calls=%fused_computation.15 | custom fusion | bytes 1573376 | tf_op jit(solution)/shard_map/scatter | solution.py:48
  36.6 2.3 all-to-all-done
  38.9 7.5 %all-to-all-start.1 = ((f32[128,24,128]{2,1,0:T(8,128)}), f32[128,24,128]{2,1,0:T(8,128)S(1)}, u32[]{:S(2)}, u32[]{:S(2)}) async-start(f32[128,24,128]{2,1,0:T(8,128)} %bitcast.7), calls=%async_computation.1 | async-start | bytes 3145728 | tf_op jit(solution)/shard_map/all_to_all | solution.py:53
  46.4 0.0 copy-done.4
  46.4 0.6 fusion.31
  50.8 0.0 copy-start.3
  50.9 9.3 %reshape.65 = f32[16384,128]{1,0:T(8,128)} reshape(f32[2048,1024]{1,0:T(8,128)} %param.8) | data formatting | bytes 16777216 | tf_op jit(solution)/shard_map/reshape | solution.py:56
  60.1 0.1 copy.18
  60.2 0.2 convert_reduce_fusion
  60.4 0.1 convert_element_type.30
  60.5 10.3 %all-to-all-done.1 = f32[128,24,128]{2,1,0:T(8,128)S(1)} async-done(((f32[128,24,128]{2,1,0:T(8,128)}), f32[128,24,128]{2,1,0:T(8,128)S(1)}, u32[]{:S(2)}, u32[]{:S(2)}) %all-to-all-start.1) | async-done | bytes 1572896 | tf_op jit(solution)/shard_map/all_to_all | solution.py:53
  70.9 0.7 broadcast_in_dim.43
  71.6 3.5 %all-to-all-start.3 = ((f32[16,1,256]{2,1,0:T(1,128)}), f32[16,1,256]{2,1,0:T(1,128)S(1)}, u32[]{:S(2)}, u32[]{:S(2)}) async-start(f32[16,1,256]{2,1,0:T(1,128)} %bitcast.15), calls=%async_computation.3 | async-start | bytes 32768 | tf_op jit(solution)/shard_map/all_to_all | solution.py:88
  75.1 23.5 %scatter_fusion = f32[16384,128]{1,0:T(8,128)} fusion(f32[16384,128]{1,0:T(8,128)} %reshape.65, s32[3072]{0:T(1024)S(1)} %bitcast.51, f32[3072,128]{1,0:T(8,128)S(1)} %bitcast.48), kind=kCustom, calls=%fused_computation.2 | custom fusion | flops 393216 | bytes 4730880 | tf_op jit(solution)/shard_map/scatter-add | solution.py:58
  98.6 9.3 %reshape.67 = f32[2048,1024]{1,0:T(8,128)} reshape(f32[16384,128]{1,0:T(8,128)} %scatter_fusion) | data formatting | bytes 16777216 | tf_op jit(solution)/shard_map/reshape | solution.py:60
  107.9 2.5 constant_dynamic-slice_fusion.3
  110.4 2.5 pad_maximum_fusion
  112.9 0.0 all-to-all-done.3
  112.9 7.6 %all-to-all-start.2 = ((f32[16,128,512]{2,1,0:T(8,128)}), f32[16,128,512]{2,1,0:T(8,128)}, u32[]{:S(2)}, u32[]{:S(2)}) async-start(f32[16,128,512]{2,1,0:T(8,128)} %bitcast.47), calls=%async_computation.2 | async-start | bytes 8388608 | tf_op jit(solution)/shard_map/all_to_all | solution.py:90
  120.5 0.0 copy-start.1
  121.9 1.1 dynamic-slice_select_fusion
  123.1 2.0 collective-permute-start
  125.0 62.1 %collective-permute-done = f32[256,256]{1,0:T(8,128)S(1)} collective-permute-done((f32[256,256]{1,0:T(8,128)S(1)}, f32[256,256]{1,0:T(8,128)S(1)}, u32[]{:S(2)}, u32[]{:S(2)}) %collective-permute-start) | collective-permute-done | bytes 262176 | tf_op jit(solution)/shard_map/ppermute | solution.py:28
  187.1 1.1 fusion.37
  188.3 0.2 collective-permute-start.1
  188.5 8.2 %collective-permute-done.1 = f32[256,256]{1,0:T(8,128)S(1)} collective-permute-done((f32[256,256]{1,0:T(8,128)S(1)}, f32[256,256]{1,0:T(8,128)S(1)}, u32[]{:S(2)}, u32[]{:S(2)}) %collective-permute-start.1) | collective-permute-done | bytes 262176 | tf_op jit(solution)/shard_map/ppermute | solution.py:28
  196.7 0.4 collective-permute-start.2
  197.1 6.2 %collective-permute-done.2 = f32[256,256]{1,0:T(8,128)S(1)} collective-permute-done((f32[256,256]{1,0:T(8,128)S(1)}, f32[256,256]{1,0:T(8,128)S(1)}, u32[]{:S(2)}, u32[]{:S(2)}) %collective-permute-start.2) | collective-permute-done | bytes 262176 | tf_op jit(solution)/shard_map/ppermute | solution.py:28
  203.3 4.0 %collective-permute-start.3 = (f32[256,256]{1,0:T(8,128)S(1)}, f32[256,256]{1,0:T(8,128)S(1)}, u32[]{:S(2)}, u32[]{:S(2)}) collective-permute-start(f32[256,256]{1,0:T(8,128)S(1)} %add.116), channel_id=1, source_target_pairs={{0,8},{1,9},{2,10},{3,11},{4,12},{5,13},{6,14},{7,15},{8,0},{9,1},... | collective-permute-start | bytes 786440 | tf_op jit(solution)/shard_map/ppermute | solution.py:28
  207.3 4.4 %collective-permute-done.3 = f32[256,256]{1,0:T(8,128)S(1)} collective-permute-done((f32[256,256]{1,0:T(8,128)S(1)}, f32[256,256]{1,0:T(8,128)S(1)}, u32[]{:S(2)}, u32[]{:S(2)}) %collective-permute-start.3) | collective-permute-done | bytes 262176 | tf_op jit(solution)/shard_map/ppermute | solution.py:28
  211.7 0.1 collective-permute-start.4
  211.8 1.5 collective-permute-done.4
  213.3 5.6 %collective-permute-start.5 = (f32[256,256]{1,0:T(8,128)S(1)}, f32[256,256]{1,0:T(8,128)S(1)}, u32[]{:S(2)}, u32[]{:S(2)}) collective-permute-start(f32[256,256]{1,0:T(8,128)S(1)} %add.118), channel_id=1, source_target_pairs={{0,32},{1,33},{2,34},{3,35},{4,36},{5,37},{6,38},{7,39},{8,40},{9,... | collective-permute-start | bytes 786440 | tf_op jit(solution)/shard_map/ppermute | solution.py:28
  219.0 6.6 %collective-permute-done.5 = f32[256,256]{1,0:T(8,128)S(1)} collective-permute-done((f32[256,256]{1,0:T(8,128)S(1)}, f32[256,256]{1,0:T(8,128)S(1)}, u32[]{:S(2)}, u32[]{:S(2)}) %collective-permute-start.5) | collective-permute-done | bytes 262176 | tf_op jit(solution)/shard_map/ppermute | solution.py:28
  225.6 0.3 collective-permute-start.6
  226.6 8.6 %collective-permute-done.6 = f32[256,256]{1,0:T(8,128)S(1)} collective-permute-done((f32[256,256]{1,0:T(8,128)S(1)}, f32[256,256]{1,0:T(8,128)S(1)}, u32[]{:S(2)}, u32[]{:S(2)}) %collective-permute-start.6) | collective-permute-done | bytes 262176 | tf_op jit(solution)/shard_map/ppermute | solution.py:28
  235.2 0.4 fusion.11
  235.5 0.0 all-to-all-done.2
  235.6 1.1 dynamic-slice_bitcast_fusion
  236.6 0.3 fusion.13
  236.9 0.4 fusion.1
  237.3 0.3 fusion.9
  237.6 0.7 collective-permute-start.7
  238.3 2.5 broadcast_in_dim.45
  240.9 7.6 %all-to-all-start.4 = ((f32[16,128,512]{2,1,0:T(8,128)}), f32[16,128,512]{2,1,0:T(8,128)}, u32[]{:S(2)}, u32[]{:S(2)}) async-start(f32[16,128,512]{2,1,0:T(8,128)} %broadcast_in_dim.45), calls=%async_computation.4 | async-start | bytes 8388608 | tf_op jit(solution)/shard_map/all_to_all | solution.py:21
  248.5 0.0 all-gather.2.cloned.1.call-start
  248.5 0.0 collective-permute-done.7
  248.5 0.7 copy-done.2
  249.2 0.0 all-gather.2.cloned.1.call-update
  249.3 0.1 copy.19
  249.3 65.7 %all-to-all-done.4 = f32[16,128,512]{2,1,0:T(8,128)} async-done(((f32[16,128,512]{2,1,0:T(8,128)}), f32[16,128,512]{2,1,0:T(8,128)}, u32[]{:S(2)}, u32[]{:S(2)}) %all-to-all-start.4) | async-done | bytes 4194336 | tf_op jit(solution)/shard_map/all_to_all | solution.py:21
  315.1 0.1 broadcast_in_dim.46
  315.2 2.3 broadcast_in_dim.47
  317.5 14.6 %fusion = f32[2048,1024]{1,0:T(8,128)} fusion(f32[2048,1024]{1,0:T(8,128)} %reshape.67, f32[256,8,8,128]{3,2,1,0:T(8,128)S(1)} %bitcast.46, f32[2048,512]{1,0:T(8,128)} %bitcast.18, f32[1024,512]{1,0:T(8,128)S(1)} %copy-done), kind=kOutput, calls=%fused_computation.4 | convolution fusion | flops 6446645248 | bytes 31457280 | tf_op jit(solution)/shard_map/dot_general | solution.py:113
  (20 shorter events, 0.3 us)
Async XLA Ops:
  7.8 38.6 %copy-start.4 = (s32[2]{0:T(128)S(1)}, s32[2]{0:T(128)}, u32[]{:S(2)}) copy-start(s32[2]{0:T(128)} %param.14) | copy-start | bytes 28
  18.3 20.6 %all-to-all-start = ((f32[128,24,1]{1,2,0:T(1,128)}), f32[128,24,1]{1,2,0:T(1,128)S(1)}, u32[]{:S(2)}, u32[]{:S(2)}) async-start(f32[128,24,1]{1,2,0:T(1,128)} %bitcast.5), calls=%async_computation | async-start | bytes 131072 | tf_op jit(solution)/shard_map/all_to_all | solution.py:54
  38.9 32.0 %all-to-all-start.1 = ((f32[128,24,128]{2,1,0:T(8,128)}), f32[128,24,128]{2,1,0:T(8,128)S(1)}, u32[]{:S(2)}, u32[]{:S(2)}) async-start(f32[128,24,128]{2,1,0:T(8,128)} %bitcast.7), calls=%async_computation.1 | async-start | bytes 3145728 | tf_op jit(solution)/shard_map/all_to_all | solution.py:53
  50.8 9.3 %copy-start.3 = (s32[16,8]{0,1:T(8,128)S(1)}, s32[16,8]{0,1:T(8,128)}, u32[]{:S(2)}) copy-start(s32[16,8]{0,1:T(8,128)} %param.9) | copy-start | bytes 1540
  71.6 41.4 %all-to-all-start.3 = ((f32[16,1,256]{2,1,0:T(1,128)}), f32[16,1,256]{2,1,0:T(1,128)S(1)}, u32[]{:S(2)}, u32[]{:S(2)}) async-start(f32[16,1,256]{2,1,0:T(1,128)} %bitcast.15), calls=%async_computation.3 | async-start | bytes 32768 | tf_op jit(solution)/shard_map/all_to_all | solution.py:88
  112.9 122.6 %all-to-all-start.2 = ((f32[16,128,512]{2,1,0:T(8,128)}), f32[16,128,512]{2,1,0:T(8,128)}, u32[]{:S(2)}, u32[]{:S(2)}) async-start(f32[16,128,512]{2,1,0:T(8,128)} %bitcast.47), calls=%async_computation.2 | async-start | bytes 8388608 | tf_op jit(solution)/shard_map/all_to_all | solution.py:90
  120.5 114.6 %copy-start.1 = (f32[2,256,256]{2,1,0:T(8,128)S(1)}, f32[2,256,256]{2,1,0:T(8,128)}, u32[]{:S(2)}) copy-start(f32[2,256,256]{2,1,0:T(8,128)} %param.15) | copy-start | bytes 1572868
  123.1 64.1 %collective-permute-start = (f32[256,256]{1,0:T(8,128)S(1)}, f32[256,256]{1,0:T(8,128)S(1)}, u32[]{:S(2)}, u32[]{:S(2)}) collective-permute-start(f32[256,256]{1,0:T(8,128)S(1)} %dynamic-slice_select_fusion), channel_id=1, source_target_pairs={{0,1},{1,0},{2,3},{3,2},{4,5},{5,4},{6,7},{7,6},{8,9},{9,8},{10,11... | collective-permute-start | bytes 786440 | tf_op jit(solution)/shard_map/ppermute | solution.py:28
  188.3 8.4 %collective-permute-start.1 = (f32[256,256]{1,0:T(8,128)S(1)}, f32[256,256]{1,0:T(8,128)S(1)}, u32[]{:S(2)}, u32[]{:S(2)}) collective-permute-start(f32[256,256]{1,0:T(8,128)S(1)} %fusion.37), channel_id=1, source_target_pairs={{0,2},{1,3},{2,0},{3,1},{4,6},{5,7},{6,4},{7,5},{8,10},{9,11},{10,... | collective-permute-start | bytes 786440 | tf_op jit(solution)/shard_map/ppermute | solution.py:28
  196.7 6.6 %collective-permute-start.2 = (f32[256,256]{1,0:T(8,128)S(1)}, f32[256,256]{1,0:T(8,128)S(1)}, u32[]{:S(2)}, u32[]{:S(2)}) collective-permute-start(f32[256,256]{1,0:T(8,128)S(1)} %add.115), channel_id=1, source_target_pairs={{0,4},{1,5},{2,6},{3,7},{4,0},{5,1},{6,2},{7,3},{8,12},{9,13},{10,... | collective-permute-start | bytes 786440 | tf_op jit(solution)/shard_map/ppermute | solution.py:28
  203.3 8.3 %collective-permute-start.3 = (f32[256,256]{1,0:T(8,128)S(1)}, f32[256,256]{1,0:T(8,128)S(1)}, u32[]{:S(2)}, u32[]{:S(2)}) collective-permute-start(f32[256,256]{1,0:T(8,128)S(1)} %add.116), channel_id=1, source_target_pairs={{0,8},{1,9},{2,10},{3,11},{4,12},{5,13},{6,14},{7,15},{8,0},{9,1},... | collective-permute-start | bytes 786440 | tf_op jit(solution)/shard_map/ppermute | solution.py:28
  211.7 1.6 collective-permute-start.4
  213.3 12.2 %collective-permute-start.5 = (f32[256,256]{1,0:T(8,128)S(1)}, f32[256,256]{1,0:T(8,128)S(1)}, u32[]{:S(2)}, u32[]{:S(2)}) collective-permute-start(f32[256,256]{1,0:T(8,128)S(1)} %add.118), channel_id=1, source_target_pairs={{0,32},{1,33},{2,34},{3,35},{4,36},{5,37},{6,38},{7,39},{8,40},{9,... | collective-permute-start | bytes 786440 | tf_op jit(solution)/shard_map/ppermute | solution.py:28
  225.6 9.5 %collective-permute-start.6 = (f32[256,256]{1,0:T(8,128)S(1)}, f32[256,256]{1,0:T(8,128)S(1)}, u32[]{:S(2)}, u32[]{:S(2)}) collective-permute-start(f32[256,256]{1,0:T(8,128)S(1)} %add.119), channel_id=1, source_target_pairs={{0,64},{1,65},{2,66},{3,67},{4,68},{5,69},{6,70},{7,71},{8,72},{9,... | collective-permute-start | bytes 786440 | tf_op jit(solution)/shard_map/ppermute | solution.py:28
  237.6 10.9 %collective-permute-start.7 = (f32[128,512]{1,0:T(8,128)S(1)}, f32[128,512]{1,0:T(8,128)S(1)}, u32[]{:S(2)}, u32[]{:S(2)}) collective-permute-start(f32[128,512]{1,0:T(8,128)S(1)} %pad_maximum_fusion.1), channel_id=1, source_target_pairs={{0,0},{1,16},{2,32},{3,48},{4,64},{5,80},{6,96},{7,112},{8,1},{9,1... | collective-permute-start | bytes 786440 | tf_op jit(solution)/shard_map/ppermute | solution.py:110
  240.9 74.2 %all-to-all-start.4 = ((f32[16,128,512]{2,1,0:T(8,128)}), f32[16,128,512]{2,1,0:T(8,128)}, u32[]{:S(2)}, u32[]{:S(2)}) async-start(f32[16,128,512]{2,1,0:T(8,128)} %broadcast_in_dim.45), calls=%async_computation.4 | async-start | bytes 8388608 | tf_op jit(solution)/shard_map/all_to_all | solution.py:21
  248.5 66.6 %all-gather.2.cloned.1.call-start = ((), (), s32[]{:S(2)}) async-start(), calls=%async_computation.5 | async-start | bytes 2359296 | tf_op jit(solution)/shard_map/all_gather | solution.py:111
  248.5 0.7 copy-start.2
  315.1 2.3 copy-start
Sparse Core Ops, SparseCore 0:
  251.0 61.1 all-gather.1
